TPU v7x, 768 devices: a whole 4x8x12 slice. The times are simulated.
768 devices in a mesh: gx: 192 (over z, y, core), gy: 4 (over x).
Axes of the slice: x: 4, y: 8, z: 12, core: 2. Of those that a mesh axis runs over, the one named last changes fastest.
Arguments:
- moisture: float32 [49152, 20, 128], P(('gx', 'gy')), may hold values from 0.05 to 1
- diffusivity: float32 [49152, 20, 128], P(('gx', 'gy')), may hold values from 0.1 to 4
- rain: float32 [49152, 128], P(('gx', 'gy')), may hold values from 0 to 2
- head: float32 [50, 3072, 512], P(None, 'gx', 'gy'), may hold values from -4 to 4
- conductivity: float32 [50, 3072, 512], P(None, 'gx', 'gy'), may hold values from 0.05 to 1
- tile_ids: int32 [49152], P(('gx', 'gy')), may hold values from 0 to 3, as said below
- offsets: int32 [49152], P(('gx', 'gy')), may hold values from 0 to 15
- patch_ids: int32 [49152], P(('gx', 'gy')), may hold values from 0 to 7
- counts: int32 [768], P(('gx', 'gy')), may hold values from 48 to 64, as said below
Outputs:
- head_out: float32 [50, 3072, 512], P(None, 'gx', 'gy')
- moisture_out: float32 [49152, 20, 128], P(('gx', 'gy'))
- patch_sums: float32 [6144, 128], P(('gx', 'gy'))
Inputs may be any that keep to these rules, and one draw needn't show every extreme that they name: `tile_ids`: only the first counts[d] block slots of device d are used; the others' entries are arbitrary. Among the used blocks of one device at most 32 name the same tile, and in every gx row one tile is named by exactly 32 used blocks of every device of that row. `counts`: some device uses all 64 slots in every draw.
All inputs are finite; a program needn't handle non-finite values.
Results may differ from a plain program's by a relative error of at most 0.00016.
Values sent between devices are 32-bit elements; how exact they have to be, the bound alone decides.
No kernel may reach another device: no remote copies, remote signals or barrier semaphores. Data moves between devices by JAX's collectives and lax.ppermute only.
A program may use at most 32 MiB of HBM per device.

v0:
```python
import jax
import jax.numpy as jnp
from jax import lax
from jax.sharding import PartitionSpec as P

PATCH_DEV = 8
SWEEPS = 6


flow_rate = 0.15
capillary = 0.5


def with_halo(cells, sides, width):
    for axis, dim in sides:
        count = lax.axis_size(axis)
        ends = count - 1
        head = lax.slice_in_dim(cells, 0, width, axis=dim)
        tail = lax.slice_in_dim(cells, cells.shape[dim] - width, cells.shape[dim], axis=dim)
        cells = jnp.concatenate(
            [
                lax.ppermute(tail, axis, [(i, (i + 1) % count) for i in range(ends)]),
                cells,
                lax.ppermute(head, axis, [((i + 1) % count, i) for i in range(ends)]),
            ],
            axis=dim,
        )
    return cells


def column_solve(moisture, diffusivity, rain):
    depth = moisture.shape[1]
    ratios = []
    forward_vals = []
    for layer_k in range(depth):
        lower_coef = diffusivity[:, layer_k, :]
        source = moisture[:, layer_k, :]
        if layer_k == 0:
            source = source + rain
            pivot = 1.0 + lower_coef
            carried = source / pivot
        else:
            upper_coef = diffusivity[:, layer_k - 1, :]
            pivot = 1.0 + lower_coef + upper_coef - upper_coef * ratios[-1]
            carried = (source + upper_coef * forward_vals[-1]) / pivot
        ratios.append(lower_coef / pivot)
        forward_vals.append(carried)
    solved = [forward_vals[-1]]
    for layer_k in range(depth - 2, -1, -1):
        solved.append(forward_vals[layer_k] + ratios[layer_k] * solved[-1])
    return jnp.stack(solved[::-1], axis=1)


def lateral_core(padded_head, padded_cond):
    inner_rows = padded_head.shape[1] - 2
    inner_cols = padded_head.shape[2] - 2
    centre = padded_head[:, 1:-1, 1:-1]
    centre_cond = padded_cond[:, 1:-1, 1:-1]
    flux_total = jnp.zeros_like(centre)
    for row_shift, col_shift in ((0, 1), (2, 1), (1, 0), (1, 2)):
        beside = padded_head[
            :, row_shift : row_shift + inner_rows, col_shift : col_shift + inner_cols
        ]
        beside_cond = padded_cond[
            :, row_shift : row_shift + inner_rows, col_shift : col_shift + inner_cols
        ]
        flux_total = flux_total + 0.5 * (centre_cond + beside_cond) * (beside - centre)
    vertical = 0.5 * (centre_cond[1:] + centre_cond[:-1]) * (centre[1:] - centre[:-1])
    flux_total = (
        flux_total
        + jnp.pad(vertical, ((0, 1), (0, 0), (0, 0)))
        - jnp.pad(vertical, ((1, 0), (0, 0), (0, 0)))
    )
    return centre + flow_rate * flux_total


def local(moisture, diffusivity, rain, head, conductivity, tile_ids, offsets, patch_ids, counts):
    highest = lax.Precision.HIGHEST
    block_count = moisture.shape[0]
    tile_count = lax.axis_size("gy")
    capacity = block_count // 2
    tile_rows = head.shape[1]
    tile_cols = head.shape[2]
    wet = column_solve(moisture, diffusivity, rain)
    bottom = wet[:, -1, :]
    drain = diffusivity[:, -1, :] * bottom
    in_use = jnp.arange(block_count, dtype=jnp.int32) < counts[0]
    in_use_f = in_use.astype(jnp.float32)
    to_tile = (
        (tile_ids[:, None] == jnp.arange(tile_count, dtype=jnp.int32)[None, :]) & in_use[:, None]
    ).astype(jnp.int32)
    before = jnp.cumsum(to_tile, axis=0) - to_tile
    slot_of = jnp.sum(before * to_tile, axis=1)
    slot_match = slot_of[None, None, :] == jnp.arange(capacity, dtype=jnp.int32)[None, :, None]
    placing = (to_tile.T[:, None, :] * slot_match).astype(jnp.float32)
    outgoing = jnp.einsum("tcb,bj->tcj", placing, drain, precision=highest)
    out_rows = (
        jnp.einsum("tcb,b->tc", placing, (offsets + 1).astype(jnp.float32), precision=highest) - 1.0
    )
    incoming, in_rows = (
        lax.all_to_all(outgoing, "gy", split_axis=0, concat_axis=0, tiled=True),
        lax.all_to_all(out_rows, "gy", split_axis=0, concat_axis=0, tiled=True),
    )
    slot_total = tile_count * capacity
    landing = (
        in_rows.reshape(1, slot_total) == jnp.arange(tile_rows, dtype=jnp.float32)[:, None]
    ).astype(jnp.float32)
    recharge = jnp.dot(landing, incoming.reshape(slot_total, tile_cols), precision=highest)
    field = head.at[0].add(recharge)
    padded_cond = with_halo(conductivity, (("gx", 1), ("gy", 2)), 1)
    for sweep_k in range(SWEEPS):
        padded_head = with_halo(field, (("gx", 1), ("gy", 2)), 1)
        field = lateral_core(padded_head, padded_cond)
    surface = field[0]
    answered = jnp.dot(landing.T, surface, precision=highest).reshape(
        tile_count, capacity, tile_cols
    )
    returned = lax.all_to_all(answered, "gy", split_axis=0, concat_axis=0, tiled=True)
    saturation = jnp.einsum("tcb,tcj->bj", placing, returned, precision=highest)
    new_bottom = bottom + capillary * (saturation - in_use_f[:, None] * bottom)
    moisture_out = wet.at[:, -1, :].set(new_bottom)
    patch_hot = (patch_ids[None, :] == jnp.arange(PATCH_DEV, dtype=jnp.int32)[:, None]).astype(
        jnp.float32
    )
    patch_sums = jnp.dot(patch_hot, saturation, precision=highest)
    return (field, moisture_out, patch_sums)


def solution(mesh):
    placed = (
        P(("gx", "gy"), None, None),
        P(("gx", "gy"), None, None),
        P(("gx", "gy"), None),
        P(None, "gx", "gy"),
        P(None, "gx", "gy"),
        P(("gx", "gy")),
        P(("gx", "gy")),
        P(("gx", "gy")),
        P(("gx", "gy")),
    )
    return jax.shard_map(
        local,
        mesh=mesh,
        in_specs=placed,
        out_specs=(P(None, "gx", "gy"), P(("gx", "gy"), None, None), P(("gx", "gy"), None)),
        check_vma=False,
    )
```

profile of v0, /device:TPU:512, one launch (start us, length us, event | category | flops | bytes accessed | tf_op | source)
XLA Modules:
  0.0 194.0 jit_solution(9854940591410129361)
XLA Ops:
  5.4 4.3 %all-to-all-start = ((f32[4,1,32]{2,1,0:T(1,128)}), f32[4,1,32]{2,1,0:T(1,128)S(1)}, u32[]{:S(2)}, u32[]{:S(2)}) async-start(f32[4,1,32]{2,1,0:T(1,128)} %bitcast.5), calls=%async_computation | async-start | bytes 4096 | tf_op jit(solution)/shard_map/all_to_all | solution.py:102
  9.7 5.7 %collective-permute-start.2 = (f32[50,1,128]{2,1,0:T(1,128)S(1)}, f32[50,1,128]{2,1,0:T(1,128)S(1)}, u32[]{:S(2)}, u32[]{:S(2)}) collective-permute-start(f32[50,1,128]{2,1,0:T(1,128)S(1)} %get-tuple-element.103), channel_id=1, source_target_pairs={{4,0},{8,4},{12,8},{16,12},{20,16},{24,20},{28,24},{32,28},{36,32}... | collective-permute-start | bytes 76808 | tf_op jit(solution)/shard_map/ppermute | solution.py:24
  15.5 1.9 collective-permute-start
  22.3 4.5 %all-to-all-start.1 = ((f32[4,32,128]{2,1,0:T(8,128)}), f32[4,32,128]{2,1,0:T(8,128)S(1)}, u32[]{:S(2)}, u32[]{:S(2)}) async-start(f32[4,32,128]{2,1,0:T(8,128)} %fusion.107), calls=%async_computation.1 | async-start | bytes 131072 | tf_op jit(solution)/shard_map/all_to_all | solution.py:101
  29.1 3.9 %collective-permute-start.4 = (f32[50,18,1]{0,1,2:T(8,128)S(1)}, f32[50,18,1]{0,1,2:T(8,128)S(1)}, u32[]{:S(2)}, u32[]{:S(2)}) collective-permute-start(f32[50,18,1]{0,1,2:T(8,128)S(1)} %copy.13), channel_id=1, source_target_pairs={{0,1},{1,2},{2,3},{4,5},{5,6},{6,7},{8,9},{9,10},{10,11},{12,13},{... | collective-permute-start | bytes 10808 | tf_op jit(solution)/shard_map/ppermute | solution.py:22
  34.5 1.9 collective-permute-start.1
  36.4 7.0 %collective-permute-start.3 = (f32[50,1,128]{2,1,0:T(1,128)S(1)}, f32[50,1,128]{2,1,0:T(1,128)S(1)}, u32[]{:S(2)}, u32[]{:S(2)}) collective-permute-start(f32[50,1,128]{2,1,0:T(1,128)S(1)} %get-tuple-element.106), channel_id=1, source_target_pairs={{4,0},{8,4},{12,8},{16,12},{20,16},{24,20},{28,24},{32,28},{36,32}... | collective-permute-start | bytes 76808 | tf_op jit(solution)/shard_map/ppermute | solution.py:24
  48.6 5.2 %collective-permute-start.5 = (f32[50,18,1]{0,1,2:T(8,128)S(1)}, f32[50,18,1]{0,1,2:T(8,128)S(1)}, u32[]{:S(2)}, u32[]{:S(2)}) collective-permute-start(f32[50,18,1]{0,1,2:T(8,128)S(1)} %copy.15), channel_id=1, source_target_pairs={{0,1},{1,2},{2,3},{4,5},{5,6},{6,7},{8,9},{9,10},{10,11},{12,13},{... | collective-permute-start | bytes 10808 | tf_op jit(solution)/shard_map/ppermute | solution.py:22
  57.6 2.6 %fusion.83 = (f32[50,16,128]{2,1,0:T(8,128)S(1)}, f32[50,16,128]{2,1,0:T(8,128)S(1)}, f32[50,16,128]{2,1,0:T(8,128)S(1)}) fusion(f32[50,16,128]{2,1,0:T(8,128)S(1)} %fusion.1, f32[50,18,1]{2,1,0:T(8,128)} %copy.20, f32[50,1,128]{2,1,0:T(1,128)} %copy-done.29, f32[50,1,128]{2,1,0:T(1,128)} %copy-done.28, f32[50,18,1]{2,1,0:T(8,128)} %copy.16, ...), kind=kLoop, calls=%fused_computation.133 | loop fusion | flops 3993600 | bytes 2566208 | tf_op jit(solution)/shard_map/add | solution.py:74
  60.2 1.9 collective-permute-start.8
  62.1 7.0 %collective-permute-start.9 = (f32[50,1,128]{2,1,0:T(1,128)S(1)}, f32[50,1,128]{2,1,0:T(1,128)S(1)}, u32[]{:S(2)}, u32[]{:S(2)}) collective-permute-start(f32[50,1,128]{2,1,0:T(1,128)S(1)} %get-tuple-element.102), channel_id=1, source_target_pairs={{4,0},{8,4},{12,8},{16,12},{20,16},{24,20},{28,24},{32,28},{36,32}... | collective-permute-start | bytes 76808 | tf_op jit(solution)/shard_map/ppermute | solution.py:24
  75.3 4.8 %collective-permute-start.10 = (f32[50,18,1]{0,1,2:T(8,128)S(1)}, f32[50,18,1]{0,1,2:T(8,128)S(1)}, u32[]{:S(2)}, u32[]{:S(2)}) collective-permute-start(f32[50,18,1]{0,1,2:T(8,128)S(1)} %copy.21), channel_id=1, source_target_pairs={{0,1},{1,2},{2,3},{4,5},{5,6},{6,7},{8,9},{9,10},{10,11},{12,13},{... | collective-permute-start | bytes 10808 | tf_op jit(solution)/shard_map/ppermute | solution.py:22
  84.9 1.9 collective-permute-start.12
  86.9 7.0 %collective-permute-start.13 = (f32[50,1,128]{2,1,0:T(1,128)S(1)}, f32[50,1,128]{2,1,0:T(1,128)S(1)}, u32[]{:S(2)}, u32[]{:S(2)}) collective-permute-start(f32[50,1,128]{2,1,0:T(1,128)S(1)} %get-tuple-element.100), channel_id=1, source_target_pairs={{4,0},{8,4},{12,8},{16,12},{20,16},{24,20},{28,24},{32,28},{36,32}... | collective-permute-start | bytes 76808 | tf_op jit(solution)/shard_map/ppermute | solution.py:24
  98.2 4.8 %collective-permute-start.14 = (f32[50,18,1]{0,1,2:T(8,128)S(1)}, f32[50,18,1]{0,1,2:T(8,128)S(1)}, u32[]{:S(2)}, u32[]{:S(2)}) collective-permute-start(f32[50,18,1]{0,1,2:T(8,128)S(1)} %copy.25), channel_id=1, source_target_pairs={{0,1},{1,2},{2,3},{4,5},{5,6},{6,7},{8,9},{9,10},{10,11},{12,13},{... | collective-permute-start | bytes 10808 | tf_op jit(solution)/shard_map/ppermute | solution.py:22
  107.9 1.9 collective-permute-start.16
  109.8 7.0 %collective-permute-start.17 = (f32[50,1,128]{2,1,0:T(1,128)S(1)}, f32[50,1,128]{2,1,0:T(1,128)S(1)}, u32[]{:S(2)}, u32[]{:S(2)}) collective-permute-start(f32[50,1,128]{2,1,0:T(1,128)S(1)} %get-tuple-element.98), channel_id=1, source_target_pairs={{4,0},{8,4},{12,8},{16,12},{20,16},{24,20},{28,24},{32,28},{36,32}... | collective-permute-start | bytes 76808 | tf_op jit(solution)/shard_map/ppermute | solution.py:24
  122.9 5.0 %collective-permute-start.18 = (f32[50,18,1]{0,1,2:T(8,128)S(1)}, f32[50,18,1]{0,1,2:T(8,128)S(1)}, u32[]{:S(2)}, u32[]{:S(2)}) collective-permute-start(f32[50,18,1]{0,1,2:T(8,128)S(1)} %copy.29), channel_id=1, source_target_pairs={{0,1},{1,2},{2,3},{4,5},{5,6},{6,7},{8,9},{9,10},{10,11},{12,13},{... | collective-permute-start | bytes 10808 | tf_op jit(solution)/shard_map/ppermute | solution.py:22
  134.5 7.0 %collective-permute-start.21 = (f32[50,1,128]{2,1,0:T(1,128)S(1)}, f32[50,1,128]{2,1,0:T(1,128)S(1)}, u32[]{:S(2)}, u32[]{:S(2)}) collective-permute-start(f32[50,1,128]{2,1,0:T(1,128)S(1)} %get-tuple-element.96), channel_id=1, source_target_pairs={{4,0},{8,4},{12,8},{16,12},{20,16},{24,20},{28,24},{32,28},{36,32}... | collective-permute-start | bytes 76808 | tf_op jit(solution)/shard_map/ppermute | solution.py:24
  147.7 4.8 %collective-permute-start.22 = (f32[50,18,1]{0,1,2:T(8,128)S(1)}, f32[50,18,1]{0,1,2:T(8,128)S(1)}, u32[]{:S(2)}, u32[]{:S(2)}) collective-permute-start(f32[50,18,1]{0,1,2:T(8,128)S(1)} %copy.33), channel_id=1, source_target_pairs={{0,1},{1,2},{2,3},{4,5},{5,6},{6,7},{8,9},{9,10},{10,11},{12,13},{... | collective-permute-start | bytes 10808 | tf_op jit(solution)/shard_map/ppermute | solution.py:22
  159.3 7.0 %collective-permute-start.25 = (f32[50,1,128]{2,1,0:T(1,128)S(1)}, f32[50,1,128]{2,1,0:T(1,128)S(1)}, u32[]{:S(2)}, u32[]{:S(2)}) collective-permute-start(f32[50,1,128]{2,1,0:T(1,128)S(1)} %get-tuple-element.94), channel_id=1, source_target_pairs={{4,0},{8,4},{12,8},{16,12},{20,16},{24,20},{28,24},{32,28},{36,32}... | collective-permute-start | bytes 76808 | tf_op jit(solution)/shard_map/ppermute | solution.py:24
  170.0 4.8 %collective-permute-start.26 = (f32[50,18,1]{0,1,2:T(8,128)S(1)}, f32[50,18,1]{0,1,2:T(8,128)S(1)}, u32[]{:S(2)}, u32[]{:S(2)}) collective-permute-start(f32[50,18,1]{0,1,2:T(8,128)S(1)} %copy.37), channel_id=1, source_target_pairs={{0,1},{1,2},{2,3},{4,5},{5,6},{6,7},{8,9},{9,10},{10,11},{12,13},{... | collective-permute-start | bytes 10808 | tf_op jit(solution)/shard_map/ppermute | solution.py:22
  179.9 6.2 %all-to-all-start.2 = ((f32[4,32,128]{2,1,0:T(8,128)}), f32[4,32,128]{2,1,0:T(8,128)S(1)}, u32[]{:S(2)}, u32[]{:S(2)}) async-start(f32[4,32,128]{2,1,0:T(8,128)} %fusion.181), calls=%async_computation.2 | async-start | bytes 131072 | tf_op jit(solution)/shard_map/all_to_all | solution.py:118
  186.1 5.6 %all-to-all-done.2 = f32[4,32,128]{2,1,0:T(8,128)S(1)} async-done(((f32[4,32,128]{2,1,0:T(8,128)}), f32[4,32,128]{2,1,0:T(8,128)S(1)}, u32[]{:S(2)}, u32[]{:S(2)}) %all-to-all-start.2) | async-done | bytes 65568 | tf_op jit(solution)/shard_map/all_to_all | solution.py:118
  (201 shorter events, 78.1 us)
Async XLA Ops:
  5.4 16.9 %all-to-all-start = ((f32[4,1,32]{2,1,0:T(1,128)}), f32[4,1,32]{2,1,0:T(1,128)S(1)}, u32[]{:S(2)}, u32[]{:S(2)}) async-start(f32[4,1,32]{2,1,0:T(1,128)} %bitcast.5), calls=%async_computation | async-start | bytes 4096 | tf_op jit(solution)/shard_map/all_to_all | solution.py:102
  9.7 18.4 %collective-permute-start.2 = (f32[50,1,128]{2,1,0:T(1,128)S(1)}, f32[50,1,128]{2,1,0:T(1,128)S(1)}, u32[]{:S(2)}, u32[]{:S(2)}) collective-permute-start(f32[50,1,128]{2,1,0:T(1,128)S(1)} %get-tuple-element.103), channel_id=1, source_target_pairs={{4,0},{8,4},{12,8},{16,12},{20,16},{24,20},{28,24},{32,28},{36,32}... | collective-permute-start | bytes 76808 | tf_op jit(solution)/shard_map/ppermute | solution.py:24
  15.5 12.6 %collective-permute-start = (f32[50,1,128]{2,1,0:T(1,128)S(1)}, f32[50,1,128]{2,1,0:T(1,128)S(1)}, u32[]{:S(2)}, u32[]{:S(2)}) collective-permute-start(f32[50,1,128]{2,1,0:T(1,128)S(1)} %get-tuple-element.104), channel_id=1, source_target_pairs={{0,4},{4,8},{8,12},{12,16},{16,20},{20,24},{24,28},{28,32},{32,36}... | collective-permute-start | bytes 76808 | tf_op jit(solution)/shard_map/ppermute | solution.py:22
  22.3 12.0 %all-to-all-start.1 = ((f32[4,32,128]{2,1,0:T(8,128)}), f32[4,32,128]{2,1,0:T(8,128)S(1)}, u32[]{:S(2)}, u32[]{:S(2)}) async-start(f32[4,32,128]{2,1,0:T(8,128)} %fusion.107), calls=%async_computation.1 | async-start | bytes 131072 | tf_op jit(solution)/shard_map/all_to_all | solution.py:101
  29.1 15.6 %collective-permute-start.4 = (f32[50,18,1]{0,1,2:T(8,128)S(1)}, f32[50,18,1]{0,1,2:T(8,128)S(1)}, u32[]{:S(2)}, u32[]{:S(2)}) collective-permute-start(f32[50,18,1]{0,1,2:T(8,128)S(1)} %copy.13), channel_id=1, source_target_pairs={{0,1},{1,2},{2,3},{4,5},{5,6},{6,7},{8,9},{9,10},{10,11},{12,13},{... | collective-permute-start | bytes 10808 | tf_op jit(solution)/shard_map/ppermute | solution.py:22
  33.0 10.5 %collective-permute-start.6 = (f32[50,18,1]{0,1,2:T(8,128)S(1)}, f32[50,18,1]{0,1,2:T(8,128)S(1)}, u32[]{:S(2)}, u32[]{:S(2)}) collective-permute-start(f32[50,18,1]{0,1,2:T(8,128)S(1)} %copy.17), channel_id=1, source_target_pairs={{1,0},{2,1},{3,2},{5,4},{6,5},{7,6},{9,8},{10,9},{11,10},{13,12},{... | collective-permute-start | bytes 10808 | tf_op jit(solution)/shard_map/ppermute | solution.py:24
  34.5 11.3 %collective-permute-start.1 = (f32[50,1,128]{2,1,0:T(1,128)S(1)}, f32[50,1,128]{2,1,0:T(1,128)S(1)}, u32[]{:S(2)}, u32[]{:S(2)}) collective-permute-start(f32[50,1,128]{2,1,0:T(1,128)S(1)} %get-tuple-element.105), channel_id=1, source_target_pairs={{0,4},{4,8},{8,12},{12,16},{16,20},{20,24},{24,28},{28,32},{32,36}... | collective-permute-start | bytes 76808 | tf_op jit(solution)/shard_map/ppermute | solution.py:22
  36.4 9.4 %collective-permute-start.3 = (f32[50,1,128]{2,1,0:T(1,128)S(1)}, f32[50,1,128]{2,1,0:T(1,128)S(1)}, u32[]{:S(2)}, u32[]{:S(2)}) collective-permute-start(f32[50,1,128]{2,1,0:T(1,128)S(1)} %get-tuple-element.106), channel_id=1, source_target_pairs={{4,0},{8,4},{12,8},{16,12},{20,16},{24,20},{28,24},{32,28},{36,32}... | collective-permute-start | bytes 76808 | tf_op jit(solution)/shard_map/ppermute | solution.py:24
  47.3 9.0 %collective-permute-start.7 = (f32[50,18,1]{0,1,2:T(8,128)S(1)}, f32[50,18,1]{0,1,2:T(8,128)S(1)}, u32[]{:S(2)}, u32[]{:S(2)}) collective-permute-start(f32[50,18,1]{0,1,2:T(8,128)S(1)} %copy.19), channel_id=1, source_target_pairs={{1,0},{2,1},{3,2},{5,4},{6,5},{7,6},{9,8},{10,9},{11,10},{13,12},{... | collective-permute-start | bytes 10808 | tf_op jit(solution)/shard_map/ppermute | solution.py:24
  60.2 9.5 %collective-permute-start.8 = (f32[50,1,128]{2,1,0:T(1,128)S(1)}, f32[50,1,128]{2,1,0:T(1,128)S(1)}, u32[]{:S(2)}, u32[]{:S(2)}) collective-permute-start(f32[50,1,128]{2,1,0:T(1,128)S(1)} %get-tuple-element.101), channel_id=1, source_target_pairs={{0,4},{4,8},{8,12},{12,16},{16,20},{20,24},{24,28},{28,32},{32,36}... | collective-permute-start | bytes 76808 | tf_op jit(solution)/shard_map/ppermute | solution.py:22
  62.1 8.5 %collective-permute-start.9 = (f32[50,1,128]{2,1,0:T(1,128)S(1)}, f32[50,1,128]{2,1,0:T(1,128)S(1)}, u32[]{:S(2)}, u32[]{:S(2)}) collective-permute-start(f32[50,1,128]{2,1,0:T(1,128)S(1)} %get-tuple-element.102), channel_id=1, source_target_pairs={{4,0},{8,4},{12,8},{16,12},{20,16},{24,20},{28,24},{32,28},{36,32}... | collective-permute-start | bytes 76808 | tf_op jit(solution)/shard_map/ppermute | solution.py:24
  74.0 7.9 %collective-permute-start.11 = (f32[50,18,1]{0,1,2:T(8,128)S(1)}, f32[50,18,1]{0,1,2:T(8,128)S(1)}, u32[]{:S(2)}, u32[]{:S(2)}) collective-permute-start(f32[50,18,1]{0,1,2:T(8,128)S(1)} %copy.23), channel_id=1, source_target_pairs={{1,0},{2,1},{3,2},{5,4},{6,5},{7,6},{9,8},{10,9},{11,10},{13,12},{... | collective-permute-start | bytes 10808 | tf_op jit(solution)/shard_map/ppermute | solution.py:24
  84.9 9.6 %collective-permute-start.12 = (f32[50,1,128]{2,1,0:T(1,128)S(1)}, f32[50,1,128]{2,1,0:T(1,128)S(1)}, u32[]{:S(2)}, u32[]{:S(2)}) collective-permute-start(f32[50,1,128]{2,1,0:T(1,128)S(1)} %get-tuple-element.99), channel_id=1, source_target_pairs={{0,4},{4,8},{8,12},{12,16},{16,20},{20,24},{24,28},{28,32},{32,36}... | collective-permute-start | bytes 76808 | tf_op jit(solution)/shard_map/ppermute | solution.py:22
  86.9 8.5 %collective-permute-start.13 = (f32[50,1,128]{2,1,0:T(1,128)S(1)}, f32[50,1,128]{2,1,0:T(1,128)S(1)}, u32[]{:S(2)}, u32[]{:S(2)}) collective-permute-start(f32[50,1,128]{2,1,0:T(1,128)S(1)} %get-tuple-element.100), channel_id=1, source_target_pairs={{4,0},{8,4},{12,8},{16,12},{20,16},{24,20},{28,24},{32,28},{36,32}... | collective-permute-start | bytes 76808 | tf_op jit(solution)/shard_map/ppermute | solution.py:24
  96.9 7.9 %collective-permute-start.15 = (f32[50,18,1]{0,1,2:T(8,128)S(1)}, f32[50,18,1]{0,1,2:T(8,128)S(1)}, u32[]{:S(2)}, u32[]{:S(2)}) collective-permute-start(f32[50,18,1]{0,1,2:T(8,128)S(1)} %copy.27), channel_id=1, source_target_pairs={{1,0},{2,1},{3,2},{5,4},{6,5},{7,6},{9,8},{10,9},{11,10},{13,12},{... | collective-permute-start | bytes 10808 | tf_op jit(solution)/shard_map/ppermute | solution.py:24
  107.9 9.5 %collective-permute-start.16 = (f32[50,1,128]{2,1,0:T(1,128)S(1)}, f32[50,1,128]{2,1,0:T(1,128)S(1)}, u32[]{:S(2)}, u32[]{:S(2)}) collective-permute-start(f32[50,1,128]{2,1,0:T(1,128)S(1)} %get-tuple-element.97), channel_id=1, source_target_pairs={{0,4},{4,8},{8,12},{12,16},{16,20},{20,24},{24,28},{28,32},{32,36}... | collective-permute-start | bytes 76808 | tf_op jit(solution)/shard_map/ppermute | solution.py:22
  109.8 8.5 %collective-permute-start.17 = (f32[50,1,128]{2,1,0:T(1,128)S(1)}, f32[50,1,128]{2,1,0:T(1,128)S(1)}, u32[]{:S(2)}, u32[]{:S(2)}) collective-permute-start(f32[50,1,128]{2,1,0:T(1,128)S(1)} %get-tuple-element.98), channel_id=1, source_target_pairs={{4,0},{8,4},{12,8},{16,12},{20,16},{24,20},{28,24},{32,28},{36,32}... | collective-permute-start | bytes 76808 | tf_op jit(solution)/shard_map/ppermute | solution.py:24
  132.6 9.6 %collective-permute-start.20 = (f32[50,1,128]{2,1,0:T(1,128)S(1)}, f32[50,1,128]{2,1,0:T(1,128)S(1)}, u32[]{:S(2)}, u32[]{:S(2)}) collective-permute-start(f32[50,1,128]{2,1,0:T(1,128)S(1)} %get-tuple-element.95), channel_id=1, source_target_pairs={{0,4},{4,8},{8,12},{12,16},{16,20},{20,24},{24,28},{28,32},{32,36}... | collective-permute-start | bytes 76808 | tf_op jit(solution)/shard_map/ppermute | solution.py:22
  134.5 8.5 %collective-permute-start.21 = (f32[50,1,128]{2,1,0:T(1,128)S(1)}, f32[50,1,128]{2,1,0:T(1,128)S(1)}, u32[]{:S(2)}, u32[]{:S(2)}) collective-permute-start(f32[50,1,128]{2,1,0:T(1,128)S(1)} %get-tuple-element.96), channel_id=1, source_target_pairs={{4,0},{8,4},{12,8},{16,12},{20,16},{24,20},{28,24},{32,28},{36,32}... | collective-permute-start | bytes 76808 | tf_op jit(solution)/shard_map/ppermute | solution.py:24
  146.4 7.9 %collective-permute-start.23 = (f32[50,18,1]{0,1,2:T(8,128)S(1)}, f32[50,18,1]{0,1,2:T(8,128)S(1)}, u32[]{:S(2)}, u32[]{:S(2)}) collective-permute-start(f32[50,18,1]{0,1,2:T(8,128)S(1)} %copy.35), channel_id=1, source_target_pairs={{1,0},{2,1},{3,2},{5,4},{6,5},{7,6},{9,8},{10,9},{11,10},{13,12},{... | collective-permute-start | bytes 10808 | tf_op jit(solution)/shard_map/ppermute | solution.py:24
  157.3 9.5 %collective-permute-start.24 = (f32[50,1,128]{2,1,0:T(1,128)S(1)}, f32[50,1,128]{2,1,0:T(1,128)S(1)}, u32[]{:S(2)}, u32[]{:S(2)}) collective-permute-start(f32[50,1,128]{2,1,0:T(1,128)S(1)} %get-tuple-element.93), channel_id=1, source_target_pairs={{0,4},{4,8},{8,12},{12,16},{16,20},{20,24},{24,28},{28,32},{32,36}... | collective-permute-start | bytes 76808 | tf_op jit(solution)/shard_map/ppermute | solution.py:22
  159.3 8.5 %collective-permute-start.25 = (f32[50,1,128]{2,1,0:T(1,128)S(1)}, f32[50,1,128]{2,1,0:T(1,128)S(1)}, u32[]{:S(2)}, u32[]{:S(2)}) collective-permute-start(f32[50,1,128]{2,1,0:T(1,128)S(1)} %get-tuple-element.94), channel_id=1, source_target_pairs={{4,0},{8,4},{12,8},{16,12},{20,16},{24,20},{28,24},{32,28},{36,32}... | collective-permute-start | bytes 76808 | tf_op jit(solution)/shard_map/ppermute | solution.py:24
  168.7 7.9 %collective-permute-start.27 = (f32[50,18,1]{0,1,2:T(8,128)S(1)}, f32[50,18,1]{0,1,2:T(8,128)S(1)}, u32[]{:S(2)}, u32[]{:S(2)}) collective-permute-start(f32[50,18,1]{0,1,2:T(8,128)S(1)} %copy.39), channel_id=1, source_target_pairs={{1,0},{2,1},{3,2},{5,4},{6,5},{7,6},{9,8},{10,9},{11,10},{13,12},{... | collective-permute-start | bytes 10808 | tf_op jit(solution)/shard_map/ppermute | solution.py:24
  179.9 11.8 %all-to-all-start.2 = ((f32[4,32,128]{2,1,0:T(8,128)}), f32[4,32,128]{2,1,0:T(8,128)S(1)}, u32[]{:S(2)}, u32[]{:S(2)}) async-start(f32[4,32,128]{2,1,0:T(8,128)} %fusion.181), calls=%async_computation.2 | async-start | bytes 131072 | tf_op jit(solution)/shard_map/all_to_all | solution.py:118
  (39 other events, 205.6 us)
where the time goes:
time: 196 us; the launch traced here: 194 us
  starting transfers between devices  118 us (60%)
  local copies, waits for them, and re-layouts  31.9 us (16%)
  other arithmetic  20.1 us (10%)
  waiting for transfers between devices  16.9 us (9%)
  matrix products  4.48 us (2%)
  between operations  2.21 us (1%)
    ppermute x14, starting transfers between devices, with_halo(): lax.ppermute(head, axis, [((i + 1) % count, i) for i in range(ends)])  56.6 us
    ppermute x14, starting transfers between devices, with_halo(): lax.ppermute(tail, axis, [(i, (i + 1) % count) for i in range(ends)])  46.8 us
    add x6, other arithmetic, lateral_core(): return centre + flow_rate * flux_total  10.6 us
    slice x19, local copies, waits for them, and re-layouts, with_halo(): lax.slice_in_dim(cells, cells.shape[dim] - width, cells.shape[dim], axis=...  9.47 us
    ppermute x7, local copies, waits for them, and re-layouts, with_halo(): lax.ppermute(head, axis, [((i + 1) % count, i) for i in range(ends)])  7.47 us
    unnamed x73, local copies, waits for them, and re-layouts  7.07 us
    ppermute x14, waiting for transfers between devices, with_halo(): lax.ppermute(tail, axis, [(i, (i + 1) % count) for i in range(ends)])  6.95 us
    all_to_all x1, starting transfers between devices, local(): lax.all_to_all(answered, 'gy', split_axis=0, concat_axis=0, tiled=True)  6.16 us
  transfers between devices with their start and end apart: 31, of which 12 were waited for; matrix products, arithmetic and copies ran while one was open for 8% of the time, Pallas kernels for 0%

commit v1 on v0

--- a/solution.py
+++ b/solution.py
@@ -97,20 +97,42 @@
     out_rows = (
         jnp.einsum("tcb,b->tc", placing, (offsets + 1).astype(jnp.float32), precision=highest) - 1.0
     )
-    incoming, in_rows = (
-        lax.all_to_all(outgoing, "gy", split_axis=0, concat_axis=0, tiled=True),
-        lax.all_to_all(out_rows, "gy", split_axis=0, concat_axis=0, tiled=True),
+    packed = jnp.concatenate(
+        [outgoing, jnp.pad(out_rows, ((0, 0), (0, tile_cols - capacity)))[:, None, :]], axis=1
     )
+    arrived = lax.all_to_all(packed, "gy", split_axis=0, concat_axis=0, tiled=True)
+    incoming = arrived[:, :capacity, :]
+    in_rows = arrived[:, capacity, :capacity]
     slot_total = tile_count * capacity
     landing = (
         in_rows.reshape(1, slot_total) == jnp.arange(tile_rows, dtype=jnp.float32)[:, None]
     ).astype(jnp.float32)
     recharge = jnp.dot(landing, incoming.reshape(slot_total, tile_cols), precision=highest)
     field = head.at[0].add(recharge)
-    padded_cond = with_halo(conductivity, (("gx", 1), ("gy", 2)), 1)
+    layers = field.shape[0]
+    both = with_halo(
+        jnp.concatenate([field, conductivity], axis=0), (("gx", 1), ("gy", 2)), SWEEPS
+    )
+    field = both[:layers]
+    padded_cond = both[layers:]
+    row_at = (
+        lax.axis_index("gx") * tile_rows - SWEEPS + jnp.arange(tile_rows + 2 * SWEEPS)
+    )[:, None]
+    col_at = (
+        lax.axis_index("gy") * tile_cols - SWEEPS + jnp.arange(tile_cols + 2 * SWEEPS)
+    )[None, :]
+    inside = (
+        (row_at >= 0)
+        & (row_at < tile_rows * lax.axis_size("gx"))
+        & (col_at >= 0)
+        & (col_at < tile_cols * tile_count)
+    )
     for sweep_k in range(SWEEPS):
-        padded_head = with_halo(field, (("gx", 1), ("gy", 2)), 1)
-        field = lateral_core(padded_head, padded_cond)
+        field = lateral_core(field, padded_cond)
+        padded_cond = padded_cond[:, 1:-1, 1:-1]
+        if sweep_k < SWEEPS - 1:
+            edge = sweep_k + 1
+            field = jnp.where(inside[None, edge:-edge, edge:-edge], field, 0.0)
     surface = field[0]
     answered = jnp.dot(landing.T, surface, precision=highest).reshape(
         tile_count, capacity, tile_cols

time: 196 us -> 98.9 us (0.50)
  the two profiles are of different devices: /device:TPU:512 before, /device:TPU:249 now
where the time goes in v1:
time: 98.9 us; the launch traced here: 98.2 us
  other arithmetic  40.5 us (41%)
  starting transfers between devices  19.8 us (20%)
  local copies, waits for them, and re-layouts  16.5 us (17%)
  waiting for transfers between devices  16.5 us (17%)
  matrix products  3.16 us (3%)
  between operations  1.73 us (2%)
    select_n x5, other arithmetic, local(): field = jnp.where(inside[None, edge:-edge, edge:-edge], field, 0.0)  17 us
    ppermute x2, waiting for transfers between devices, with_halo(): lax.ppermute(head, axis, [((i + 1) % count, i) for i in range(ends)])  9.74 us
    ppermute x2, starting transfers between devices, with_halo(): lax.ppermute(tail, axis, [(i, (i + 1) % count) for i in range(ends)])  8.9 us
    mul x6, other arithmetic, lateral_core(): 0.5 * (centre_cond[1:] + centre_cond[:-1]) * (centre[1:] - centre[:-1])  7.3 us
    unnamed x10, other arithmetic  7.21 us
    unnamed x37, local copies, waits for them, and re-layouts  7.12 us
    all_to_all x1, waiting for transfers between devices, local(): lax.all_to_all(answered, 'gy', split_axis=0, concat_axis=0, tiled=True)  4.47 us
    slice x2, local copies, waits for them, and re-layouts, with_halo(): lax.slice_in_dim(cells, cells.shape[dim] - width, cells.shape[dim], axis=...  4.08 us
  transfers between devices with their start and end apart: 6, of which 4 were waited for; matrix products, arithmetic and copies ran while one was open for 15% of the time, Pallas kernels for 0%

profile of v1, /device:TPU:249, one launch (start us, length us, event | category | flops | bytes accessed | tf_op | source)
XLA Modules:
  0.0 98.2 jit_solution(2096007398161947398)
XLA Ops:
  3.7 1.3 %fusion.171 = (f32[64,128]{1,0:T(8,128)S(1)}, f32[64,128]{1,0:T(8,128)S(1)}, f32[64,128]{1,0:T(8,128)S(1)}, f32[64,128]{1,0:T(8,128)S(1)}, f32[64,128]{1,0:T(8,1...) fusion(f32[64,20,128]{2,0,1:T(8,128)} %param.13, ...), kind=kLoop, calls=%fused_computation.353 | loop fusion | flops 1138688 | bytes 2326528 | tf_op jit(solution)/shard_map/div | solution.py:45
  5.1 1.6 %constant_dynamic-update-slice_fusion.19 = (f32[64,20,128]{2,0,1:T(8,128)}, f32[64,128]{1,0:T(8,128)S(1)}, f32[64,128]{1,0:T(8,128)S(1)}, f32[64,128]{1,0:T(8,12...) fusion(f32[64,20,128]{2,0,1:T(8,128)S(1)} %copy-done.9, ...), kind=kLoop, calls=%fused_computation.217 | loop fusion | flops 540671 | bytes 2064384
  8.0 4.0 %all-to-all-start = ((f32[4,33,128]{2,1,0:T(8,128)}), f32[4,33,128]{2,1,0:T(8,128)S(1)}, u32[]{:S(2)}, u32[]{:S(2)}) async-start(f32[4,33,128]{2,1,0:T(8,128)} %pad_maximum_fusion.15), calls=%async_computation | async-start | bytes 163840 | tf_op jit(solution)/shard_map/all_to_all | solution.py:103
  23.5 5.3 %collective-permute-start = (f32[100,6,128]{2,1,0:T(8,128)S(1)}, f32[100,6,128]{2,1,0:T(8,128)S(1)}, u32[]{:S(2)}, u32[]{:S(2)}) collective-permute-start(f32[100,6,128]{2,1,0:T(8,128)S(1)} %get-tuple-element.76), channel_id=1, source_target_pairs={{0,4},{4,8},{8,12},{12,16},{16,20},{20,24},{24,28},{28,32},{32,36}... | collective-permute-start | bytes 921608 | tf_op jit(solution)/shard_map/ppermute | solution.py:22
  28.8 1.9 %collective-permute-start.1 = (f32[100,6,128]{2,1,0:T(8,128)S(1)}, f32[100,6,128]{2,1,0:T(8,128)S(1)}, u32[]{:S(2)}, u32[]{:S(2)}) collective-permute-start(f32[100,6,128]{2,1,0:T(8,128)S(1)} %get-tuple-element.77), channel_id=1, source_target_pairs={{4,0},{8,4},{12,8},{16,12},{20,16},{24,20},{28,24},{32,28},{36,32}... | collective-permute-start | bytes 921608 | tf_op jit(solution)/shard_map/ppermute | solution.py:24
  31.3 2.3 %collective-permute-done = f32[100,6,128]{2,1,0:T(8,128)S(1)} collective-permute-done((f32[100,6,128]{2,1,0:T(8,128)S(1)}, f32[100,6,128]{2,1,0:T(8,128)S(1)}, u32[]{:S(2)}, u32[]{:S(2)}) %collective-permute-start) | collective-permute-done | bytes 307232 | tf_op jit(solution)/shard_map/ppermute | solution.py:22
  33.6 7.7 %collective-permute-done.1 = f32[100,6,128]{2,1,0:T(8,128)S(1)} collective-permute-done((f32[100,6,128]{2,1,0:T(8,128)S(1)}, f32[100,6,128]{2,1,0:T(8,128)S(1)}, u32[]{:S(2)}, u32[]{:S(2)}) %collective-permute-start.1) | collective-permute-done | bytes 307232 | tf_op jit(solution)/shard_map/ppermute | solution.py:24
  42.4 1.8 %fusion.233 = (f32[100,28,6]{2,1,0:T(8,128)}, f32[100,28,6]{2,1,0:T(8,128)S(1)}) fusion(f32[100,28,128]{2,1,0:T(8,128)S(1)} %pad_maximum_fusion.1), kind=kLoop, calls=%fused_computation.431 | loop fusion | bytes 268800 | tf_op jit(solution)/shard_map/slice | solution.py:19
  44.1 2.3 %copy.12 = f32[100,28,6]{0,1,2:T(8,128)S(1)} copy(f32[100,28,6]{2,1,0:T(8,128)} %get-tuple-element.74) | data formatting | bytes 134400 | tf_op jit(solution)/shard_map/slice | solution.py:19
  46.5 3.6 %collective-permute-start.2 = (f32[100,28,6]{0,1,2:T(8,128)S(1)}, f32[100,28,6]{0,1,2:T(8,128)S(1)}, u32[]{:S(2)}, u32[]{:S(2)}) collective-permute-start(f32[100,28,6]{0,1,2:T(8,128)S(1)} %copy.12), channel_id=1, source_target_pairs={{0,1},{1,2},{2,3},{4,5},{5,6},{6,7},{8,9},{9,10},{10,11},{12,13},{... | collective-permute-start | bytes 201608 | tf_op jit(solution)/shard_map/ppermute | solution.py:22
  53.0 1.5 %copy.14 = f32[100,28,6]{2,1,0:T(8,128)S(1)} copy(f32[100,28,6]{0,1,2:T(8,128)S(1)} %collective-permute-done.2) | data formatting | bytes 134400 | tf_op jit(solution)/shard_map/ppermute | solution.py:22
  54.5 2.0 %collective-permute-done.3 = f32[100,28,6]{0,1,2:T(8,128)S(1)} collective-permute-done((f32[100,28,6]{0,1,2:T(8,128)S(1)}, f32[100,28,6]{0,1,2:T(8,128)S(1)}, u32[]{:S(2)}, u32[]{:S(2)}) %collective-permute-start.3) | collective-permute-done | bytes 67232 | tf_op jit(solution)/shard_map/ppermute | solution.py:24
  56.6 1.5 %copy.15 = f32[100,28,6]{2,1,0:T(8,128)S(1)} copy(f32[100,28,6]{0,1,2:T(8,128)S(1)} %collective-permute-done.3) | data formatting | bytes 134400 | tf_op jit(solution)/shard_map/ppermute | solution.py:24
  58.1 3.2 %pad_maximum_fusion = f32[100,28,140]{2,1,0:T(8,128)S(1)} fusion(f32[100,28,6]{2,1,0:T(8,128)S(1)} %copy.15, f32[100,6,128]{2,1,0:T(8,128)} %copy-done.7, f32[50,16,128]{2,1,0:T(8,128)} %param.17, f32[50,16,128]{2,1,0:T(8,128)} %copy-done.2, f32[100,6,128]{2,1,0:T(8,128)} %copy-done.5, f32[100,28,6]{2,1,0:T(8,128)S(1)} %copy.14), kind=kLoop, calls=%fused_computation | loop fusion | flops 1960000 | bytes 3136000 | tf_op jit(solution)/shard_map/concatenate | solution.py:20
  61.3 1.8 %fusion.16 = f32[49,26,138]{2,1,0:T(8,128)S(1)} fusion(f32[100,28,140]{2,1,0:T(8,128)S(1)} %pad_maximum_fusion), kind=kLoop, calls=%fused_computation.27 | loop fusion | flops 703248 | bytes 3516240 | tf_op jit(solution)/shard_map/mul | solution.py:68
  63.1 3.8 %fusion.6 = f32[50,26,138]{2,1,0:T(8,128)S(1)} fusion(f32[100,28,140]{2,1,0:T(8,128)S(1)} %pad_maximum_fusion, f32[49,26,138]{2,1,0:T(8,128)S(1)} %fusion.16, pred[26,138]{1,0:T(8,128)(4,1)S(1)} %slice.682), kind=kLoop, calls=%fused_computation.8 | loop fusion | flops 4305600 | bytes 8600436 | tf_op jit(solution)/shard_map/jit(_where)/select_n | solution.py:135
  66.8 1.3 %fusion.88 = f32[49,24,136]{2,1,0:T(8,128)S(1)} fusion(f32[50,26,138]{2,1,0:T(8,128)S(1)} %fusion.6, f32[100,28,140]{2,1,0:T(8,128)S(1)} %pad_maximum_fusion), kind=kLoop, calls=%fused_computation.139 | loop fusion | flops 639744 | bytes 3198720 | tf_op jit(solution)/shard_map/mul | solution.py:68
  68.2 3.1 %fusion.72 = f32[50,24,136]{2,1,0:T(8,128)S(1)} fusion(f32[50,26,138]{2,1,0:T(8,128)S(1)} %fusion.6, f32[100,28,140]{2,1,0:T(8,128)S(1)} %pad_maximum_fusion, f32[49,24,136]{2,1,0:T(8,128)S(1)} %fusion.88, pred[24,136]{1,0:T(8,128)(4,1)S(1)} %slice.681), kind=kLoop, calls=%fused_computation.109 | loop fusion | flops 3916800 | bytes 7823808 | tf_op jit(solution)/shard_map/jit(_where)/select_n | solution.py:135
  72.5 3.1 %fusion.56 = f32[50,22,134]{2,1,0:T(8,128)S(1)} fusion(f32[50,24,136]{2,1,0:T(8,128)S(1)} %fusion.72, f32[100,28,140]{2,1,0:T(8,128)S(1)} %pad_maximum_fusion, f32[49,22,134]{2,1,0:T(8,128)S(1)} %fusion.86, pred[22,134]{1,0:T(8,128)(4,1)S(1)} %slice.680), kind=kLoop, calls=%fused_computation.85 | loop fusion | flops 3537600 | bytes 7066356 | tf_op jit(solution)/shard_map/jit(_where)/select_n | solution.py:135
  75.6 1.3 %fusion.84 = f32[49,20,132]{2,1,0:T(8,128)S(1)} fusion(f32[50,22,134]{2,1,0:T(8,128)S(1)} %fusion.56, f32[100,28,140]{2,1,0:T(8,128)S(1)} %pad_maximum_fusion), kind=kLoop, calls=%fused_computation.131 | loop fusion | flops 517440 | bytes 2587200 | tf_op jit(solution)/shard_map/mul | solution.py:68
  77.0 3.1 %fusion.40 = f32[50,20,132]{2,1,0:T(8,128)S(1)} fusion(f32[50,22,134]{2,1,0:T(8,128)S(1)} %fusion.56, f32[100,28,140]{2,1,0:T(8,128)S(1)} %pad_maximum_fusion, f32[49,20,132]{2,1,0:T(8,128)S(1)} %fusion.84, pred[20,132]{1,0:T(8,128)(4,1)S(1)} %slice.679), kind=kLoop, calls=%fused_computation.61 | loop fusion | flops 3168000 | bytes 6328080 | tf_op jit(solution)/shard_map/jit(_where)/select_n | solution.py:135
  81.5 4.0 %fusion.24 = f32[50,18,130]{2,1,0:T(8,128)S(1)} fusion(f32[50,20,132]{2,1,0:T(8,128)S(1)} %fusion.40, f32[100,28,6]{2,1,0:T(8,128)S(1)} %copy.15, f32[100,6,128]{2,1,0:T(8,128)S(1)} %copy-done.8, f32[100,6,128]{2,1,0:T(8,128)S(1)} %copy-done.6, f32[50,16,128]{2,1,0:T(8,128)S(1)} %copy-done.1, f32[50,16,128]{2,1,0:T(8,128)S(1)} %copy-done.3, ...), kind=kLoop, calls=%fused_computation.37 | loop fusion | flops 3744000 | bytes 6240980 | tf_op jit(solution)/shard_map/jit(_where)/select_n | solution.py:135
  88.4 3.7 %all-to-all-start.1 = ((f32[4,32,128]{2,1,0:T(8,128)}), f32[4,32,128]{2,1,0:T(8,128)S(1)}, u32[]{:S(2)}, u32[]{:S(2)}) async-start(f32[4,32,128]{2,1,0:T(8,128)} %fusion.188), calls=%async_computation.1 | async-start | bytes 131072 | tf_op jit(solution)/shard_map/all_to_all | solution.py:140
  92.1 4.5 %all-to-all-done.1 = f32[4,32,128]{2,1,0:T(8,128)S(1)} async-done(((f32[4,32,128]{2,1,0:T(8,128)}), f32[4,32,128]{2,1,0:T(8,128)S(1)}, u32[]{:S(2)}, u32[]{:S(2)}) %all-to-all-start.1) | async-done | bytes 65568 | tf_op jit(solution)/shard_map/all_to_all | solution.py:140
  (84 shorter events, 26.8 us)
Async XLA Ops:
  0.6 3.1 %copy-start.9 = (f32[64,20,128]{2,0,1:T(8,128)S(1)}, f32[64,20,128]{2,0,1:T(8,128)}, u32[]{:S(2)}) copy-start(f32[64,20,128]{2,0,1:T(8,128)} %param.14) | copy-start | bytes 1966084
  2.9 2.2 %copy-start.11 = (f32[64,128]{1,0:T(8,128)S(1)}, f32[64,128]{1,0:T(8,128)}, u32[]{:S(2)}) copy-start(f32[64,128]{1,0:T(8,128)} %param.15) | copy-start | bytes 98308
  5.1 1.9 %copy-start.13 = (s32[64]{0:T(128)S(1)}, s32[64]{0:T(128)}, u32[]{:S(2)}) copy-start(s32[64]{0:T(128)} %param.19) | copy-start | bytes 772
  6.7 16.6 %copy-start.4 = (f32[50,16,128]{2,1,0:T(8,128)S(1)}, f32[50,16,128]{2,1,0:T(8,128)}, u32[]{:S(2)}) copy-start(f32[50,16,128]{2,1,0:T(8,128)} %param.16) | copy-start | bytes 1228804
  6.9 16.5 %copy-start = (f32[50,16,128]{2,1,0:T(8,128)S(1)}, f32[50,16,128]{2,1,0:T(8,128)}, u32[]{:S(2)}) copy-start(f32[50,16,128]{2,1,0:T(8,128)} %param.17) | copy-start | bytes 1228804
  8.0 15.2 %all-to-all-start = ((f32[4,33,128]{2,1,0:T(8,128)}), f32[4,33,128]{2,1,0:T(8,128)S(1)}, u32[]{:S(2)}, u32[]{:S(2)}) async-start(f32[4,33,128]{2,1,0:T(8,128)} %pad_maximum_fusion.15), calls=%async_computation | async-start | bytes 163840 | tf_op jit(solution)/shard_map/all_to_all | solution.py:103
  23.4 19.0 %copy-start.2 = (f32[50,16,128]{2,1,0:T(8,128)}, f32[50,16,128]{2,1,0:T(8,128)S(1)}, u32[]{:S(2)}) copy-start(f32[50,16,128]{2,1,0:T(8,128)S(1)} %fusion.91) | copy-start | bytes 1228804
  23.5 10.1 %collective-permute-start = (f32[100,6,128]{2,1,0:T(8,128)S(1)}, f32[100,6,128]{2,1,0:T(8,128)S(1)}, u32[]{:S(2)}, u32[]{:S(2)}) collective-permute-start(f32[100,6,128]{2,1,0:T(8,128)S(1)} %get-tuple-element.76), channel_id=1, source_target_pairs={{0,4},{4,8},{8,12},{12,16},{16,20},{20,24},{24,28},{28,32},{32,36}... | collective-permute-start | bytes 921608 | tf_op jit(solution)/shard_map/ppermute | solution.py:22
  28.8 12.6 %collective-permute-start.1 = (f32[100,6,128]{2,1,0:T(8,128)S(1)}, f32[100,6,128]{2,1,0:T(8,128)S(1)}, u32[]{:S(2)}, u32[]{:S(2)}) collective-permute-start(f32[100,6,128]{2,1,0:T(8,128)S(1)} %get-tuple-element.77), channel_id=1, source_target_pairs={{4,0},{8,4},{12,8},{16,12},{20,16},{24,20},{28,24},{32,28},{36,32}... | collective-permute-start | bytes 921608 | tf_op jit(solution)/shard_map/ppermute | solution.py:24
  33.6 7.7 %copy-start.5 = (f32[100,6,128]{2,1,0:T(8,128)}, f32[100,6,128]{2,1,0:T(8,128)S(1)}, u32[]{:S(2)}) copy-start(f32[100,6,128]{2,1,0:T(8,128)S(1)} %collective-permute-done) | copy-start | bytes 921604
  41.4 0.8 copy-start.7
  46.5 6.5 %collective-permute-start.2 = (f32[100,28,6]{0,1,2:T(8,128)S(1)}, f32[100,28,6]{0,1,2:T(8,128)S(1)}, u32[]{:S(2)}, u32[]{:S(2)}) collective-permute-start(f32[100,28,6]{0,1,2:T(8,128)S(1)} %copy.12), channel_id=1, source_target_pairs={{0,1},{1,2},{2,3},{4,5},{5,6},{6,7},{8,9},{9,10},{10,11},{12,13},{... | collective-permute-start | bytes 201608 | tf_op jit(solution)/shard_map/ppermute | solution.py:22
  51.2 5.4 %collective-permute-start.3 = (f32[100,28,6]{0,1,2:T(8,128)S(1)}, f32[100,28,6]{0,1,2:T(8,128)S(1)}, u32[]{:S(2)}, u32[]{:S(2)}) collective-permute-start(f32[100,28,6]{0,1,2:T(8,128)S(1)} %copy.13), channel_id=1, source_target_pairs={{1,0},{2,1},{3,2},{5,4},{6,5},{7,6},{9,8},{10,9},{11,10},{13,12},{... | collective-permute-start | bytes 201608 | tf_op jit(solution)/shard_map/ppermute | solution.py:24
  80.1 1.4 %copy-start.1 = (f32[50,16,128]{2,1,0:T(8,128)S(1)}, f32[50,16,128]{2,1,0:T(8,128)}, u32[]{:S(2)}) copy-start(f32[50,16,128]{2,1,0:T(8,128)} %param.17) | copy-start | bytes 1228804
  80.1 1.4 %copy-start.3 = (f32[50,16,128]{2,1,0:T(8,128)S(1)}, f32[50,16,128]{2,1,0:T(8,128)}, u32[]{:S(2)}) copy-start(f32[50,16,128]{2,1,0:T(8,128)} %copy-done.2) | copy-start | bytes 1228804
  80.1 1.4 %copy-start.6 = (f32[100,6,128]{2,1,0:T(8,128)S(1)}, f32[100,6,128]{2,1,0:T(8,128)}, u32[]{:S(2)}) copy-start(f32[100,6,128]{2,1,0:T(8,128)} %copy-done.5) | copy-start | bytes 921604
  80.1 1.4 %copy-start.8 = (f32[100,6,128]{2,1,0:T(8,128)S(1)}, f32[100,6,128]{2,1,0:T(8,128)}, u32[]{:S(2)}) copy-start(f32[100,6,128]{2,1,0:T(8,128)} %copy-done.7) | copy-start | bytes 921604
  85.7 11.7 %copy-start.12 = (s32[64]{0:T(128)S(1)}, s32[64]{0:T(128)}, u32[]{:S(2)}) copy-start(s32[64]{0:T(128)} %param.20) | copy-start | bytes 772
  86.8 0.8 copy-start.10
  88.4 8.1 %all-to-all-start.1 = ((f32[4,32,128]{2,1,0:T(8,128)}), f32[4,32,128]{2,1,0:T(8,128)S(1)}, u32[]{:S(2)}, u32[]{:S(2)}) async-start(f32[4,32,128]{2,1,0:T(8,128)} %fusion.188), calls=%async_computation.1 | async-start | bytes 131072 | tf_op jit(solution)/shard_map/all_to_all | solution.py:140

commit v2 on v1

--- a/solution.py
+++ b/solution.py
@@ -48,7 +48,7 @@
     solved = [forward_vals[-1]]
     for layer_k in range(depth - 2, -1, -1):
         solved.append(forward_vals[layer_k] + ratios[layer_k] * solved[-1])
-    return jnp.stack(solved[::-1], axis=1)
+    return solved[::-1]
 
 
 def lateral_core(padded_head, padded_cond):
@@ -82,7 +82,7 @@
     tile_rows = head.shape[1]
     tile_cols = head.shape[2]
     wet = column_solve(moisture, diffusivity, rain)
-    bottom = wet[:, -1, :]
+    bottom = wet[-1]
     drain = diffusivity[:, -1, :] * bottom
     in_use = jnp.arange(block_count, dtype=jnp.int32) < counts[0]
     in_use_f = in_use.astype(jnp.float32)
@@ -108,13 +108,12 @@
         in_rows.reshape(1, slot_total) == jnp.arange(tile_rows, dtype=jnp.float32)[:, None]
     ).astype(jnp.float32)
     recharge = jnp.dot(landing, incoming.reshape(slot_total, tile_cols), precision=highest)
-    field = head.at[0].add(recharge)
-    layers = field.shape[0]
-    both = with_halo(
-        jnp.concatenate([field, conductivity], axis=0), (("gx", 1), ("gy", 2)), SWEEPS
-    )
-    field = both[:layers]
-    padded_cond = both[layers:]
+    layers = head.shape[0]
+    sides = (("gx", 1), ("gy", 2))
+    rest = with_halo(jnp.concatenate([head[1:], conductivity], axis=0), sides, SWEEPS)
+    top = with_halo(head[:1] + recharge[None], sides, SWEEPS)
+    field = jnp.concatenate([top, rest[: layers - 1]], axis=0)
+    padded_cond = rest[layers - 1 :]
     row_at = (
         lax.axis_index("gx") * tile_rows - SWEEPS + jnp.arange(tile_rows + 2 * SWEEPS)
     )[:, None]
@@ -140,7 +139,7 @@
     returned = lax.all_to_all(answered, "gy", split_axis=0, concat_axis=0, tiled=True)
     saturation = jnp.einsum("tcb,tcj->bj", placing, returned, precision=highest)
     new_bottom = bottom + capillary * (saturation - in_use_f[:, None] * bottom)
-    moisture_out = wet.at[:, -1, :].set(new_bottom)
+    moisture_out = jnp.stack(wet[:-1] + [new_bottom], axis=1)
     patch_hot = (patch_ids[None, :] == jnp.arange(PATCH_DEV, dtype=jnp.int32)[:, None]).astype(
         jnp.float32
     )

time: 98.9 us -> 117 us (1.18)
  starting transfers between devices: 19.8 us -> 35.1 us
  waiting for transfers between devices: 16.5 us -> 10.3 us
  other arithmetic: 40.5 us -> 45.3 us
  local copies, waits for them, and re-layouts: 16.5 us -> 19.4 us
    ppermute x2 -> x4, starting transfers between devices: 8.9 us -> 19.8 us  [with_halo(): lax.ppermute(tail, axis, [(i, (i + 1) % count) for i in range(ends)])]
    ppermute x2 -> x4, waiting for transfers between devices: 9.74 us -> 5.81 us  [with_halo(): lax.ppermute(head, axis, [((i + 1) % count, i) for i in range(ends)])]
    ppermute x2 -> x4, starting transfers between devices: 3.21 us -> 6.42 us  [with_halo(): lax.ppermute(head, axis, [((i + 1) % count, i) for i in range(ends)])]
    unnamed x37 -> x59, local copies, waits for them, and re-layouts: 7.12 us -> 9.94 us
    unnamed x10, other arithmetic: 7.21 us -> 9.52 us
    ppermute x2 -> x4, waiting for transfers between devices: 2.32 us -> 0.01 us  [with_halo(): lax.ppermute(tail, axis, [(i, (i + 1) % count) for i in range(ends)])]
    concatenate x1 -> x2, other arithmetic: 0.06 us -> 2.16 us  [the longest x1 1.23 us: local(): jnp.concatenate([head[1:], conductivity], axis=0)]
    convert_element_type x2, other arithmetic: 1.4 us -> 0.09 us  [local(): to_tile = ((tile_ids[:, None] == jnp.arange(tile_count, dtype=jnp.int32)[...]
  transfers between devices with their start and end apart: 6 -> 10, of which waited for: 4 -> 2; matrix products, arithmetic and copies ran while one was open for 15% -> 25% of each run, Pallas kernels for 0% -> 0%
where the time goes in v2:
time: 117 us; the launch traced here: 116 us
  other arithmetic  45.3 us (39%)
  starting transfers between devices  35.1 us (30%)
  local copies, waits for them, and re-layouts  19.4 us (17%)
  waiting for transfers between devices  10.3 us (9%)
  matrix products  3.86 us (3%)
  between operations  1.88 us (2%)
    ppermute x4, starting transfers between devices, with_halo(): lax.ppermute(tail, axis, [(i, (i + 1) % count) for i in range(ends)])  19.8 us
    select_n x5, other arithmetic, local(): field = jnp.where(inside[None, edge:-edge, edge:-edge], field, 0.0)  18.2 us
    unnamed x59, local copies, waits for them, and re-layouts  9.94 us
    unnamed x10, other arithmetic  9.52 us
    mul x6, other arithmetic, lateral_core(): 0.5 * (centre_cond[1:] + centre_cond[:-1]) * (centre[1:] - centre[:-1])  7.31 us
    ppermute x4, starting transfers between devices, with_halo(): lax.ppermute(head, axis, [((i + 1) % count, i) for i in range(ends)])  6.42 us
    ppermute x4, waiting for transfers between devices, with_halo(): lax.ppermute(head, axis, [((i + 1) % count, i) for i in range(ends)])  5.81 us
    all_to_all x1, starting transfers between devices, local(): lax.all_to_all(answered, 'gy', split_axis=0, concat_axis=0, tiled=True)  4.86 us
  transfers between devices with their start and end apart: 10, of which 2 were waited for; matrix products, arithmetic and copies ran while one was open for 25% of the time, Pallas kernels for 0%

profile of v2, /device:TPU:249, one launch (start us, length us, event | category | flops | bytes accessed | tf_op | source)
XLA Modules:
  0.0 115.9 jit_solution(927099498655780503)
XLA Ops:
  3.1 5.0 %collective-permute-start.4 = (f32[99,6,128]{2,1,0:T(8,128)S(1)}, f32[99,6,128]{2,1,0:T(8,128)}, u32[]{:S(2)}, u32[]{:S(2)}) collective-permute-start(f32[99,6,128]{2,1,0:T(8,128)S(1)} %get-tuple-element.52), channel_id=1, source_target_pairs={{0,4},{4,8},{8,12},{12,16},{16,20},{20,24},{24,28},{28,32},{32,36}... | collective-permute-start | bytes 912392 | tf_op jit(solution)/shard_map/ppermute | solution.py:22
  8.0 1.9 %collective-permute-start.5 = (f32[99,6,128]{2,1,0:T(8,128)S(1)}, f32[99,6,128]{2,1,0:T(8,128)}, u32[]{:S(2)}, u32[]{:S(2)}) collective-permute-start(f32[99,6,128]{2,1,0:T(8,128)S(1)} %get-tuple-element.53), channel_id=1, source_target_pairs={{4,0},{8,4},{12,8},{16,12},{20,16},{24,20},{28,24},{32,28},{36,32}... | collective-permute-start | bytes 912392 | tf_op jit(solution)/shard_map/ppermute | solution.py:24
  13.5 4.0 %all-to-all-start = ((f32[4,33,128]{2,1,0:T(8,128)}), f32[4,33,128]{2,1,0:T(8,128)S(1)}, u32[]{:S(2)}, u32[]{:S(2)}) async-start(f32[4,33,128]{2,1,0:T(8,128)} %pad_maximum_fusion.16), calls=%async_computation | async-start | bytes 163840 | tf_op jit(solution)/shard_map/all_to_all | solution.py:103
  18.9 1.4 %constant_dynamic-update-slice_fusion.17 = f32[64,20,128]{2,0,1:T(8,128)} fusion(f32[64,20,128]{2,0,1:T(8,128)} %constant_dynamic-update-slice_fusion.18, f32[64,128]{1,0:T(8,128)S(1)} %get-tuple-element.31, f32[64,128]{1,0:T(8,128)S(1)} %get-tuple-element.48, f32[64,128]{1,0:T(8,128)} %get-tuple-element.5), kind=kLoop, calls=%fused_computation.215 | loop fusion | flops 16384 | bytes 131072
  21.7 1.4 %constant_dynamic-update-slice_fusion.15 = f32[64,20,128]{2,0,1:T(8,128)} fusion(f32[64,20,128]{2,0,1:T(8,128)} %constant_dynamic-update-slice_fusion.16, f32[64,128]{1,0:T(8,128)S(1)} %get-tuple-element.29, f32[64,128]{1,0:T(8,128)S(1)} %get-tuple-element.46, f32[64,128]{1,0:T(8,128)} %get-tuple-element.6), kind=kLoop, calls=%fused_computation.213 | loop fusion | flops 16384 | bytes 131072
  24.4 1.4 %constant_dynamic-update-slice_fusion.13 = f32[64,20,128]{2,0,1:T(8,128)} fusion(f32[64,20,128]{2,0,1:T(8,128)} %constant_dynamic-update-slice_fusion.14, f32[64,128]{1,0:T(8,128)S(1)} %get-tuple-element.27, f32[64,128]{1,0:T(8,128)S(1)} %get-tuple-element.44, f32[64,128]{1,0:T(8,128)} %get-tuple-element.7), kind=kLoop, calls=%fused_computation.211 | loop fusion | flops 16384 | bytes 131072
  36.3 7.2 %collective-permute-start = (f32[1,6,128]{2,1,0:T(8,128)S(1)}, f32[1,6,128]{2,1,0:T(8,128)S(1)}, u32[]{:S(2)}, u32[]{:S(2)}) collective-permute-start(f32[1,6,128]{2,1,0:T(8,128)S(1)} %get-tuple-element.58), channel_id=1, source_target_pairs={{0,4},{4,8},{8,12},{12,16},{16,20},{20,24},{24,28},{28,32},{32,36}... | collective-permute-start | bytes 9224 | tf_op jit(solution)/shard_map/ppermute | solution.py:22
  43.6 1.9 %collective-permute-start.1 = (f32[1,6,128]{2,1,0:T(8,128)S(1)}, f32[1,6,128]{2,1,0:T(8,128)S(1)}, u32[]{:S(2)}, u32[]{:S(2)}) collective-permute-start(f32[1,6,128]{2,1,0:T(8,128)S(1)} %get-tuple-element.59), channel_id=1, source_target_pairs={{4,0},{8,4},{12,8},{16,12},{20,16},{24,20},{28,24},{32,28},{36,32}... | collective-permute-start | bytes 9224 | tf_op jit(solution)/shard_map/ppermute | solution.py:24
  46.0 5.8 %collective-permute-done.1 = f32[1,6,128]{2,1,0:T(8,128)S(1)} collective-permute-done((f32[1,6,128]{2,1,0:T(8,128)S(1)}, f32[1,6,128]{2,1,0:T(8,128)S(1)}, u32[]{:S(2)}, u32[]{:S(2)}) %collective-permute-start.1) | collective-permute-done | bytes 3104 | tf_op jit(solution)/shard_map/ppermute | solution.py:24
  53.9 1.7 %copy.12 = f32[99,28,6]{0,1,2:T(8,128)} copy(f32[99,28,6]{2,1,0:T(8,128)S(1)} %get-tuple-element.50) | data formatting | bytes 133056 | tf_op jit(solution)/shard_map/slice | solution.py:19
  57.9 4.3 %collective-permute-start.6 = (f32[99,28,6]{0,1,2:T(8,128)S(1)}, f32[99,28,6]{0,1,2:T(8,128)S(1)}, u32[]{:S(2)}, u32[]{:S(2)}) collective-permute-start(f32[99,28,6]{0,1,2:T(8,128)S(1)} %copy-done.14), channel_id=1, source_target_pairs={{0,1},{1,2},{2,3},{4,5},{5,6},{6,7},{8,9},{9,10},{10,11},{12,13},{... | collective-permute-start | bytes 199592 | tf_op jit(solution)/shard_map/ppermute | solution.py:22
  62.9 3.3 %collective-permute-start.2 = (f32[1,28,6]{2,1,0:T(8,128)}, f32[1,28,6]{2,1,0:T(8,128)S(1)}, u32[]{:S(2)}, u32[]{:S(2)}) collective-permute-start(f32[1,28,6]{2,1,0:T(8,128)} %get-tuple-element.56), channel_id=1, source_target_pairs={{0,1},{1,2},{2,3},{4,5},{5,6},{6,7},{8,9},{9,10},{10,11},{12,13},{... | collective-permute-start | bytes 2024 | tf_op jit(solution)/shard_map/ppermute | solution.py:22
  67.5 1.5 %copy.14 = f32[99,28,6]{2,1,0:T(8,128)S(1)} copy(f32[99,28,6]{0,1,2:T(8,128)S(1)} %collective-permute-done.6) | data formatting | bytes 133056 | tf_op jit(solution)/shard_map/ppermute | solution.py:22
  69.1 1.5 %copy.15 = f32[99,28,6]{2,1,0:T(8,128)S(1)} copy(f32[99,28,6]{0,1,2:T(8,128)S(1)} %collective-permute-done.7) | data formatting | bytes 133056 | tf_op jit(solution)/shard_map/ppermute | solution.py:24
  70.6 3.1 %pad_maximum_fusion = f32[99,28,140]{2,1,0:T(8,128)S(1)} fusion(f32[99,28,6]{2,1,0:T(8,128)S(1)} %copy.15, f32[99,6,128]{2,1,0:T(8,128)} %collective-permute-done.5, f32[50,16,128]{2,1,0:T(8,128)} %param.13, f32[49,16,128]{2,1,0:T(8,128)} %copy-done.2, f32[99,6,128]{2,1,0:T(8,128)} %collective-permute-done.4, f32[99,28,6]{2,1,0:T(8,128)S(1)} %copy.14), kind=kLoop, calls=%fused_computation | loop fusion | flops 1940400 | bytes 3104640 | tf_op jit(solution)/shard_map/concatenate | solution.py:20
  75.4 1.8 %fusion.16 = f32[49,26,138]{2,1,0:T(8,128)S(1)} fusion(f32[50,28,140]{2,1,0:T(8,128)S(1)} %pad_maximum_fusion.1, f32[99,28,140]{2,1,0:T(8,128)S(1)} %pad_maximum_fusion), kind=kLoop, calls=%fused_computation.28 | loop fusion | flops 703248 | bytes 3516240 | tf_op jit(solution)/shard_map/mul | solution.py:68
  77.2 3.8 %fusion.6 = f32[50,26,138]{2,1,0:T(8,128)S(1)} fusion(f32[50,28,140]{2,1,0:T(8,128)S(1)} %pad_maximum_fusion.1, f32[99,28,140]{2,1,0:T(8,128)S(1)} %pad_maximum_fusion, f32[49,26,138]{2,1,0:T(8,128)S(1)} %fusion.16, pred[26,138]{1,0:T(8,128)(4,1)S(1)} %slice.663), kind=kLoop, calls=%fused_computation.8 | loop fusion | flops 4305600 | bytes 8600436 | tf_op jit(solution)/shard_map/jit(_where)/select_n | solution.py:134
  82.3 3.1 %fusion.72 = f32[50,24,136]{2,1,0:T(8,128)S(1)} fusion(f32[50,26,138]{2,1,0:T(8,128)S(1)} %fusion.6, f32[99,28,140]{2,1,0:T(8,128)S(1)} %pad_maximum_fusion, f32[49,24,136]{2,1,0:T(8,128)S(1)} %fusion.88, pred[24,136]{1,0:T(8,128)(4,1)S(1)} %slice.662), kind=kLoop, calls=%fused_computation.110 | loop fusion | flops 3916800 | bytes 7823808 | tf_op jit(solution)/shard_map/jit(_where)/select_n | solution.py:134
  86.7 3.1 %fusion.56 = f32[50,22,134]{2,1,0:T(8,128)S(1)} fusion(f32[50,24,136]{2,1,0:T(8,128)S(1)} %fusion.72, f32[99,28,140]{2,1,0:T(8,128)S(1)} %pad_maximum_fusion, f32[49,22,134]{2,1,0:T(8,128)S(1)} %fusion.86, pred[22,134]{1,0:T(8,128)(4,1)S(1)} %slice.661), kind=kLoop, calls=%fused_computation.86 | loop fusion | flops 3537600 | bytes 7066356 | tf_op jit(solution)/shard_map/jit(_where)/select_n | solution.py:134
  91.1 3.1 %fusion.40 = f32[50,20,132]{2,1,0:T(8,128)S(1)} fusion(f32[50,22,134]{2,1,0:T(8,128)S(1)} %fusion.56, f32[99,28,140]{2,1,0:T(8,128)S(1)} %pad_maximum_fusion, f32[49,20,132]{2,1,0:T(8,128)S(1)} %fusion.84, pred[20,132]{1,0:T(8,128)(4,1)S(1)} %slice.660), kind=kLoop, calls=%fused_computation.62 | loop fusion | flops 3168000 | bytes 6328080 | tf_op jit(solution)/shard_map/jit(_where)/select_n | solution.py:134
  95.5 5.1 %fusion.24 = f32[50,18,130]{2,1,0:T(8,128)S(1)} fusion(f32[50,20,132]{2,1,0:T(8,128)S(1)} %fusion.40, f32[99,28,6]{2,1,0:T(8,128)S(1)} %copy.15, f32[99,6,128]{2,1,0:T(8,128)} %collective-permute-done.5, f32[99,6,128]{2,1,0:T(8,128)} %collective-permute-done.4, f32[50,16,128]{2,1,0:T(8,128)S(1)} %copy-done.1, f32[49,16,128]{2,1,0:T(8,128)S(1)} %copy-done.3, ...), kind=kLoop, calls=%fused_computation.38 | loop fusion | flops 3744000 | bytes 6225300 | tf_op jit(solution)/shard_map/jit(_where)/select_n | solution.py:134
  101.0 2.3 %fusion.96 = f32[50,16,128]{2,1,0:T(8,128)S(1)} fusion(f32[50,18,130]{2,1,0:T(8,128)S(1)} %fusion.24, f32[50,16,128]{2,1,0:T(8,128)S(1)} %copy-done.1, f32[99,28,6]{2,1,0:T(8,128)S(1)} %copy.15, f32[99,6,128]{2,1,0:T(8,128)} %collective-permute-done.5, f32[99,6,128]{2,1,0:T(8,128)} %collective-permute-done.4, f32[49,16,128]{2,1,0:T(8,128)S(1)} %copy-done.3, ...), kind=kLoop, calls=%fused_computation.154 | loop fusion | flops 3584000 | bytes 4411328 | tf_op jit(solution)/shard_map/add | solution.py:74
  104.9 4.9 %all-to-all-start.1 = ((f32[4,32,128]{2,1,0:T(8,128)}), f32[4,32,128]{2,1,0:T(8,128)S(1)}, u32[]{:S(2)}, u32[]{:S(2)}) async-start(f32[4,32,128]{2,1,0:T(8,128)} %fusion.187), calls=%async_computation.1 | async-start | bytes 131072 | tf_op jit(solution)/shard_map/all_to_all | solution.py:139
  109.8 4.5 %all-to-all-done.1 = f32[4,32,128]{2,1,0:T(8,128)S(1)} async-done(((f32[4,32,128]{2,1,0:T(8,128)}), f32[4,32,128]{2,1,0:T(8,128)S(1)}, u32[]{:S(2)}, u32[]{:S(2)}) %all-to-all-start.1) | async-done | bytes 65568 | tf_op jit(solution)/shard_map/all_to_all | solution.py:139
  (119 shorter events, 36.9 us)
Async XLA Ops:
  0.6 10.4 %copy-start.24 = (s32[64]{0:T(128)S(1)}, s32[64]{0:T(128)}, u32[]{:S(2)}) copy-start(s32[64]{0:T(128)} %param.15) | copy-start | bytes 772
  0.7 10.8 %copy-start.4 = (f32[64,20,128]{2,0,1:T(8,128)S(1)}, f32[64,20,128]{2,0,1:T(8,128)}, u32[]{:S(2)}) copy-start(f32[64,20,128]{2,0,1:T(8,128)} %param.10) | copy-start | bytes 1966084
  0.7 10.8 %copy-start.11 = (f32[64,128]{1,0:T(8,128)S(1)}, f32[64,128]{1,0:T(8,128)}, u32[]{:S(2)}) copy-start(f32[64,128]{1,0:T(8,128)} %param.11) | copy-start | bytes 98308
  0.7 10.8 %copy-start.5 = (f32[64,20,128]{2,0,1:T(8,128)S(1)}, f32[64,20,128]{2,0,1:T(8,128)}, u32[]{:S(2)}) copy-start(f32[64,20,128]{2,0,1:T(8,128)} %param.9) | copy-start | bytes 1966084
  1.8 50.0 %copy-start.2 = (f32[49,16,128]{2,1,0:T(8,128)}, f32[49,16,128]{2,1,0:T(8,128)S(1)}, u32[]{:S(2)}) copy-start(f32[49,16,128]{2,1,0:T(8,128)S(1)} %slice.569) | copy-start | bytes 1204228
  3.1 48.8 %collective-permute-start.4 = (f32[99,6,128]{2,1,0:T(8,128)S(1)}, f32[99,6,128]{2,1,0:T(8,128)}, u32[]{:S(2)}, u32[]{:S(2)}) collective-permute-start(f32[99,6,128]{2,1,0:T(8,128)S(1)} %get-tuple-element.52), channel_id=1, source_target_pairs={{0,4},{4,8},{8,12},{12,16},{16,20},{20,24},{24,28},{28,32},{32,36}... | collective-permute-start | bytes 912392 | tf_op jit(solution)/shard_map/ppermute | solution.py:22
  8.0 43.8 %collective-permute-start.5 = (f32[99,6,128]{2,1,0:T(8,128)S(1)}, f32[99,6,128]{2,1,0:T(8,128)}, u32[]{:S(2)}, u32[]{:S(2)}) collective-permute-start(f32[99,6,128]{2,1,0:T(8,128)S(1)} %get-tuple-element.53), channel_id=1, source_target_pairs={{4,0},{8,4},{12,8},{16,12},{20,16},{24,20},{28,24},{32,28},{36,32}... | collective-permute-start | bytes 912392 | tf_op jit(solution)/shard_map/ppermute | solution.py:24
  12.6 16.0 %copy-start.10 = (f32[64,128]{1,0:T(8,128)S(1)}, f32[64,128]{1,0:T(8,128)}, u32[]{:S(2)}) copy-start(f32[64,128]{1,0:T(8,128)} %get-tuple-element.8) | copy-start | bytes 98308
  12.6 16.6 %copy-start.9 = (f32[64,128]{1,0:T(8,128)S(1)}, f32[64,128]{1,0:T(8,128)}, u32[]{:S(2)}) copy-start(f32[64,128]{1,0:T(8,128)} %get-tuple-element.9) | copy-start | bytes 98308
  12.6 17.8 %copy-start.8 = (f32[64,128]{1,0:T(8,128)S(1)}, f32[64,128]{1,0:T(8,128)}, u32[]{:S(2)}) copy-start(f32[64,128]{1,0:T(8,128)} %get-tuple-element.10) | copy-start | bytes 98308
  12.6 19.1 %copy-start.7 = (f32[64,128]{1,0:T(8,128)S(1)}, f32[64,128]{1,0:T(8,128)}, u32[]{:S(2)}) copy-start(f32[64,128]{1,0:T(8,128)} %get-tuple-element.11) | copy-start | bytes 98308
  12.6 21.5 %copy-start.12 = (f32[64,128]{1,0:T(8,128)S(1)}, f32[64,128]{1,0:T(8,128)}, u32[]{:S(2)}) copy-start(f32[64,128]{1,0:T(8,128)} %get-tuple-element.14) | copy-start | bytes 98308
  12.6 21.5 %copy-start.13 = (f32[64,128]{1,0:T(8,128)S(1)}, f32[64,128]{1,0:T(8,128)}, u32[]{:S(2)}) copy-start(f32[64,128]{1,0:T(8,128)} %get-tuple-element.15) | copy-start | bytes 98308
  12.9 39.0 %copy-start = (f32[50,16,128]{2,1,0:T(8,128)S(1)}, f32[50,16,128]{2,1,0:T(8,128)}, u32[]{:S(2)}) copy-start(f32[50,16,128]{2,1,0:T(8,128)} %param.13) | copy-start | bytes 1228804
  13.5 21.3 %all-to-all-start = ((f32[4,33,128]{2,1,0:T(8,128)}), f32[4,33,128]{2,1,0:T(8,128)S(1)}, u32[]{:S(2)}, u32[]{:S(2)}) async-start(f32[4,33,128]{2,1,0:T(8,128)} %pad_maximum_fusion.16), calls=%async_computation | async-start | bytes 163840 | tf_op jit(solution)/shard_map/all_to_all | solution.py:103
  36.3 9.7 %collective-permute-start = (f32[1,6,128]{2,1,0:T(8,128)S(1)}, f32[1,6,128]{2,1,0:T(8,128)S(1)}, u32[]{:S(2)}, u32[]{:S(2)}) collective-permute-start(f32[1,6,128]{2,1,0:T(8,128)S(1)} %get-tuple-element.58), channel_id=1, source_target_pairs={{0,4},{4,8},{8,12},{12,16},{16,20},{20,24},{24,28},{28,32},{32,36}... | collective-permute-start | bytes 9224 | tf_op jit(solution)/shard_map/ppermute | solution.py:22
  43.6 8.2 %collective-permute-start.1 = (f32[1,6,128]{2,1,0:T(8,128)S(1)}, f32[1,6,128]{2,1,0:T(8,128)S(1)}, u32[]{:S(2)}, u32[]{:S(2)}) collective-permute-start(f32[1,6,128]{2,1,0:T(8,128)S(1)} %get-tuple-element.59), channel_id=1, source_target_pairs={{4,0},{8,4},{12,8},{16,12},{20,16},{24,20},{28,24},{32,28},{36,32}... | collective-permute-start | bytes 9224 | tf_op jit(solution)/shard_map/ppermute | solution.py:24
  56.6 12.4 %collective-permute-start.7 = (f32[99,28,6]{0,1,2:T(8,128)S(1)}, f32[99,28,6]{0,1,2:T(8,128)S(1)}, u32[]{:S(2)}, u32[]{:S(2)}) collective-permute-start(f32[99,28,6]{0,1,2:T(8,128)S(1)} %copy.13), channel_id=1, source_target_pairs={{1,0},{2,1},{3,2},{5,4},{6,5},{7,6},{9,8},{10,9},{11,10},{13,12},{... | collective-permute-start | bytes 199592 | tf_op jit(solution)/shard_map/ppermute | solution.py:24
  57.9 9.6 %collective-permute-start.6 = (f32[99,28,6]{0,1,2:T(8,128)S(1)}, f32[99,28,6]{0,1,2:T(8,128)S(1)}, u32[]{:S(2)}, u32[]{:S(2)}) collective-permute-start(f32[99,28,6]{0,1,2:T(8,128)S(1)} %copy-done.14), channel_id=1, source_target_pairs={{0,1},{1,2},{2,3},{4,5},{5,6},{6,7},{8,9},{9,10},{10,11},{12,13},{... | collective-permute-start | bytes 199592 | tf_op jit(solution)/shard_map/ppermute | solution.py:22
  62.9 11.1 %collective-permute-start.2 = (f32[1,28,6]{2,1,0:T(8,128)}, f32[1,28,6]{2,1,0:T(8,128)S(1)}, u32[]{:S(2)}, u32[]{:S(2)}) collective-permute-start(f32[1,28,6]{2,1,0:T(8,128)} %get-tuple-element.56), channel_id=1, source_target_pairs={{0,1},{1,2},{2,3},{4,5},{5,6},{6,7},{8,9},{9,10},{10,11},{12,13},{... | collective-permute-start | bytes 2024 | tf_op jit(solution)/shard_map/ppermute | solution.py:22
  66.2 7.7 %collective-permute-start.3 = (f32[1,28,6]{2,1,0:T(8,128)}, f32[1,28,6]{2,1,0:T(8,128)}, u32[]{:S(2)}, u32[]{:S(2)}) collective-permute-start(f32[1,28,6]{2,1,0:T(8,128)} %get-tuple-element.57), channel_id=1, source_target_pairs={{1,0},{2,1},{3,2},{5,4},{6,5},{7,6},{9,8},{10,9},{11,10},{13,12},{... | collective-permute-start | bytes 2024 | tf_op jit(solution)/shard_map/ppermute | solution.py:24
  101.0 13.3 %copy-start.16 = (s32[4,64]{1,0:T(4,128)S(1)}, s32[4,64]{1,0:T(4,128)}, u32[]{:S(2)}) copy-start(s32[4,64]{1,0:T(4,128)} %copy-done.15) | copy-start | bytes 3076
  101.0 14.2 %copy-start.23 = (s32[64]{0:T(128)S(1)}, s32[64]{0:T(128)}, u32[]{:S(2)}) copy-start(s32[64]{0:T(128)} %param.16) | copy-start | bytes 772
  104.9 9.3 %all-to-all-start.1 = ((f32[4,32,128]{2,1,0:T(8,128)}), f32[4,32,128]{2,1,0:T(8,128)S(1)}, u32[]{:S(2)}, u32[]{:S(2)}) async-start(f32[4,32,128]{2,1,0:T(8,128)} %fusion.187), calls=%async_computation.1 | async-start | bytes 131072 | tf_op jit(solution)/shard_map/all_to_all | solution.py:139
  (11 other events, 30.9 us)

commit v3 on v1

--- a/solution.py
+++ b/solution.py
@@ -2,6 +2,8 @@
 import jax.numpy as jnp
 from jax import lax
 from jax.sharding import PartitionSpec as P
+from jax.experimental import pallas as pl
+from jax.experimental.pallas import tpu as pltpu
 
 PATCH_DEV = 8
 SWEEPS = 6
@@ -28,27 +30,55 @@
     return cells
 
 
+def column_kernel(moist_ref, diff_ref, rain_ref, wet_ref, ratio_ref):
+    lanes = rain_ref.shape[1]
+    depth = moist_ref.shape[1] // lanes
+    group = 8
+
+    def layer(ref, rows, k):
+        return ref[rows, k * lanes : (k + 1) * lanes]
+
+    def body(g, carry):
+        rows = pl.ds(pl.multiple_of(g * group, group), group)
+        ratio = None
+        carried = None
+        for layer_k in range(depth):
+            lower_coef = layer(diff_ref, rows, layer_k)
+            source = layer(moist_ref, rows, layer_k)
+            if layer_k == 0:
+                source = source + rain_ref[rows, :]
+                pivot = 1.0 + lower_coef
+                carried = source / pivot
+            else:
+                upper_coef = layer(diff_ref, rows, layer_k - 1)
+                pivot = 1.0 + lower_coef + upper_coef - upper_coef * ratio
+                carried = (source + upper_coef * carried) / pivot
+            ratio = lower_coef / pivot
+            ratio_ref[rows, layer_k * lanes : (layer_k + 1) * lanes] = ratio
+            wet_ref[rows, layer_k * lanes : (layer_k + 1) * lanes] = carried
+        solved = carried
+        for layer_k in range(depth - 2, -1, -1):
+            solved = layer(wet_ref, rows, layer_k) + layer(ratio_ref, rows, layer_k) * solved
+            wet_ref[rows, layer_k * lanes : (layer_k + 1) * lanes] = solved
+        return carry
+
+    lax.fori_loop(0, moist_ref.shape[0] // group, body, 0)
+
+
 def column_solve(moisture, diffusivity, rain):
-    depth = moisture.shape[1]
-    ratios = []
-    forward_vals = []
-    for layer_k in range(depth):
-        lower_coef = diffusivity[:, layer_k, :]
-        source = moisture[:, layer_k, :]
-        if layer_k == 0:
-            source = source + rain
-            pivot = 1.0 + lower_coef
-            carried = source / pivot
-        else:
-            upper_coef = diffusivity[:, layer_k - 1, :]
-            pivot = 1.0 + lower_coef + upper_coef - upper_coef * ratios[-1]
-            carried = (source + upper_coef * forward_vals[-1]) / pivot
-        ratios.append(lower_coef / pivot)
-        forward_vals.append(carried)
-    solved = [forward_vals[-1]]
-    for layer_k in range(depth - 2, -1, -1):
-        solved.append(forward_vals[layer_k] + ratios[layer_k] * solved[-1])
-    return jnp.stack(solved[::-1], axis=1)
+    blocks, depth, lanes = moisture.shape
+    flat = (blocks, depth * lanes)
+    wet = pl.pallas_call(
+        column_kernel,
+        out_shape=jax.ShapeDtypeStruct(flat, jnp.float32),
+        in_specs=[pl.BlockSpec(memory_space=pltpu.VMEM)] * 3,
+        out_specs=pl.BlockSpec(memory_space=pltpu.VMEM),
+        scratch_shapes=[pltpu.VMEM(flat, jnp.float32)],
+        cost_estimate=pl.CostEstimate(
+            flops=12 * blocks * depth * lanes, transcendentals=0, bytes_accessed=12 * blocks * depth * lanes
+        ),
+    )(moisture.reshape(flat), diffusivity.reshape(flat), rain)
+    return wet
 
 
 def lateral_core(padded_head, padded_cond):
@@ -82,7 +112,8 @@
     tile_rows = head.shape[1]
     tile_cols = head.shape[2]
     wet = column_solve(moisture, diffusivity, rain)
-    bottom = wet[:, -1, :]
+    depth = moisture.shape[1]
+    bottom = wet[:, (depth - 1) * tile_cols :]
     drain = diffusivity[:, -1, :] * bottom
     in_use = jnp.arange(block_count, dtype=jnp.int32) < counts[0]
     in_use_f = in_use.astype(jnp.float32)
@@ -140,7 +171,9 @@
     returned = lax.all_to_all(answered, "gy", split_axis=0, concat_axis=0, tiled=True)
     saturation = jnp.einsum("tcb,tcj->bj", placing, returned, precision=highest)
     new_bottom = bottom + capillary * (saturation - in_use_f[:, None] * bottom)
-    moisture_out = wet.at[:, -1, :].set(new_bottom)
+    moisture_out = jnp.concatenate(
+        [wet[:, : (depth - 1) * tile_cols], new_bottom], axis=1
+    ).reshape(moisture.shape)
     patch_hot = (patch_ids[None, :] == jnp.arange(PATCH_DEV, dtype=jnp.int32)[:, None]).astype(
         jnp.float32
     )

time: 98.9 us -> 100 us (1.011)
  blocking collectives: 0 us -> 8.38 us
  other arithmetic: 40.5 us -> 32.2 us
  Pallas kernels: 0 us -> 3.95 us
  starting transfers between devices: 19.8 us -> 16.4 us
  local copies, waits for them, and re-layouts: 16.5 us -> 18.4 us
  waiting for transfers between devices: 16.5 us -> 15.1 us
    all_to_all x0 -> x1, blocking collectives: none -> 8.38 us  [local(): lax.all_to_all(packed, 'gy', split_axis=0, concat_axis=0, tiled=True)]
    unnamed x10 -> x1, other arithmetic: 7.21 us -> 0.91 us
    unnamed x37 -> x36, local copies, waits for them, and re-layouts: 7.12 us -> 1.44 us
    all_to_all x1 -> x0, starting transfers between devices: 4.01 us -> none  [local(): lax.all_to_all(packed, 'gy', split_axis=0, concat_axis=0, tiled=True)]
    pallas_call x0 -> x1, Pallas kernels: none -> 3.95 us  [column_solve(): pl.pallas_call(column_kernel, out_shape=jax.ShapeDtypeStruct(flat, jnp.fl...]
    ppermute x2, waiting for transfers between devices: 9.74 us -> 7.72 us  [with_halo(): lax.ppermute(head, axis, [((i + 1) % count, i) for i in range(ends)])]
    ppermute x1, local copies, waits for them, and re-layouts: 1.53 us -> 3.36 us  [with_halo(): lax.ppermute(head, axis, [((i + 1) % count, i) for i in range(ends)])]
    slice x5, local copies, waits for them, and re-layouts: 0.4 us -> 2.18 us  [local(): field = jnp.where(inside[None, edge:-edge, edge:-edge], field, 0.0)]
  transfers between devices with their start and end apart: 6 -> 5, of which waited for: 4 -> 3; matrix products, arithmetic and copies ran while one was open for 15% -> 6% of each run, Pallas kernels for 0% -> 0%
where the time goes in v3:
time: 100 us; the launch traced here: 99.5 us
  other arithmetic  32.2 us (32%)
  local copies, waits for them, and re-layouts  18.4 us (18%)
  starting transfers between devices  16.4 us (16%)
  waiting for transfers between devices  15.1 us (15%)
  blocking collectives  8.38 us (8%)
  Pallas kernels  3.95 us (4%)
  matrix products  3.31 us (3%)
  between operations  1.79 us (2%)
    select_n x5, other arithmetic, local(): field = jnp.where(inside[None, edge:-edge, edge:-edge], field, 0.0)  16.8 us
    ppermute x2, starting transfers between devices, with_halo(): lax.ppermute(tail, axis, [(i, (i + 1) % count) for i in range(ends)])  9.23 us
    all_to_all x1, blocking collectives, local(): lax.all_to_all(packed, 'gy', split_axis=0, concat_axis=0, tiled=True)  8.38 us
    ppermute x2, waiting for transfers between devices, with_halo(): lax.ppermute(head, axis, [((i + 1) % count, i) for i in range(ends)])  7.72 us
    mul x6, other arithmetic, lateral_core(): 0.5 * (centre_cond[1:] + centre_cond[:-1]) * (centre[1:] - centre[:-1])  7.31 us
    slice x2, local copies, waits for them, and re-layouts, with_halo(): lax.slice_in_dim(cells, cells.shape[dim] - width, cells.shape[dim], axis=...  5.32 us
    all_to_all x1, waiting for transfers between devices, local(): lax.all_to_all(answered, 'gy', split_axis=0, concat_axis=0, tiled=True)  4.47 us
    all_to_all x1, starting transfers between devices, local(): lax.all_to_all(answered, 'gy', split_axis=0, concat_axis=0, tiled=True)  3.95 us
  transfers between devices with their start and end apart: 5, of which 3 were waited for; matrix products, arithmetic and copies ran while one was open for 6% of the time, Pallas kernels for 0%

profile of v3, /device:TPU:249, one launch (start us, length us, event | category | flops | bytes accessed | tf_op | source)
XLA Modules:
  0.0 99.5 jit_solution(11544903279586489023)
XLA Ops:
  5.0 4.0 %shard_map.112 = f32[64,2560]{1,0:T(8,128)} custom-call(f32[64,2560]{1,0:T(8,128)} %get-tuple-element.33.moist_ref, f32[64,2560]{1,0:T(8,128)} %get-tuple-element.32.diff_ref, f32[64,128]{1,0:T(8,128)} %rain_ref.1), custom_call_target="tpu_custom_call" | custom-call | flops 1966080 | bytes 1966080 | tf_op jit(solution)/shard_map/pallas_call | solution.py:71
  10.4 8.4 %all_to_all.10 = f32[4,33,128]{2,1,0:T(8,128)S(1)} all-to-all(f32[4,33,128]{2,1,0:T(8,128)S(1)} %pad_maximum_fusion.15), channel_id=1, replica_groups=mesh['gx'=192,'gy'=4] {'gy'}, dimensions={0} | all-to-all | bytes 135168 | tf_op jit(solution)/shard_map/all_to_all | solution.py:134
  19.6 6.4 %collective-permute-start = (f32[100,6,128]{2,1,0:T(8,128)S(1)}, f32[100,6,128]{2,1,0:T(8,128)S(1)}, u32[]{:S(2)}, u32[]{:S(2)}) collective-permute-start(f32[100,6,128]{2,1,0:T(8,128)S(1)} %get-tuple-element.26), channel_id=1, source_target_pairs={{0,4},{4,8},{8,12},{12,16},{16,20},{20,24},{24,28},{28,32},{32,36}... | collective-permute-start | bytes 921608 | tf_op jit(solution)/shard_map/ppermute | solution.py:24
  26.1 1.9 %collective-permute-start.1 = (f32[100,6,128]{2,1,0:T(8,128)S(1)}, f32[100,6,128]{2,1,0:T(8,128)S(1)}, u32[]{:S(2)}, u32[]{:S(2)}) collective-permute-start(f32[100,6,128]{2,1,0:T(8,128)S(1)} %get-tuple-element.27), channel_id=1, source_target_pairs={{4,0},{8,4},{12,8},{16,12},{20,16},{24,20},{28,24},{32,28},{36,32}... | collective-permute-start | bytes 921608 | tf_op jit(solution)/shard_map/ppermute | solution.py:26
  28.0 2.9 %collective-permute-done = f32[100,6,128]{2,1,0:T(8,128)S(1)} collective-permute-done((f32[100,6,128]{2,1,0:T(8,128)S(1)}, f32[100,6,128]{2,1,0:T(8,128)S(1)}, u32[]{:S(2)}, u32[]{:S(2)}) %collective-permute-start) | collective-permute-done | bytes 307232 | tf_op jit(solution)/shard_map/ppermute | solution.py:24
  30.9 7.7 %collective-permute-done.1 = f32[100,6,128]{2,1,0:T(8,128)S(1)} collective-permute-done((f32[100,6,128]{2,1,0:T(8,128)S(1)}, f32[100,6,128]{2,1,0:T(8,128)S(1)}, u32[]{:S(2)}, u32[]{:S(2)}) %collective-permute-start.1) | collective-permute-done | bytes 307232 | tf_op jit(solution)/shard_map/ppermute | solution.py:26
  39.4 2.3 %fusion.150 = (f32[100,28,6]{2,1,0:T(8,128)}, f32[100,28,6]{2,1,0:T(8,128)}) fusion(f32[100,28,128]{2,1,0:T(8,128)S(1)} %pad_maximum_fusion.1), kind=kLoop, calls=%fused_computation.244 | loop fusion | bytes 268800 | tf_op jit(solution)/shard_map/slice | solution.py:21
  41.7 3.1 %copy.20 = f32[100,28,6]{0,1,2:T(8,128)} copy(f32[100,28,6]{2,1,0:T(8,128)} %get-tuple-element.24) | data formatting | bytes 134400 | tf_op jit(solution)/shard_map/slice | solution.py:21
  44.7 2.8 %collective-permute-start.2 = (f32[100,28,6]{0,1,2:T(8,128)}, f32[100,28,6]{0,1,2:T(8,128)}, u32[]{:S(2)}, u32[]{:S(2)}) collective-permute-start(f32[100,28,6]{0,1,2:T(8,128)} %copy.20), channel_id=1, source_target_pairs={{0,1},{1,2},{2,3},{4,5},{5,6},{6,7},{8,9},{9,10},{10,11},{12,13},{... | collective-permute-start | bytes 201608 | tf_op jit(solution)/shard_map/ppermute | solution.py:24
  47.5 1.7 %copy.21 = f32[100,28,6]{0,1,2:T(8,128)} copy(f32[100,28,6]{2,1,0:T(8,128)S(1)} %copy-done.6) | data formatting | bytes 134400 | tf_op jit(solution)/shard_map/slice | solution.py:20
  52.8 2.4 %copy.22 = f32[100,28,6]{2,1,0:T(8,128)S(1)} copy(f32[100,28,6]{0,1,2:T(8,128)} %collective-permute-done.2) | data formatting | bytes 134400 | tf_op jit(solution)/shard_map/ppermute | solution.py:24
  55.3 3.4 %copy.23 = f32[100,28,6]{2,1,0:T(8,128)} copy(f32[100,28,6]{0,1,2:T(8,128)} %collective-permute-done.3) | data formatting | bytes 134400 | tf_op jit(solution)/shard_map/ppermute | solution.py:26
  58.6 3.3 %pad_maximum_fusion = f32[100,28,140]{2,1,0:T(8,128)S(1)} fusion(f32[100,28,6]{2,1,0:T(8,128)} %copy.23, f32[100,6,128]{2,1,0:T(8,128)} %copy-done.4, f32[50,16,128]{2,1,0:T(8,128)S(1)} %copy-done.2, f32[50,16,128]{2,1,0:T(8,128)S(1)} %fusion.91, f32[100,6,128]{2,1,0:T(8,128)S(1)} %collective-permute-done, f32[100,28,6]{2,1,0:T(8,128)S(1)} %copy.22), kind=kLoop, calls=%fused_computation | loop fusion | flops 1960000 | bytes 3136000 | tf_op jit(solution)/shard_map/concatenate | solution.py:22
  61.9 1.8 %fusion.16 = f32[49,26,138]{2,1,0:T(8,128)S(1)} fusion(f32[100,28,140]{2,1,0:T(8,128)S(1)} %pad_maximum_fusion), kind=kLoop, calls=%fused_computation.27 | loop fusion | flops 703248 | bytes 3516240 | tf_op jit(solution)/shard_map/mul | solution.py:98
  63.7 3.8 %fusion.6 = f32[50,26,138]{2,1,0:T(8,128)S(1)} fusion(f32[100,28,140]{2,1,0:T(8,128)S(1)} %pad_maximum_fusion, f32[49,26,138]{2,1,0:T(8,128)S(1)} %fusion.16, pred[26,138]{1,0:T(8,128)(4,1)S(1)} %slice.494), kind=kLoop, calls=%fused_computation.8 | loop fusion | flops 4305600 | bytes 8600436 | tf_op jit(solution)/shard_map/jit(_where)/select_n | solution.py:166
  67.5 1.3 %fusion.88 = f32[49,24,136]{2,1,0:T(8,128)S(1)} fusion(f32[50,26,138]{2,1,0:T(8,128)S(1)} %fusion.6, f32[100,28,140]{2,1,0:T(8,128)S(1)} %pad_maximum_fusion), kind=kLoop, calls=%fused_computation.139 | loop fusion | flops 639744 | bytes 3198720 | tf_op jit(solution)/shard_map/mul | solution.py:98
  68.8 3.1 %fusion.72 = f32[50,24,136]{2,1,0:T(8,128)S(1)} fusion(f32[50,26,138]{2,1,0:T(8,128)S(1)} %fusion.6, f32[100,28,140]{2,1,0:T(8,128)S(1)} %pad_maximum_fusion, f32[49,24,136]{2,1,0:T(8,128)S(1)} %fusion.88, pred[24,136]{1,0:T(8,128)(4,1)S(1)} %copy-done.12), kind=kLoop, calls=%fused_computation.109 | loop fusion | flops 3916800 | bytes 7823808 | tf_op jit(solution)/shard_map/jit(_where)/select_n | solution.py:166
  73.2 3.1 %fusion.56 = f32[50,22,134]{2,1,0:T(8,128)S(1)} fusion(f32[50,24,136]{2,1,0:T(8,128)S(1)} %fusion.72, f32[100,28,140]{2,1,0:T(8,128)S(1)} %pad_maximum_fusion, f32[49,22,134]{2,1,0:T(8,128)S(1)} %fusion.86, pred[22,134]{1,0:T(8,128)(4,1)S(1)} %copy-done.11), kind=kLoop, calls=%fused_computation.85 | loop fusion | flops 3537600 | bytes 7066356 | tf_op jit(solution)/shard_map/jit(_where)/select_n | solution.py:166
  76.3 1.3 %fusion.84 = f32[49,20,132]{2,1,0:T(8,128)S(1)} fusion(f32[50,22,134]{2,1,0:T(8,128)S(1)} %fusion.56, f32[100,28,140]{2,1,0:T(8,128)S(1)} %pad_maximum_fusion), kind=kLoop, calls=%fused_computation.131 | loop fusion | flops 517440 | bytes 2587200 | tf_op jit(solution)/shard_map/mul | solution.py:98
  77.7 3.1 %fusion.40 = f32[50,20,132]{2,1,0:T(8,128)S(1)} fusion(f32[50,22,134]{2,1,0:T(8,128)S(1)} %fusion.56, f32[100,28,140]{2,1,0:T(8,128)S(1)} %pad_maximum_fusion, f32[49,20,132]{2,1,0:T(8,128)S(1)} %fusion.84, pred[20,132]{1,0:T(8,128)(4,1)S(1)} %copy-done.10), kind=kLoop, calls=%fused_computation.61 | loop fusion | flops 3168000 | bytes 6328080 | tf_op jit(solution)/shard_map/jit(_where)/select_n | solution.py:166
  80.8 1.3 %fusion.82 = f32[49,18,130]{2,1,0:T(8,128)S(1)} fusion(f32[50,20,132]{2,1,0:T(8,128)S(1)} %fusion.40, f32[100,28,140]{2,1,0:T(8,128)S(1)} %pad_maximum_fusion), kind=kLoop, calls=%fused_computation.127 | loop fusion | flops 458640 | bytes 2293200 | tf_op jit(solution)/shard_map/mul | solution.py:98
  82.3 3.8 %fusion.24 = f32[50,18,130]{2,1,0:T(8,128)S(1)} fusion(f32[50,20,132]{2,1,0:T(8,128)S(1)} %fusion.40, f32[100,28,6]{2,1,0:T(8,128)S(1)} %copy-done.1, f32[100,6,128]{2,1,0:T(8,128)S(1)} %copy-done.5, f32[100,6,128]{2,1,0:T(8,128)S(1)} %collective-permute-done, f32[50,16,128]{2,1,0:T(8,128)S(1)} %copy-done.2, f32[50,16,128]{2,1,0:T(8,128)S(1)} %fusion.91, ...), kind=kLoop, calls=%fused_computation.37 | loop fusion | flops 3744000 | bytes 6240980 | tf_op jit(solution)/shard_map/jit(_where)/select_n | solution.py:166
  89.1 4.0 %all-to-all-start.1 = ((f32[4,32,128]{2,1,0:T(8,128)}), f32[4,32,128]{2,1,0:T(8,128)S(1)}, u32[]{:S(2)}, u32[]{:S(2)}) async-start(f32[4,32,128]{2,1,0:T(8,128)} %fusion.132), calls=%async_computation.1 | async-start | bytes 131072 | tf_op jit(solution)/shard_map/all_to_all | solution.py:171
  93.0 4.5 %all-to-all-done.1 = f32[4,32,128]{2,1,0:T(8,128)S(1)} async-done(((f32[4,32,128]{2,1,0:T(8,128)}), f32[4,32,128]{2,1,0:T(8,128)S(1)}, u32[]{:S(2)}, u32[]{:S(2)}) %all-to-all-start.1) | async-done | bytes 65568 | tf_op jit(solution)/shard_map/all_to_all | solution.py:171
  (75 shorter events, 16.5 us)
Async XLA Ops:
  0.6 3.1 %copy-start = (f32[64,20,128]{2,0,1:T(8,128)S(1)}, f32[64,20,128]{2,0,1:T(8,128)}, u32[]{:S(2)}) copy-start(f32[64,20,128]{2,0,1:T(8,128)} %param.11) | copy-start | bytes 1966084
  0.6 3.1 %copy-start.8 = (f32[64,20,128]{2,0,1:T(8,128)S(1)}, f32[64,20,128]{2,0,1:T(8,128)}, u32[]{:S(2)}) copy-start(f32[64,20,128]{2,0,1:T(8,128)} %param.12) | copy-start | bytes 1966084
  2.8 7.1 %copy-start.13 = (s32[4,64]{1,0:T(4,128)}, s32[4,64]{1,0:T(4,128)S(1)}, u32[]{:S(2)}) copy-start(s32[4,64]{1,0:T(4,128)S(1)} %fusion.141) | copy-start | bytes 3076
  5.0 4.9 %copy-start.17 = (s32[64]{0:T(128)S(1)}, s32[64]{0:T(128)}, u32[]{:S(2)}) copy-start(s32[64]{0:T(128)} %param.17) | copy-start | bytes 772
  5.0 14.4 %copy-start.3 = (f32[50,16,128]{2,1,0:T(8,128)S(1)}, f32[50,16,128]{2,1,0:T(8,128)}, u32[]{:S(2)}) copy-start(f32[50,16,128]{2,1,0:T(8,128)} %param.14) | copy-start | bytes 1228804
  5.0 14.5 %copy-start.2 = (f32[50,16,128]{2,1,0:T(8,128)S(1)}, f32[50,16,128]{2,1,0:T(8,128)}, u32[]{:S(2)}) copy-start(f32[50,16,128]{2,1,0:T(8,128)} %param.15) | copy-start | bytes 1228804
  19.6 11.3 %collective-permute-start = (f32[100,6,128]{2,1,0:T(8,128)S(1)}, f32[100,6,128]{2,1,0:T(8,128)S(1)}, u32[]{:S(2)}, u32[]{:S(2)}) collective-permute-start(f32[100,6,128]{2,1,0:T(8,128)S(1)} %get-tuple-element.26), channel_id=1, source_target_pairs={{0,4},{4,8},{8,12},{12,16},{16,20},{20,24},{24,28},{28,32},{32,36}... | collective-permute-start | bytes 921608 | tf_op jit(solution)/shard_map/ppermute | solution.py:24
  26.1 12.6 %collective-permute-start.1 = (f32[100,6,128]{2,1,0:T(8,128)S(1)}, f32[100,6,128]{2,1,0:T(8,128)S(1)}, u32[]{:S(2)}, u32[]{:S(2)}) collective-permute-start(f32[100,6,128]{2,1,0:T(8,128)S(1)} %get-tuple-element.27), channel_id=1, source_target_pairs={{4,0},{8,4},{12,8},{16,12},{20,16},{24,20},{28,24},{32,28},{36,32}... | collective-permute-start | bytes 921608 | tf_op jit(solution)/shard_map/ppermute | solution.py:26
  38.6 0.8 copy-start.4
  41.7 5.9 %copy-start.6 = (f32[100,28,6]{2,1,0:T(8,128)S(1)}, f32[100,28,6]{2,1,0:T(8,128)}, u32[]{:S(2)}) copy-start(f32[100,28,6]{2,1,0:T(8,128)} %get-tuple-element.25) | copy-start | bytes 201604
  44.7 8.1 %collective-permute-start.2 = (f32[100,28,6]{0,1,2:T(8,128)}, f32[100,28,6]{0,1,2:T(8,128)}, u32[]{:S(2)}, u32[]{:S(2)}) collective-permute-start(f32[100,28,6]{0,1,2:T(8,128)} %copy.20), channel_id=1, source_target_pairs={{0,1},{1,2},{2,3},{4,5},{5,6},{6,7},{8,9},{9,10},{10,11},{12,13},{... | collective-permute-start | bytes 201608 | tf_op jit(solution)/shard_map/ppermute | solution.py:24
  49.3 6.0 %collective-permute-start.3 = (f32[100,28,6]{0,1,2:T(8,128)}, f32[100,28,6]{0,1,2:T(8,128)}, u32[]{:S(2)}, u32[]{:S(2)}) collective-permute-start(f32[100,28,6]{0,1,2:T(8,128)} %copy.21), channel_id=1, source_target_pairs={{1,0},{2,1},{3,2},{5,4},{6,5},{7,6},{9,8},{10,9},{11,10},{13,12},{... | collective-permute-start | bytes 201608 | tf_op jit(solution)/shard_map/ppermute | solution.py:26
  67.5 1.3 %copy-start.12 = (pred[24,136]{1,0:T(8,128)(4,1)S(1)}, pred[24,136]{1,0:T(8,128)(4,1)}, u32[]{:S(2)}) copy-start(pred[24,136]{1,0:T(8,128)(4,1)} %slice.493) | copy-start | bytes 9796
  71.9 1.3 %copy-start.11 = (pred[22,134]{1,0:T(8,128)(4,1)S(1)}, pred[22,134]{1,0:T(8,128)(4,1)}, u32[]{:S(2)}) copy-start(pred[22,134]{1,0:T(8,128)(4,1)} %slice.492) | copy-start | bytes 8848
  76.3 1.3 %copy-start.10 = (pred[20,132]{1,0:T(8,128)(4,1)S(1)}, pred[20,132]{1,0:T(8,128)(4,1)}, u32[]{:S(2)}) copy-start(pred[20,132]{1,0:T(8,128)(4,1)} %slice.491) | copy-start | bytes 7924
  80.8 1.4 %copy-start.1 = (f32[100,28,6]{2,1,0:T(8,128)S(1)}, f32[100,28,6]{2,1,0:T(8,128)}, u32[]{:S(2)}) copy-start(f32[100,28,6]{2,1,0:T(8,128)} %copy.23) | copy-start | bytes 201604
  80.8 1.5 %copy-start.5 = (f32[100,6,128]{2,1,0:T(8,128)S(1)}, f32[100,6,128]{2,1,0:T(8,128)}, u32[]{:S(2)}) copy-start(f32[100,6,128]{2,1,0:T(8,128)} %copy-done.4) | copy-start | bytes 921604
  86.4 1.8 %copy-start.15 = (f32[4,1,32]{2,1,0:T(1,128)S(1)}, f32[4,1,32]{2,1,0:T(1,128)}, u32[]{:S(2)}) copy-start(f32[4,1,32]{2,1,0:T(1,128)} %get-tuple-element.28) | copy-start | bytes 1540
  87.4 0.8 copy-start.9
  87.5 10.1 %copy-start.7 = (f32[64,2560]{1,0:T(8,128)S(1)}, f32[64,2560]{1,0:T(8,128)}, u32[]{:S(2)}) copy-start(f32[64,2560]{1,0:T(8,128)} %shard_map.112) | copy-start | bytes 1966084
  87.5 10.1 %copy-start.14 = (s32[4,64]{1,0:T(4,128)S(1)}, s32[4,64]{1,0:T(4,128)}, u32[]{:S(2)}) copy-start(s32[4,64]{1,0:T(4,128)} %copy-done.13) | copy-start | bytes 3076
  87.5 10.3 %slice-start = ((f32[64,2560]{1,0:T(8,128)}), f32[64,2432]{1,0:T(8,128)S(1)}, s32[]{:S(2)}) async-start(f32[64,2560]{1,0:T(8,128)} %shard_map.112), calls=%async_computation.2 | async-start | bytes 1245184 | tf_op jit(solution)/shard_map/slice | solution.py:175
  89.1 8.4 %all-to-all-start.1 = ((f32[4,32,128]{2,1,0:T(8,128)}), f32[4,32,128]{2,1,0:T(8,128)S(1)}, u32[]{:S(2)}, u32[]{:S(2)}) async-start(f32[4,32,128]{2,1,0:T(8,128)} %fusion.132), calls=%async_computation.1 | async-start | bytes 131072 | tf_op jit(solution)/shard_map/all_to_all | solution.py:171
  93.0 5.7 %copy-start.16 = (s32[64]{0:T(128)S(1)}, s32[64]{0:T(128)}, u32[]{:S(2)}) copy-start(s32[64]{0:T(128)} %param.18) | copy-start | bytes 772

commit v4 on v3

--- a/solution.py
+++ b/solution.py
@@ -104,6 +104,87 @@
     return centre + flow_rate * flux_total
 
 
+def turn(x, shift, axis):
+    return pltpu.roll(x, shift % x.shape[axis], axis)
+
+
+def sweep_kernel(both_ref, mask_ref, out_ref, first_ref, second_ref, cond_ref):
+    layers = both_ref.shape[0] // 2
+    out_rows, out_cols = out_ref.shape[1], out_ref.shape[2]
+    keep = mask_ref[...] > 0.5
+
+    def conductances(layer_k, carry):
+        here = both_ref[layers + layer_k]
+        below = both_ref[layers + jnp.minimum(layer_k + 1, layers - 1)]
+        cond_ref[0, layer_k] = 0.5 * (here + turn(here, 1, 0))
+        cond_ref[1, layer_k] = 0.5 * (here + turn(here, -1, 0))
+        cond_ref[2, layer_k] = 0.5 * (here + turn(here, 1, 1))
+        cond_ref[3, layer_k] = 0.5 * (here + turn(here, -1, 1))
+        cond_ref[4, layer_k] = 0.5 * (below + here)
+        return carry
+
+    lax.fori_loop(0, layers, conductances, 0)
+
+    def sweep(read, write, last):
+        def body(layer_k, carry):
+            centre, upward = carry
+            below = read(jnp.minimum(layer_k + 1, layers - 1))
+            flux = cond_ref[0, layer_k] * (turn(centre, 1, 0) - centre)
+            flux = flux + cond_ref[1, layer_k] * (turn(centre, -1, 0) - centre)
+            flux = flux + cond_ref[2, layer_k] * (turn(centre, 1, 1) - centre)
+            flux = flux + cond_ref[3, layer_k] * (turn(centre, -1, 1) - centre)
+            downward = jnp.where(
+                layer_k < layers - 1, cond_ref[4, layer_k] * (below - centre), 0.0
+            )
+            flux = flux + downward
+            flux = flux - upward
+            fresh = centre + flow_rate * flux
+            if last:
+                moved = turn(turn(fresh, -SWEEPS, 0), -SWEEPS, 1)
+                out_ref[layer_k] = moved[:out_rows, :out_cols]
+            else:
+                write(layer_k, jnp.where(keep, fresh, 0.0))
+            return (below, downward)
+
+        start = (read(0), jnp.zeros(mask_ref.shape, jnp.float32))
+        lax.fori_loop(0, layers, body, start)
+
+    def reader(ref):
+        return lambda layer_k: ref[layer_k]
+
+    def writer(ref):
+        def write(layer_k, value):
+            ref[layer_k] = value
+
+        return write
+
+    sweep(reader(both_ref), writer(first_ref), False)
+    for sweep_k in range(1, SWEEPS):
+        source, target = (first_ref, second_ref) if sweep_k % 2 else (second_ref, first_ref)
+        sweep(reader(source), writer(target), sweep_k == SWEEPS - 1)
+
+
+def sweeps(both, mask, tile_shape):
+    layers, rows, cols = both.shape[0] // 2, both.shape[1], both.shape[2]
+    return pl.pallas_call(
+        sweep_kernel,
+        out_shape=jax.ShapeDtypeStruct(tile_shape, jnp.float32),
+        in_specs=[pl.BlockSpec(memory_space=pltpu.VMEM)] * 2,
+        out_specs=pl.BlockSpec(memory_space=pltpu.VMEM),
+        scratch_shapes=[
+            pltpu.VMEM((layers, rows, cols), jnp.float32),
+            pltpu.VMEM((layers, rows, cols), jnp.float32),
+            pltpu.VMEM((5, layers, rows, cols), jnp.float32),
+        ],
+        compiler_params=pltpu.CompilerParams(vmem_limit_bytes=48 * 1024 * 1024),
+        cost_estimate=pl.CostEstimate(
+            flops=20 * SWEEPS * layers * rows * cols,
+            transcendentals=0,
+            bytes_accessed=4 * (2 * layers * rows * cols + layers * tile_shape[1] * tile_shape[2]),
+        ),
+    )(both, mask)
+
+
 def local(moisture, diffusivity, rain, head, conductivity, tile_ids, offsets, patch_ids, counts):
     highest = lax.Precision.HIGHEST
     block_count = moisture.shape[0]
@@ -144,8 +225,6 @@
     both = with_halo(
         jnp.concatenate([field, conductivity], axis=0), (("gx", 1), ("gy", 2)), SWEEPS
     )
-    field = both[:layers]
-    padded_cond = both[layers:]
     row_at = (
         lax.axis_index("gx") * tile_rows - SWEEPS + jnp.arange(tile_rows + 2 * SWEEPS)
     )[:, None]
@@ -158,12 +237,11 @@
         & (col_at >= 0)
         & (col_at < tile_cols * tile_count)
     )
-    for sweep_k in range(SWEEPS):
-        field = lateral_core(field, padded_cond)
-        padded_cond = padded_cond[:, 1:-1, 1:-1]
-        if sweep_k < SWEEPS - 1:
-            edge = sweep_k + 1
-            field = jnp.where(inside[None, edge:-edge, edge:-edge], field, 0.0)
+    rows_up = -(-(tile_rows + 2 * SWEEPS) // 8) * 8 - (tile_rows + 2 * SWEEPS)
+    cols_up = -(-(tile_cols + 2 * SWEEPS) // 128) * 128 - (tile_cols + 2 * SWEEPS)
+    mask = jnp.pad(inside.astype(jnp.float32), ((0, rows_up), (0, cols_up)))
+    both = jnp.pad(both, ((0, 0), (0, rows_up), (0, cols_up)))
+    field = sweeps(both, mask, head.shape)
     surface = field[0]
     answered = jnp.dot(landing.T, surface, precision=highest).reshape(
         tile_count, capacity, tile_cols

time: 100 us -> 112 us (1.12)
  Pallas kernels: 3.95 us -> 40.2 us
  other arithmetic: 32.2 us -> 9.78 us
  blocking collectives: 8.38 us -> 0 us
  waiting for transfers between devices: 15.1 us -> 20.2 us
  starting transfers between devices: 16.4 us -> 19.7 us
  local copies, waits for them, and re-layouts: 18.4 us -> 16 us
    pallas_call x0 -> x1, Pallas kernels: none -> 36.3 us  [sweeps(): pl.pallas_call(sweep_kernel, out_shape=jax.ShapeDtypeStruct(tile_shape, j...]
    select_n x5 -> x0, other arithmetic: 16.8 us -> none  [local(): field = jnp.where(inside[None, edge:-edge, edge:-edge], field, 0.0)]
    all_to_all x1 -> x0, blocking collectives: 8.38 us -> none  [local(): lax.all_to_all(packed, 'gy', split_axis=0, concat_axis=0, tiled=True)]
    mul x6 -> x0, other arithmetic: 7.31 us -> none  [lateral_core(): 0.5 * (centre_cond[1:] + centre_cond[:-1]) * (centre[1:] - centre[:-1])]
    all_to_all x0 -> x1, waiting for transfers between devices: none -> 4.56 us  [local(): lax.all_to_all(packed, 'gy', split_axis=0, concat_axis=0, tiled=True)]
    all_to_all x0 -> x1, starting transfers between devices: none -> 4.01 us  [local(): lax.all_to_all(packed, 'gy', split_axis=0, concat_axis=0, tiled=True)]
    slice x5 -> x0, local copies, waits for them, and re-layouts: 2.18 us -> none  [local(): field = jnp.where(inside[None, edge:-edge, edge:-edge], field, 0.0)]
    ppermute x2, waiting for transfers between devices: 7.72 us -> 8.96 us  [with_halo(): lax.ppermute(head, axis, [((i + 1) % count, i) for i in range(ends)])]
  transfers between devices with their start and end apart: 5 -> 6, of which waited for: 3 -> 5; matrix products, arithmetic and copies ran while one was open for 6% -> 5% of each run, Pallas kernels for 0% -> 0%
where the time goes in v4:
time: 112 us
  Pallas kernels  40.2 us (36%)
  waiting for transfers between devices  20.2 us (18%)
  starting transfers between devices  19.7 us (18%)
  local copies, waits for them, and re-layouts  16 us (14%)
  other arithmetic  9.78 us (9%)
  matrix products  4.03 us (4%)
  between operations  1.67 us (1%)
    pallas_call x1, Pallas kernels, sweeps(): pl.pallas_call(sweep_kernel, out_shape=jax.ShapeDtypeStruct(tile_shape, j...  36.3 us
    ppermute x2, starting transfers between devices, with_halo(): lax.ppermute(tail, axis, [(i, (i + 1) % count) for i in range(ends)])  9.22 us
    ppermute x2, waiting for transfers between devices, with_halo(): lax.ppermute(head, axis, [((i + 1) % count, i) for i in range(ends)])  8.96 us
    slice x2, local copies, waits for them, and re-layouts, with_halo(): lax.slice_in_dim(cells, cells.shape[dim] - width, cells.shape[dim], axis=...  4.72 us
    all_to_all x1, waiting for transfers between devices, local(): lax.all_to_all(packed, 'gy', split_axis=0, concat_axis=0, tiled=True)  4.56 us
    all_to_all x1, waiting for transfers between devices, local(): lax.all_to_all(answered, 'gy', split_axis=0, concat_axis=0, tiled=True)  4.43 us
    concatenate x2, other arithmetic, with_halo(): jnp.concatenate([lax.ppermute(tail, axis, [(i, (i + 1) % count) for i in...  4.41 us
    all_to_all x1, starting transfers between devices, local(): lax.all_to_all(packed, 'gy', split_axis=0, concat_axis=0, tiled=True)  4.01 us
  transfers between devices with their start and end apart: 6, of which 5 were waited for; matrix products, arithmetic and copies ran while one was open for 5% of the time, Pallas kernels for 0%

profile of v4, /device:TPU:249, one launch (start us, length us, event | category | flops | bytes accessed | tf_op | source)
XLA Modules:
  0.0 111.6 jit_solution(7092335928933607624)
XLA Ops:
  3.0 0.8 select_reduce_fusion
  3.8 2.3 %copy_bitcast_fusion = (f32[64,2560]{1,0:T(8,128)}, f32[64,2560]{1,0:T(8,128)}) fusion(f32[64,20,128]{2,0,1:T(8,128)S(1)} %copy-done, f32[64,20,128]{2,0,1:T(8,128)} %param.12), kind=kLoop, calls=%fused_computation.23 | loop fusion | bytes 2621440 | tf_op jit(solution)/shard_map/reshape | solution.py:80
  6.1 3.9 %shard_map.112 = f32[64,2560]{1,0:T(8,128)} custom-call(f32[64,2560]{1,0:T(8,128)} %get-tuple-element.33.moist_ref, f32[64,2560]{1,0:T(8,128)} %get-tuple-element.32.diff_ref, f32[64,128]{1,0:T(8,128)} %rain_ref.1), custom_call_target="tpu_custom_call" | custom-call | flops 1966080 | bytes 1966080 | tf_op jit(solution)/shard_map/pallas_call | solution.py:71
  10.0 1.0 fusion.18
  12.0 4.0 %all-to-all-start = ((f32[4,33,128]{2,1,0:T(8,128)}), f32[4,33,128]{2,1,0:T(8,128)S(1)}, u32[]{:S(2)}, u32[]{:S(2)}) async-start(f32[4,33,128]{2,1,0:T(8,128)} %pad_maximum_fusion.2), calls=%async_computation | async-start | bytes 163840 | tf_op jit(solution)/shard_map/all_to_all | solution.py:215
  16.1 4.6 %all-to-all-done = f32[4,33,128]{2,1,0:T(8,128)S(1)} async-done(((f32[4,33,128]{2,1,0:T(8,128)}), f32[4,33,128]{2,1,0:T(8,128)S(1)}, u32[]{:S(2)}, u32[]{:S(2)}) %all-to-all-start) | async-done | bytes 67616 | tf_op jit(solution)/shard_map/all_to_all | solution.py:215
  21.5 6.4 %collective-permute-start = (f32[100,6,128]{2,1,0:T(8,128)S(1)}, f32[100,6,128]{2,1,0:T(8,128)S(1)}, u32[]{:S(2)}, u32[]{:S(2)}) collective-permute-start(f32[100,6,128]{2,1,0:T(8,128)S(1)} %get-tuple-element.26), channel_id=1, source_target_pairs={{0,4},{4,8},{8,12},{12,16},{16,20},{20,24},{24,28},{28,32},{32,36}... | collective-permute-start | bytes 921608 | tf_op jit(solution)/shard_map/ppermute | solution.py:24
  27.9 1.9 %collective-permute-start.1 = (f32[100,6,128]{2,1,0:T(8,128)S(1)}, f32[100,6,128]{2,1,0:T(8,128)S(1)}, u32[]{:S(2)}, u32[]{:S(2)}) collective-permute-start(f32[100,6,128]{2,1,0:T(8,128)S(1)} %get-tuple-element.27), channel_id=1, source_target_pairs={{4,0},{8,4},{12,8},{16,12},{20,16},{24,20},{28,24},{32,28},{36,32}... | collective-permute-start | bytes 921608 | tf_op jit(solution)/shard_map/ppermute | solution.py:26
  30.6 2.3 %collective-permute-done = f32[100,6,128]{2,1,0:T(8,128)S(1)} collective-permute-done((f32[100,6,128]{2,1,0:T(8,128)S(1)}, f32[100,6,128]{2,1,0:T(8,128)S(1)}, u32[]{:S(2)}, u32[]{:S(2)}) %collective-permute-start) | collective-permute-done | bytes 307232 | tf_op jit(solution)/shard_map/ppermute | solution.py:24
  32.8 7.7 %collective-permute-done.1 = f32[100,6,128]{2,1,0:T(8,128)S(1)} collective-permute-done((f32[100,6,128]{2,1,0:T(8,128)S(1)}, f32[100,6,128]{2,1,0:T(8,128)S(1)}, u32[]{:S(2)}, u32[]{:S(2)}) %collective-permute-start.1) | collective-permute-done | bytes 307232 | tf_op jit(solution)/shard_map/ppermute | solution.py:26
  41.5 1.8 %fusion.52 = (f32[100,28,6]{2,1,0:T(8,128)}, f32[100,28,6]{2,1,0:T(8,128)S(1)}) fusion(f32[100,28,128]{2,1,0:T(8,128)S(1)} %pad_maximum_fusion), kind=kLoop, calls=%fused_computation.83 | loop fusion | bytes 268800 | tf_op jit(solution)/shard_map/slice | solution.py:21
  43.3 3.0 %copy.20 = f32[100,28,6]{0,1,2:T(8,128)} copy(f32[100,28,6]{2,1,0:T(8,128)} %get-tuple-element.24) | data formatting | bytes 134400 | tf_op jit(solution)/shard_map/slice | solution.py:21
  46.3 2.8 %collective-permute-start.2 = (f32[100,28,6]{0,1,2:T(8,128)}, f32[100,28,6]{0,1,2:T(8,128)}, u32[]{:S(2)}, u32[]{:S(2)}) collective-permute-start(f32[100,28,6]{0,1,2:T(8,128)} %copy.20), channel_id=1, source_target_pairs={{0,1},{1,2},{2,3},{4,5},{5,6},{6,7},{8,9},{9,10},{10,11},{12,13},{... | collective-permute-start | bytes 201608 | tf_op jit(solution)/shard_map/ppermute | solution.py:24
  49.1 1.7 %copy.21 = f32[100,28,6]{0,1,2:T(8,128)} copy(f32[100,28,6]{2,1,0:T(8,128)S(1)} %get-tuple-element.25) | data formatting | bytes 134400 | tf_op jit(solution)/shard_map/slice | solution.py:20
  50.8 1.3 %collective-permute-start.3 = (f32[100,28,6]{0,1,2:T(8,128)}, f32[100,28,6]{0,1,2:T(8,128)}, u32[]{:S(2)}, u32[]{:S(2)}) collective-permute-start(f32[100,28,6]{0,1,2:T(8,128)} %copy.21), channel_id=1, source_target_pairs={{1,0},{2,1},{3,2},{5,4},{6,5},{7,6},{9,8},{10,9},{11,10},{13,12},{... | collective-permute-start | bytes 201608 | tf_op jit(solution)/shard_map/ppermute | solution.py:26
  52.8 2.4 %copy.22 = f32[100,28,6]{2,1,0:T(8,128)S(1)} copy(f32[100,28,6]{0,1,2:T(8,128)} %collective-permute-done.2) | data formatting | bytes 134400 | tf_op jit(solution)/shard_map/ppermute | solution.py:24
  55.2 1.2 %collective-permute-done.3 = f32[100,28,6]{0,1,2:T(8,128)} collective-permute-done((f32[100,28,6]{0,1,2:T(8,128)}, f32[100,28,6]{0,1,2:T(8,128)}, u32[]{:S(2)}, u32[]{:S(2)}) %collective-permute-start.3) | collective-permute-done | bytes 67232 | tf_op jit(solution)/shard_map/ppermute | solution.py:26
  56.5 3.3 %copy.23 = f32[100,28,6]{2,1,0:T(8,128)} copy(f32[100,28,6]{0,1,2:T(8,128)} %collective-permute-done.3) | data formatting | bytes 134400 | tf_op jit(solution)/shard_map/ppermute | solution.py:26
  59.8 4.2 %select_maximum_fusion.both_ref = f32[100,32,256]{2,1,0:T(8,128)S(1)} fusion(f32[100,28,6]{2,1,0:T(8,128)} %copy.23, f32[100,28,6]{2,1,0:T(8,128)S(1)} %copy.22, f32[100,6,128]{2,1,0:T(8,128)} %copy-done.4, f32[100,6,128]{2,1,0:T(8,128)S(1)} %collective-permute-done, f32[50,16,128]{2,1,0:T(8,128)S(1)} %copy-done.2, f32[50,16,128]{2,1,0:T(8,128)S(1)} %fusion.13), kind=kLoop, calls=%fused_computation | loop fusion | flops 16384000 | bytes 4844800 | tf_op jit(solution)/shard_map/concatenate | solution.py:22
  64.0 36.3 %shard_map.113 = f32[50,16,128]{2,1,0:T(8,128)} custom-call(f32[100,32,256]{2,1,0:T(8,128)S(1)} %select_maximum_fusion.both_ref, f32[32,256]{1,0:T(8,128)S(1)} %pad_convert_fusion.mask_ref), custom_call_target="tpu_custom_call" | custom-call | flops 49152000 | bytes 3686400 | tf_op jit(solution)/shard_map/pallas_call | solution.py:169
  100.3 1.6 %fusion.34 = f32[4,32,128]{2,1,0:T(8,128)} fusion(f32[4,32]{1,0:T(4,128)S(1)} %bitcast.54, f32[50,16,128]{2,1,0:T(8,128)} %shard_map.113), kind=kOutput, calls=%fused_computation.54 | convolution fusion | flops 3147776 | bytes 74240 | tf_op jit(solution)/shard_map/dot_general | solution.py:246
  101.9 3.3 %all-to-all-start.1 = ((f32[4,32,128]{2,1,0:T(8,128)}), f32[4,32,128]{2,1,0:T(8,128)S(1)}, u32[]{:S(2)}, u32[]{:S(2)}) async-start(f32[4,32,128]{2,1,0:T(8,128)} %fusion.34), calls=%async_computation.1 | async-start | bytes 131072 | tf_op jit(solution)/shard_map/all_to_all | solution.py:249
  105.2 4.4 %all-to-all-done.1 = f32[4,32,128]{2,1,0:T(8,128)S(1)} async-done(((f32[4,32,128]{2,1,0:T(8,128)}), f32[4,32,128]{2,1,0:T(8,128)S(1)}, u32[]{:S(2)}, u32[]{:S(2)}) %all-to-all-start.1) | async-done | bytes 65568 | tf_op jit(solution)/shard_map/all_to_all | solution.py:249
  109.9 0.9 copy_bitcast_fusion.2
  (49 shorter events, 6.9 us)
Async XLA Ops:
  0.6 3.2 %copy-start = (f32[64,20,128]{2,0,1:T(8,128)S(1)}, f32[64,20,128]{2,0,1:T(8,128)}, u32[]{:S(2)}) copy-start(f32[64,20,128]{2,0,1:T(8,128)} %param.11) | copy-start | bytes 1966084
  0.6 20.7 %copy-start.1 = (f32[50,16,128]{2,1,0:T(8,128)S(1)}, f32[50,16,128]{2,1,0:T(8,128)}, u32[]{:S(2)}) copy-start(f32[50,16,128]{2,1,0:T(8,128)} %param.14) | copy-start | bytes 1228804
  0.7 20.8 %copy-start.2 = (f32[50,16,128]{2,1,0:T(8,128)S(1)}, f32[50,16,128]{2,1,0:T(8,128)}, u32[]{:S(2)}) copy-start(f32[50,16,128]{2,1,0:T(8,128)} %param.15) | copy-start | bytes 1228804
  0.7 10.3 %copy-start.11 = (s32[64]{0:T(128)S(1)}, s32[64]{0:T(128)}, u32[]{:S(2)}) copy-start(s32[64]{0:T(128)} %param.17) | copy-start | bytes 772
  2.9 9.2 %copy-start.7 = (s32[4,64]{1,0:T(4,128)}, s32[4,64]{1,0:T(4,128)S(1)}, u32[]{:S(2)}) copy-start(s32[4,64]{1,0:T(4,128)S(1)} %fusion.43) | copy-start | bytes 3076
  3.8 17.7 %copy-start.5 = (s32[32,64]{1,0:T(8,128)}, s32[32,64]{1,0:T(8,128)S(1)}, u32[]{:S(2)}) copy-start(s32[32,64]{1,0:T(8,128)S(1)} %fusion.38) | copy-start | bytes 24580
  12.0 8.6 %all-to-all-start = ((f32[4,33,128]{2,1,0:T(8,128)}), f32[4,33,128]{2,1,0:T(8,128)S(1)}, u32[]{:S(2)}, u32[]{:S(2)}) async-start(f32[4,33,128]{2,1,0:T(8,128)} %pad_maximum_fusion.2), calls=%async_computation | async-start | bytes 163840 | tf_op jit(solution)/shard_map/all_to_all | solution.py:215
  21.5 11.3 %collective-permute-start = (f32[100,6,128]{2,1,0:T(8,128)S(1)}, f32[100,6,128]{2,1,0:T(8,128)S(1)}, u32[]{:S(2)}, u32[]{:S(2)}) collective-permute-start(f32[100,6,128]{2,1,0:T(8,128)S(1)} %get-tuple-element.26), channel_id=1, source_target_pairs={{0,4},{4,8},{8,12},{12,16},{16,20},{20,24},{24,28},{28,32},{32,36}... | collective-permute-start | bytes 921608 | tf_op jit(solution)/shard_map/ppermute | solution.py:24
  27.9 12.6 %collective-permute-start.1 = (f32[100,6,128]{2,1,0:T(8,128)S(1)}, f32[100,6,128]{2,1,0:T(8,128)S(1)}, u32[]{:S(2)}, u32[]{:S(2)}) collective-permute-start(f32[100,6,128]{2,1,0:T(8,128)S(1)} %get-tuple-element.27), channel_id=1, source_target_pairs={{4,0},{8,4},{12,8},{16,12},{20,16},{24,20},{28,24},{32,28},{36,32}... | collective-permute-start | bytes 921608 | tf_op jit(solution)/shard_map/ppermute | solution.py:26
  40.5 0.8 copy-start.4
  46.3 6.5 %collective-permute-start.2 = (f32[100,28,6]{0,1,2:T(8,128)}, f32[100,28,6]{0,1,2:T(8,128)}, u32[]{:S(2)}, u32[]{:S(2)}) collective-permute-start(f32[100,28,6]{0,1,2:T(8,128)} %copy.20), channel_id=1, source_target_pairs={{0,1},{1,2},{2,3},{4,5},{5,6},{6,7},{8,9},{9,10},{10,11},{12,13},{... | collective-permute-start | bytes 201608 | tf_op jit(solution)/shard_map/ppermute | solution.py:24
  50.8 5.7 %collective-permute-start.3 = (f32[100,28,6]{0,1,2:T(8,128)}, f32[100,28,6]{0,1,2:T(8,128)}, u32[]{:S(2)}, u32[]{:S(2)}) collective-permute-start(f32[100,28,6]{0,1,2:T(8,128)} %copy.21), channel_id=1, source_target_pairs={{1,0},{2,1},{3,2},{5,4},{6,5},{7,6},{9,8},{10,9},{11,10},{13,12},{... | collective-permute-start | bytes 201608 | tf_op jit(solution)/shard_map/ppermute | solution.py:26
  64.0 36.3 %copy-start.9 = (f32[4,1,32]{2,1,0:T(1,128)S(1)}, f32[4,1,32]{2,1,0:T(1,128)}, u32[]{:S(2)}) copy-start(f32[4,1,32]{2,1,0:T(1,128)} %get-tuple-element.28) | copy-start | bytes 1540
  64.0 45.6 %copy-start.3 = (f32[64,2560]{1,0:T(8,128)S(1)}, f32[64,2560]{1,0:T(8,128)}, u32[]{:S(2)}) copy-start(f32[64,2560]{1,0:T(8,128)} %shard_map.112) | copy-start | bytes 1966084
  64.0 45.6 %copy-start.6 = (s32[32,64]{1,0:T(8,128)S(1)}, s32[32,64]{1,0:T(8,128)}, u32[]{:S(2)}) copy-start(s32[32,64]{1,0:T(8,128)} %copy-done.5) | copy-start | bytes 24580
  64.0 45.6 %copy-start.8 = (s32[4,64]{1,0:T(4,128)S(1)}, s32[4,64]{1,0:T(4,128)}, u32[]{:S(2)}) copy-start(s32[4,64]{1,0:T(4,128)} %copy-done.7) | copy-start | bytes 3076
  64.0 45.9 %slice-start = ((f32[64,2560]{1,0:T(8,128)}), f32[64,2432]{1,0:T(8,128)S(1)}, s32[]{:S(2)}) async-start(f32[64,2560]{1,0:T(8,128)} %shard_map.112), calls=%async_computation.2 | async-start | bytes 1245184 | tf_op jit(solution)/shard_map/slice | solution.py:253
  64.0 46.8 %copy-start.10 = (s32[64]{0:T(128)S(1)}, s32[64]{0:T(128)}, u32[]{:S(2)}) copy-start(s32[64]{0:T(128)} %param.18) | copy-start | bytes 772
  101.9 7.7 %all-to-all-start.1 = ((f32[4,32,128]{2,1,0:T(8,128)}), f32[4,32,128]{2,1,0:T(8,128)S(1)}, u32[]{:S(2)}, u32[]{:S(2)}) async-start(f32[4,32,128]{2,1,0:T(8,128)} %fusion.34), calls=%async_computation.1 | async-start | bytes 131072 | tf_op jit(solution)/shard_map/all_to_all | solution.py:249

commit v5 on v3

--- a/solution.py
+++ b/solution.py
@@ -4,6 +4,7 @@
 from jax.sharding import PartitionSpec as P
 from jax.experimental import pallas as pl
 from jax.experimental.pallas import tpu as pltpu
+from jax.experimental.layout import Layout, with_layout_constraint
 
 PATCH_DEV = 8
 SWEEPS = 6
@@ -141,9 +142,35 @@
     recharge = jnp.dot(landing, incoming.reshape(slot_total, tile_cols), precision=highest)
     field = head.at[0].add(recharge)
     layers = field.shape[0]
-    both = with_halo(
-        jnp.concatenate([field, conductivity], axis=0), (("gx", 1), ("gy", 2)), SWEEPS
-    )
+    stacked = jnp.concatenate([field, conductivity], axis=0)
+    rowed = with_halo(stacked, (("gx", 1),), SWEEPS)
+    halo_rows = rowed.shape[1]
+    tiled_rows = -(-halo_rows // 8) * 8
+    flat = jnp.pad(rowed, ((0, 0), (0, tiled_rows - halo_rows), (0, 0))).reshape(-1, tile_cols)
+    picks = jnp.arange(SWEEPS, dtype=jnp.int32)[:, None]
+    lanes = jnp.arange(tile_cols, dtype=jnp.int32)[None, :]
+    by_lane = (((1,), (1,)), ((), ()))
+    left_strip = lax.dot_general(
+        (lanes == picks).astype(jnp.float32), flat, by_lane, precision=highest
+    )
+    right_strip = lax.dot_general(
+        (lanes == tile_cols - SWEEPS + picks).astype(jnp.float32), flat, by_lane, precision=highest
+    )
+    ends = tile_count - 1
+    from_left = lax.ppermute(right_strip, "gy", [(i, i + 1) for i in range(ends)])
+    from_right = lax.ppermute(left_strip, "gy", [(i + 1, i) for i in range(ends)])
+    width = tile_cols + 2 * SWEEPS
+    out_lanes = jnp.arange(width, dtype=jnp.int32)[None, :]
+    side = jnp.dot(
+        jnp.concatenate([from_left, from_right], axis=0).T,
+        jnp.concatenate(
+            [out_lanes == picks, out_lanes == tile_cols + SWEEPS + picks], axis=0
+        ).astype(jnp.float32),
+        precision=highest,
+    )
+    side = with_layout_constraint(side, Layout((0, 1)))
+    middle = jnp.pad(flat, ((0, 0), (SWEEPS, SWEEPS)))
+    both = (middle + side).reshape(stacked.shape[0], tiled_rows, width)[:, :halo_rows, :]
     field = both[:layers]
     padded_cond = both[layers:]
     row_at = (

time: 100 us -> 87.1 us (0.87)
  local copies, waits for them, and re-layouts: 18.4 us -> 1.78 us
  blocking collectives: 8.38 us -> 0 us
  waiting for transfers between devices: 15.1 us -> 23.1 us
  matrix products: 3.31 us -> 7.41 us
  other arithmetic: 32.2 us -> 29.4 us
  starting transfers between devices: 16.4 us -> 19.1 us
    all_to_all x1 -> x0, blocking collectives: 8.38 us -> none  [local(): lax.all_to_all(packed, 'gy', split_axis=0, concat_axis=0, tiled=True)]
    slice x3 -> x0, local copies, waits for them, and re-layouts: 7.04 us -> none  [the longest x2 5.32 us: with_halo(): lax.slice_in_dim(cells, cells.shape[dim] - width, cells.shape[dim], axis=...]
    ppermute x2 -> x0, local copies, waits for them, and re-layouts: 5.78 us -> none  [the longest x1 3.36 us: with_halo(): lax.ppermute(head, axis, [((i + 1) % count, i) for i in range(ends)])]
    all_to_all x0 -> x1, waiting for transfers between devices: none -> 4.53 us  [local(): lax.all_to_all(packed, 'gy', split_axis=0, concat_axis=0, tiled=True)]
    dot_general x0 -> x3, matrix products: none -> 4.09 us  [the longest x1 2.33 us: local(): jnp.dot(jnp.concatenate([from_left, from_right], axis=0).T, jnp.concatena...]
    all_to_all x0 -> x1, starting transfers between devices: none -> 4.01 us  [local(): lax.all_to_all(packed, 'gy', split_axis=0, concat_axis=0, tiled=True)]
    ppermute x0 -> x2, waiting for transfers between devices: none -> 3.62 us  [the longest x1 3.62 us: local(): lax.ppermute(left_strip, 'gy', [(i + 1, i) for i in range(ends)])]
    ppermute x0 -> x2, starting transfers between devices: none -> 3.5 us  [the longest x1 2.21 us: local(): lax.ppermute(right_strip, 'gy', [(i, i + 1) for i in range(ends)])]
  transfers between devices with their start and end apart: 5 -> 6, of which waited for: 3 -> 5; matrix products, arithmetic and copies ran while one was open for 6% -> 1% of each run, Pallas kernels for 0% -> 0%
where the time goes in v5:
time: 87.1 us; the launch traced here: 86.6 us
  other arithmetic  29.4 us (34%)
  waiting for transfers between devices  23.1 us (27%)
  starting transfers between devices  19.1 us (22%)
  matrix products  7.41 us (9%)
  Pallas kernels  3.98 us (5%)
  local copies, waits for them, and re-layouts  1.78 us (2%)
  between operations  1.71 us (2%)
    select_n x5, other arithmetic, local(): field = jnp.where(inside[None, edge:-edge, edge:-edge], field, 0.0)  16.4 us
    ppermute x1, waiting for transfers between devices, with_halo(): lax.ppermute(head, axis, [((i + 1) % count, i) for i in range(ends)])  7.72 us
    mul x6, other arithmetic, lateral_core(): 0.5 * (centre_cond[1:] + centre_cond[:-1]) * (centre[1:] - centre[:-1])  7.6 us
    ppermute x1, starting transfers between devices, with_halo(): lax.ppermute(tail, axis, [(i, (i + 1) % count) for i in range(ends)])  6.41 us
    all_to_all x1, waiting for transfers between devices, local(): lax.all_to_all(packed, 'gy', split_axis=0, concat_axis=0, tiled=True)  4.53 us
    all_to_all x1, waiting for transfers between devices, local(): lax.all_to_all(answered, 'gy', split_axis=0, concat_axis=0, tiled=True)  4.42 us
    all_to_all x1, starting transfers between devices, local(): lax.all_to_all(packed, 'gy', split_axis=0, concat_axis=0, tiled=True)  4.01 us
    pallas_call x1, Pallas kernels, column_solve(): pl.pallas_call(column_kernel, out_shape=jax.ShapeDtypeStruct(flat, jnp.fl...  3.98 us
  transfers between devices with their start and end apart: 6, of which 5 were waited for; matrix products, arithmetic and copies ran while one was open for 1% of the time, Pallas kernels for 0%

profile of v5, /device:TPU:249, one launch (start us, length us, event | category | flops | bytes accessed | tf_op | source)
XLA Modules:
  0.0 86.6 jit_solution(12927859913649292969)
XLA Ops:
  3.8 1.2 %copy_bitcast_fusion = (f32[64,2560]{1,0:T(8,128)}, f32[64,2560]{1,0:T(8,128)}) fusion(f32[64,20,128]{2,0,1:T(8,128)S(1)} %copy-done, f32[64,20,128]{2,0,1:T(8,128)S(1)} %copy-done.4), kind=kLoop, calls=%fused_computation.153 | loop fusion | bytes 2621440 | tf_op jit(solution)/shard_map/reshape | solution.py:81
  5.0 4.0 %shard_map.112 = f32[64,2560]{1,0:T(8,128)} custom-call(f32[64,2560]{1,0:T(8,128)} %get-tuple-element.28.moist_ref, f32[64,2560]{1,0:T(8,128)} %get-tuple-element.27.diff_ref, f32[64,128]{1,0:T(8,128)} %rain_ref.1), custom_call_target="tpu_custom_call" | custom-call | flops 1966080 | bytes 1966080 | tf_op jit(solution)/shard_map/pallas_call | solution.py:72
  11.0 4.0 %all-to-all-start = ((f32[4,33,128]{2,1,0:T(8,128)}), f32[4,33,128]{2,1,0:T(8,128)S(1)}, u32[]{:S(2)}, u32[]{:S(2)}) async-start(f32[4,33,128]{2,1,0:T(8,128)} %pad_maximum_fusion.1), calls=%async_computation | async-start | bytes 163840 | tf_op jit(solution)/shard_map/all_to_all | solution.py:135
  15.0 4.5 %all-to-all-done = f32[4,33,128]{2,1,0:T(8,128)S(1)} async-done(((f32[4,33,128]{2,1,0:T(8,128)}), f32[4,33,128]{2,1,0:T(8,128)S(1)}, u32[]{:S(2)}, u32[]{:S(2)}) %all-to-all-start) | async-done | bytes 67616 | tf_op jit(solution)/shard_map/all_to_all | solution.py:135
  19.9 6.4 %collective-permute-start = (f32[100,6,128]{2,1,0:T(8,128)S(1)}, f32[100,6,128]{2,1,0:T(8,128)S(1)}, u32[]{:S(2)}, u32[]{:S(2)}) collective-permute-start(f32[100,6,128]{2,1,0:T(8,128)S(1)} %get-tuple-element.21), channel_id=1, source_target_pairs={{0,4},{4,8},{8,12},{12,16},{16,20},{20,24},{24,28},{28,32},{32,36}... | collective-permute-start | bytes 921608 | tf_op jit(solution)/shard_map/ppermute | solution.py:25
  26.3 1.9 %collective-permute-start.1 = (f32[100,6,128]{2,1,0:T(8,128)S(1)}, f32[100,6,128]{2,1,0:T(8,128)S(1)}, u32[]{:S(2)}, u32[]{:S(2)}) collective-permute-start(f32[100,6,128]{2,1,0:T(8,128)S(1)} %get-tuple-element.22), channel_id=1, source_target_pairs={{4,0},{8,4},{12,8},{16,12},{20,16},{24,20},{28,24},{32,28},{36,32}... | collective-permute-start | bytes 921608 | tf_op jit(solution)/shard_map/ppermute | solution.py:27
  28.3 2.9 %collective-permute-done = f32[100,6,128]{2,1,0:T(8,128)S(1)} collective-permute-done((f32[100,6,128]{2,1,0:T(8,128)S(1)}, f32[100,6,128]{2,1,0:T(8,128)S(1)}, u32[]{:S(2)}, u32[]{:S(2)}) %collective-permute-start) | collective-permute-done | bytes 307232 | tf_op jit(solution)/shard_map/ppermute | solution.py:25
  31.2 7.7 %collective-permute-done.1 = f32[100,6,128]{2,1,0:T(8,128)S(1)} collective-permute-done((f32[100,6,128]{2,1,0:T(8,128)S(1)}, f32[100,6,128]{2,1,0:T(8,128)S(1)}, u32[]{:S(2)}, u32[]{:S(2)}) %collective-permute-start.1) | collective-permute-done | bytes 307232 | tf_op jit(solution)/shard_map/ppermute | solution.py:27
  41.0 2.2 %collective-permute-start.2 = (f32[6,3200]{1,0:T(8,128)S(1)}, f32[6,3200]{1,0:T(8,128)S(1)}, u32[]{:S(2)}, u32[]{:S(2)}) collective-permute-start(f32[6,3200]{1,0:T(8,128)S(1)} %fusion.147), channel_id=1, source_target_pairs={{0,1},{1,2},{2,3},{4,5},{5,6},{6,7},{8,9},{9,10},{10,11},{12,13},{... | collective-permute-start | bytes 230408 | tf_op jit(solution)/shard_map/ppermute | solution.py:160
  43.2 1.3 %collective-permute-start.3 = (f32[6,3200]{1,0:T(8,128)S(1)}, f32[6,3200]{1,0:T(8,128)S(1)}, u32[]{:S(2)}, u32[]{:S(2)}) collective-permute-start(f32[6,3200]{1,0:T(8,128)S(1)} %fusion.148), channel_id=1, source_target_pairs={{1,0},{2,1},{3,2},{5,4},{6,5},{7,6},{9,8},{10,9},{11,10},{13,12},{... | collective-permute-start | bytes 230408 | tf_op jit(solution)/shard_map/ppermute | solution.py:161
  45.0 3.6 %collective-permute-done.3 = f32[6,3200]{1,0:T(8,128)S(1)} collective-permute-done((f32[6,3200]{1,0:T(8,128)S(1)}, f32[6,3200]{1,0:T(8,128)S(1)}, u32[]{:S(2)}, u32[]{:S(2)}) %collective-permute-start.3) | collective-permute-done | bytes 76832 | tf_op jit(solution)/shard_map/ppermute | solution.py:161
  48.6 2.3 %pad_add_fusion = f32[3200,140]{1,0:T(8,128)S(1)} fusion(f32[3200,128]{1,0:T(8,128)S(1)} %bitcast.70, f32[6,3200]{1,0:T(8,128)S(1)} %collective-permute-done.3, f32[6,3200]{1,0:T(8,128)S(1)} %collective-permute-done.2, pred[6,140]{1,0:T(8,128)(4,1)S(1)} %get-tuple-element.29, pred[6,140]{1,0:T(8,128)(4,1)S(1)} %get-tuple-element.30), kind=kOutput, calls=%fused_computation | convolution fusion | flops 65000080 | bytes 3585680 | tf_op jit(solution)/shard_map/dot_general | solution.py:164
  50.9 1.8 %fusion.19 = f32[49,26,138]{2,1,0:T(8,128)S(1)} fusion(f32[100,32,140]{2,1,0:T(8,128)S(1)} %bitcast.56), kind=kLoop, calls=%fused_computation.32 | loop fusion | flops 703248 | bytes 3516240 | tf_op jit(solution)/shard_map/mul | solution.py:99
  52.7 3.8 %fusion.6 = f32[50,26,138]{2,1,0:T(8,128)S(1)} fusion(f32[100,32,140]{2,1,0:T(8,128)S(1)} %bitcast.57, f32[49,26,138]{2,1,0:T(8,128)S(1)} %fusion.19, pred[26,138]{1,0:T(8,128)(4,1)S(1)} %slice.484), kind=kLoop, calls=%fused_computation.8 | loop fusion | flops 4305600 | bytes 8600436 | tf_op jit(solution)/shard_map/jit(_where)/select_n | solution.py:193
  56.5 1.3 %fusion.91 = f32[49,24,136]{2,1,0:T(8,128)S(1)} fusion(f32[50,26,138]{2,1,0:T(8,128)S(1)} %fusion.6, f32[100,32,140]{2,1,0:T(8,128)S(1)} %bitcast.58), kind=kLoop, calls=%fused_computation.144 | loop fusion | flops 639744 | bytes 3198720 | tf_op jit(solution)/shard_map/mul | solution.py:99
  57.8 3.1 %fusion.75 = f32[50,24,136]{2,1,0:T(8,128)S(1)} fusion(f32[50,26,138]{2,1,0:T(8,128)S(1)} %fusion.6, f32[100,32,140]{2,1,0:T(8,128)S(1)} %bitcast.59, f32[49,24,136]{2,1,0:T(8,128)S(1)} %fusion.91, pred[24,136]{1,0:T(8,128)(4,1)S(1)} %slice.483), kind=kLoop, calls=%fused_computation.114 | loop fusion | flops 3916800 | bytes 7823808 | tf_op jit(solution)/shard_map/jit(_where)/select_n | solution.py:193
  60.9 1.3 %fusion.89 = f32[49,22,134]{2,1,0:T(8,128)S(1)} fusion(f32[50,24,136]{2,1,0:T(8,128)S(1)} %fusion.75, f32[100,32,140]{2,1,0:T(8,128)S(1)} %bitcast.60), kind=kLoop, calls=%fused_computation.140 | loop fusion | flops 577808 | bytes 2889040 | tf_op jit(solution)/shard_map/mul | solution.py:99
  62.3 3.1 %fusion.59 = f32[50,22,134]{2,1,0:T(8,128)S(1)} fusion(f32[50,24,136]{2,1,0:T(8,128)S(1)} %fusion.75, f32[100,32,140]{2,1,0:T(8,128)S(1)} %bitcast.61, f32[49,22,134]{2,1,0:T(8,128)S(1)} %fusion.89, pred[22,134]{1,0:T(8,128)(4,1)S(1)} %slice.482), kind=kLoop, calls=%fused_computation.90 | loop fusion | flops 3537600 | bytes 7066356 | tf_op jit(solution)/shard_map/jit(_where)/select_n | solution.py:193
  65.4 1.3 %fusion.87 = f32[49,20,132]{2,1,0:T(8,128)S(1)} fusion(f32[50,22,134]{2,1,0:T(8,128)S(1)} %fusion.59, f32[100,32,140]{2,1,0:T(8,128)S(1)} %bitcast.62), kind=kLoop, calls=%fused_computation.136 | loop fusion | flops 517440 | bytes 2587200 | tf_op jit(solution)/shard_map/mul | solution.py:99
  66.7 3.1 %fusion.43 = f32[50,20,132]{2,1,0:T(8,128)S(1)} fusion(f32[50,22,134]{2,1,0:T(8,128)S(1)} %fusion.59, f32[100,32,140]{2,1,0:T(8,128)S(1)} %bitcast.63, f32[49,20,132]{2,1,0:T(8,128)S(1)} %fusion.87, pred[20,132]{1,0:T(8,128)(4,1)S(1)} %slice.481), kind=kLoop, calls=%fused_computation.66 | loop fusion | flops 3168000 | bytes 6328080 | tf_op jit(solution)/shard_map/jit(_where)/select_n | solution.py:193
  69.8 1.3 %fusion.85 = f32[49,18,130]{2,1,0:T(8,128)S(1)} fusion(f32[50,20,132]{2,1,0:T(8,128)S(1)} %fusion.43, f32[100,32,140]{2,1,0:T(8,128)S(1)} %bitcast.64), kind=kLoop, calls=%fused_computation.132 | loop fusion | flops 458640 | bytes 2293200 | tf_op jit(solution)/shard_map/mul | solution.py:99
  71.2 3.3 %fusion.27 = f32[50,18,130]{2,1,0:T(8,128)S(1)} fusion(f32[50,20,132]{2,1,0:T(8,128)S(1)} %fusion.43, f32[100,32,140]{2,1,0:T(8,128)S(1)} %bitcast.65, f32[49,18,130]{2,1,0:T(8,128)S(1)} %fusion.85, pred[18,130]{1,0:T(8,128)(4,1)S(1)} %slice.480), kind=kLoop, calls=%fused_computation.42 | loop fusion | flops 2808000 | bytes 5608980 | tf_op jit(solution)/shard_map/jit(_where)/select_n | solution.py:193
  76.9 3.3 %all-to-all-start.1 = ((f32[4,32,128]{2,1,0:T(8,128)}), f32[4,32,128]{2,1,0:T(8,128)S(1)}, u32[]{:S(2)}, u32[]{:S(2)}) async-start(f32[4,32,128]{2,1,0:T(8,128)} %fusion.138), calls=%async_computation.1 | async-start | bytes 131072 | tf_op jit(solution)/shard_map/all_to_all | solution.py:198
  80.2 4.4 %all-to-all-done.1 = f32[4,32,128]{2,1,0:T(8,128)S(1)} async-done(((f32[4,32,128]{2,1,0:T(8,128)}), f32[4,32,128]{2,1,0:T(8,128)S(1)}, u32[]{:S(2)}, u32[]{:S(2)}) %all-to-all-start.1) | async-done | bytes 65568 | tf_op jit(solution)/shard_map/all_to_all | solution.py:198
  (56 shorter events, 11.6 us)
Async XLA Ops:
  0.6 3.1 %copy-start = (f32[64,20,128]{2,0,1:T(8,128)S(1)}, f32[64,20,128]{2,0,1:T(8,128)}, u32[]{:S(2)}) copy-start(f32[64,20,128]{2,0,1:T(8,128)} %param.11) | copy-start | bytes 1966084
  0.6 3.1 %copy-start.4 = (f32[64,20,128]{2,0,1:T(8,128)S(1)}, f32[64,20,128]{2,0,1:T(8,128)}, u32[]{:S(2)}) copy-start(f32[64,20,128]{2,0,1:T(8,128)} %param.12) | copy-start | bytes 1966084
  5.0 5.0 %copy-start.7 = (s32[64]{0:T(128)S(1)}, s32[64]{0:T(128)}, u32[]{:S(2)}) copy-start(s32[64]{0:T(128)} %param.17) | copy-start | bytes 772
  5.0 14.7 %copy-start.1 = (f32[50,16,128]{2,1,0:T(8,128)S(1)}, f32[50,16,128]{2,1,0:T(8,128)}, u32[]{:S(2)}) copy-start(f32[50,16,128]{2,1,0:T(8,128)} %param.14) | copy-start | bytes 1228804
  5.0 14.8 %copy-start.3 = (f32[50,16,128]{2,1,0:T(8,128)S(1)}, f32[50,16,128]{2,1,0:T(8,128)}, u32[]{:S(2)}) copy-start(f32[50,16,128]{2,1,0:T(8,128)} %param.15) | copy-start | bytes 1228804
  11.0 8.6 %all-to-all-start = ((f32[4,33,128]{2,1,0:T(8,128)}), f32[4,33,128]{2,1,0:T(8,128)S(1)}, u32[]{:S(2)}, u32[]{:S(2)}) async-start(f32[4,33,128]{2,1,0:T(8,128)} %pad_maximum_fusion.1), calls=%async_computation | async-start | bytes 163840 | tf_op jit(solution)/shard_map/all_to_all | solution.py:135
  19.9 11.3 %collective-permute-start = (f32[100,6,128]{2,1,0:T(8,128)S(1)}, f32[100,6,128]{2,1,0:T(8,128)S(1)}, u32[]{:S(2)}, u32[]{:S(2)}) collective-permute-start(f32[100,6,128]{2,1,0:T(8,128)S(1)} %get-tuple-element.21), channel_id=1, source_target_pairs={{0,4},{4,8},{8,12},{12,16},{16,20},{20,24},{24,28},{28,32},{32,36}... | collective-permute-start | bytes 921608 | tf_op jit(solution)/shard_map/ppermute | solution.py:25
  26.3 12.6 %collective-permute-start.1 = (f32[100,6,128]{2,1,0:T(8,128)S(1)}, f32[100,6,128]{2,1,0:T(8,128)S(1)}, u32[]{:S(2)}, u32[]{:S(2)}) collective-permute-start(f32[100,6,128]{2,1,0:T(8,128)S(1)} %get-tuple-element.22), channel_id=1, source_target_pairs={{4,0},{8,4},{12,8},{16,12},{20,16},{24,20},{28,24},{32,28},{36,32}... | collective-permute-start | bytes 921608 | tf_op jit(solution)/shard_map/ppermute | solution.py:27
  41.0 4.0 %collective-permute-start.2 = (f32[6,3200]{1,0:T(8,128)S(1)}, f32[6,3200]{1,0:T(8,128)S(1)}, u32[]{:S(2)}, u32[]{:S(2)}) collective-permute-start(f32[6,3200]{1,0:T(8,128)S(1)} %fusion.147), channel_id=1, source_target_pairs={{0,1},{1,2},{2,3},{4,5},{5,6},{6,7},{8,9},{9,10},{10,11},{12,13},{... | collective-permute-start | bytes 230408 | tf_op jit(solution)/shard_map/ppermute | solution.py:160
  43.2 5.4 %collective-permute-start.3 = (f32[6,3200]{1,0:T(8,128)S(1)}, f32[6,3200]{1,0:T(8,128)S(1)}, u32[]{:S(2)}, u32[]{:S(2)}) collective-permute-start(f32[6,3200]{1,0:T(8,128)S(1)} %fusion.148), channel_id=1, source_target_pairs={{1,0},{2,1},{3,2},{5,4},{6,5},{7,6},{9,8},{10,9},{11,10},{13,12},{... | collective-permute-start | bytes 230408 | tf_op jit(solution)/shard_map/ppermute | solution.py:161
  76.0 9.9 %copy-start.5 = (f32[50,16,128]{2,1,0:T(8,128)}, f32[50,16,128]{2,1,0:T(8,128)S(1)}, u32[]{:S(2)}) copy-start(f32[50,16,128]{2,1,0:T(8,128)S(1)} %fusion.101) | copy-start | bytes 1228804
  76.0 8.6 %copy-start.2 = (f32[64,2560]{1,0:T(8,128)S(1)}, f32[64,2560]{1,0:T(8,128)}, u32[]{:S(2)}) copy-start(f32[64,2560]{1,0:T(8,128)} %shard_map.112) | copy-start | bytes 1966084
  76.0 8.9 %slice-start = ((f32[64,2560]{1,0:T(8,128)}), f32[64,2432]{1,0:T(8,128)S(1)}, s32[]{:S(2)}) async-start(f32[64,2560]{1,0:T(8,128)} %shard_map.112), calls=%async_computation.2 | async-start | bytes 1245184 | tf_op jit(solution)/shard_map/slice | solution.py:202
  76.9 7.7 %all-to-all-start.1 = ((f32[4,32,128]{2,1,0:T(8,128)}), f32[4,32,128]{2,1,0:T(8,128)S(1)}, u32[]{:S(2)}, u32[]{:S(2)}) async-start(f32[4,32,128]{2,1,0:T(8,128)} %fusion.138), calls=%async_computation.1 | async-start | bytes 131072 | tf_op jit(solution)/shard_map/all_to_all | solution.py:198
  80.2 5.6 %copy-start.6 = (s32[64]{0:T(128)S(1)}, s32[64]{0:T(128)}, u32[]{:S(2)}) copy-start(s32[64]{0:T(128)} %param.18) | copy-start | bytes 772

commit v6 on v5

--- a/solution.py
+++ b/solution.py
@@ -96,13 +96,32 @@
             :, row_shift : row_shift + inner_rows, col_shift : col_shift + inner_cols
         ]
         flux_total = flux_total + 0.5 * (centre_cond + beside_cond) * (beside - centre)
-    vertical = 0.5 * (centre_cond[1:] + centre_cond[:-1]) * (centre[1:] - centre[:-1])
+    downward = 0.5 * (centre_cond[1:] + centre_cond[:-1]) * (centre[1:] - centre[:-1])
+    upward = 0.5 * (centre_cond[:-1] + centre_cond[1:]) * (centre[1:] - centre[:-1])
     flux_total = (
         flux_total
-        + jnp.pad(vertical, ((0, 1), (0, 0), (0, 0)))
-        - jnp.pad(vertical, ((1, 0), (0, 0), (0, 0)))
+        + jnp.pad(downward, ((0, 1), (0, 0), (0, 0)))
+        - jnp.pad(upward, ((1, 0), (0, 0), (0, 0)))
     )
     return centre + flow_rate * flux_total
+
+
+def exchange(chunks, axis):
+    count = lax.axis_size(axis)
+    me = lax.axis_index(axis)
+    own = lax.dynamic_index_in_dim(chunks, me, axis=0, keepdims=False)
+    got = [own]
+    for shift in range(1, count):
+        outgoing = lax.dynamic_index_in_dim(chunks, (me + shift) % count, axis=0, keepdims=False)
+        got.append(lax.ppermute(outgoing, axis, [(i, (i + shift) % count) for i in range(count)]))
+    placed = []
+    for source in range(count):
+        distance = (me - source) % count
+        pick = got[0]
+        for shift in range(1, count):
+            pick = jnp.where(distance == shift, got[shift], pick)
+        placed.append(pick)
+    return jnp.stack(placed)
 
 
 def local(moisture, diffusivity, rain, head, conductivity, tile_ids, offsets, patch_ids, counts):
@@ -132,7 +151,7 @@
     packed = jnp.concatenate(
         [outgoing, jnp.pad(out_rows, ((0, 0), (0, tile_cols - capacity)))[:, None, :]], axis=1
     )
-    arrived = lax.all_to_all(packed, "gy", split_axis=0, concat_axis=0, tiled=True)
+    arrived = exchange(packed, "gy")
     incoming = arrived[:, :capacity, :]
     in_rows = arrived[:, capacity, :capacity]
     slot_total = tile_count * capacity
@@ -195,7 +214,7 @@
     answered = jnp.dot(landing.T, surface, precision=highest).reshape(
         tile_count, capacity, tile_cols
     )
-    returned = lax.all_to_all(answered, "gy", split_axis=0, concat_axis=0, tiled=True)
+    returned = exchange(answered, "gy")
     saturation = jnp.einsum("tcb,tcj->bj", placing, returned, precision=highest)
     new_bottom = bottom + capillary * (saturation - in_use_f[:, None] * bottom)
     moisture_out = jnp.concatenate(

time: 87.1 us -> 95.7 us (1.099)
  starting transfers between devices: 19.1 us -> 29.7 us
  waiting for transfers between devices: 23.1 us -> 21.1 us
    ppermute x0 -> x6, starting transfers between devices: none -> 18.4 us  [exchange(): lax.ppermute(outgoing, axis, [(i, (i + shift) % count) for i in range(cou...]
    all_to_all x2 -> x0, waiting for transfers between devices: 8.95 us -> none  [the longest x1 4.53 us: local(): lax.all_to_all(packed, 'gy', split_axis=0, concat_axis=0, tiled=True)]
    all_to_all x2 -> x0, starting transfers between devices: 7.3 us -> none  [the longest x1 4.01 us: local(): lax.all_to_all(packed, 'gy', split_axis=0, concat_axis=0, tiled=True)]
    ppermute x0 -> x6, waiting for transfers between devices: none -> 6.8 us  [exchange(): lax.ppermute(outgoing, axis, [(i, (i + shift) % count) for i in range(cou...]
  transfers between devices with their start and end apart: 6 -> 10, of which waited for: 5 -> 6; matrix products, arithmetic and copies ran while one was open for 1% -> 1% of each run, Pallas kernels for 0% -> 0%
where the time goes in v6:
time: 95.7 us; the launch traced here: 95.2 us
  starting transfers between devices  29.7 us (31%)
  other arithmetic  29.5 us (31%)
  waiting for transfers between devices  21.1 us (22%)
  matrix products  6.77 us (7%)
  Pallas kernels  3.96 us (4%)
  local copies, waits for them, and re-layouts  2.31 us (2%)
  between operations  1.95 us (2%)
    ppermute x6, starting transfers between devices, exchange(): lax.ppermute(outgoing, axis, [(i, (i + shift) % count) for i in range(cou...  18.4 us
    select_n x5, other arithmetic, local(): field = jnp.where(inside[None, edge:-edge, edge:-edge], field, 0.0)  16.4 us
    ppermute x1, waiting for transfers between devices, with_halo(): lax.ppermute(head, axis, [((i + 1) % count, i) for i in range(ends)])  7.72 us
    mul x6, other arithmetic, lateral_core(): 0.5 * (centre_cond[1:] + centre_cond[:-1]) * (centre[1:] - centre[:-1])  7.6 us
    ppermute x6, waiting for transfers between devices, exchange(): lax.ppermute(outgoing, axis, [(i, (i + shift) % count) for i in range(cou...  6.8 us
    ppermute x1, starting transfers between devices, with_halo(): lax.ppermute(tail, axis, [(i, (i + 1) % count) for i in range(ends)])  6.69 us
    pallas_call x1, Pallas kernels, column_solve(): pl.pallas_call(column_kernel, out_shape=jax.ShapeDtypeStruct(flat, jnp.fl...  3.96 us
    ppermute x1, waiting for transfers between devices, local(): lax.ppermute(left_strip, 'gy', [(i + 1, i) for i in range(ends)])  3.68 us
  transfers between devices with their start and end apart: 10, of which 6 were waited for; matrix products, arithmetic and copies ran while one was open for 1% of the time, Pallas kernels for 0%

profile of v6, /device:TPU:249, one launch (start us, length us, event | category | flops | bytes accessed | tf_op | source)
XLA Modules:
  0.0 95.2 jit_solution(6359093194859052116)
XLA Ops:
  5.1 4.0 %shard_map.112 = f32[64,2560]{1,0:T(8,128)} custom-call(f32[64,2560]{1,0:T(8,128)} %get-tuple-element.43.moist_ref, f32[64,2560]{1,0:T(8,128)} %get-tuple-element.42.diff_ref, f32[64,128]{1,0:T(8,128)} %rain_ref.1), custom_call_target="tpu_custom_call" | custom-call | flops 1966080 | bytes 1966080 | tf_op jit(solution)/shard_map/pallas_call | solution.py:72
  10.4 4.4 %collective-permute-start = (f32[33,128]{1,0:T(8,128)S(1)}, f32[33,128]{1,0:T(8,128)S(1)}, u32[]{:S(2)}, u32[]{:S(2)}) collective-permute-start(f32[33,128]{1,0:T(8,128)S(1)} %get-tuple-element.35), channel_id=1, source_target_pairs={{0,3},{1,0},{2,1},{3,2},{4,7},{5,4},{6,5},{7,6},{8,11},{9,8},{10,9... | collective-permute-start | bytes 50696 | tf_op jit(solution)/shard_map/ppermute | solution.py:116
  14.8 2.4 %collective-permute-start.1 = (f32[33,128]{1,0:T(8,128)S(1)}, f32[33,128]{1,0:T(8,128)S(1)}, u32[]{:S(2)}, u32[]{:S(2)}) collective-permute-start(f32[33,128]{1,0:T(8,128)S(1)} %get-tuple-element.36), channel_id=1, source_target_pairs={{0,2},{1,3},{2,0},{3,1},{4,6},{5,7},{6,4},{7,5},{8,10},{9,11},{10,... | collective-permute-start | bytes 50696 | tf_op jit(solution)/shard_map/ppermute | solution.py:116
  17.2 2.5 %collective-permute-start.2 = (f32[33,128]{1,0:T(8,128)S(1)}, f32[33,128]{1,0:T(8,128)S(1)}, u32[]{:S(2)}, u32[]{:S(2)}) collective-permute-start(f32[33,128]{1,0:T(8,128)S(1)} %get-tuple-element.34), channel_id=1, source_target_pairs={{0,1},{1,2},{2,3},{3,0},{4,5},{5,6},{6,7},{7,4},{8,9},{9,10},{10,1... | collective-permute-start | bytes 50696 | tf_op jit(solution)/shard_map/ppermute | solution.py:116
  20.8 2.1 %collective-permute-done.2 = f32[33,128]{1,0:T(8,128)S(1)} collective-permute-done((f32[33,128]{1,0:T(8,128)S(1)}, f32[33,128]{1,0:T(8,128)S(1)}, u32[]{:S(2)}, u32[]{:S(2)}) %collective-permute-start.2) | collective-permute-done | bytes 16928 | tf_op jit(solution)/shard_map/ppermute | solution.py:116
  24.5 6.7 %collective-permute-start.3 = (f32[100,6,128]{2,1,0:T(8,128)S(1)}, f32[100,6,128]{2,1,0:T(8,128)S(1)}, u32[]{:S(2)}, u32[]{:S(2)}) collective-permute-start(f32[100,6,128]{2,1,0:T(8,128)S(1)} %get-tuple-element.25), channel_id=1, source_target_pairs={{0,4},{4,8},{8,12},{12,16},{16,20},{20,24},{24,28},{28,32},{32,36}... | collective-permute-start | bytes 921608 | tf_op jit(solution)/shard_map/ppermute | solution.py:25
  31.2 1.9 %collective-permute-start.4 = (f32[100,6,128]{2,1,0:T(8,128)S(1)}, f32[100,6,128]{2,1,0:T(8,128)S(1)}, u32[]{:S(2)}, u32[]{:S(2)}) collective-permute-start(f32[100,6,128]{2,1,0:T(8,128)S(1)} %get-tuple-element.26), channel_id=1, source_target_pairs={{4,0},{8,4},{12,8},{16,12},{20,16},{24,20},{28,24},{32,28},{36,32}... | collective-permute-start | bytes 921608 | tf_op jit(solution)/shard_map/ppermute | solution.py:27
  33.2 2.9 %collective-permute-done.3 = f32[100,6,128]{2,1,0:T(8,128)S(1)} collective-permute-done((f32[100,6,128]{2,1,0:T(8,128)S(1)}, f32[100,6,128]{2,1,0:T(8,128)S(1)}, u32[]{:S(2)}, u32[]{:S(2)}) %collective-permute-start.3) | collective-permute-done | bytes 307232 | tf_op jit(solution)/shard_map/ppermute | solution.py:25
  36.1 7.7 %collective-permute-done.4 = f32[100,6,128]{2,1,0:T(8,128)S(1)} collective-permute-done((f32[100,6,128]{2,1,0:T(8,128)S(1)}, f32[100,6,128]{2,1,0:T(8,128)S(1)}, u32[]{:S(2)}, u32[]{:S(2)}) %collective-permute-start.4) | collective-permute-done | bytes 307232 | tf_op jit(solution)/shard_map/ppermute | solution.py:27
  49.0 3.7 %collective-permute-done.6 = f32[6,3200]{1,0:T(8,128)S(1)} collective-permute-done((f32[6,3200]{1,0:T(8,128)S(1)}, f32[6,3200]{1,0:T(8,128)S(1)}, u32[]{:S(2)}, u32[]{:S(2)}) %collective-permute-start.6) | collective-permute-done | bytes 76832 | tf_op jit(solution)/shard_map/ppermute | solution.py:180
  52.7 2.3 %pad_add_fusion = f32[3200,140]{1,0:T(8,128)S(1)} fusion(f32[3200,128]{1,0:T(8,128)S(1)} %bitcast.129, f32[6,3200]{1,0:T(8,128)S(1)} %collective-permute-done.6, f32[6,3200]{1,0:T(8,128)S(1)} %collective-permute-done.5, pred[6,140]{1,0:T(8,128)(4,1)S(1)} %get-tuple-element.44, pred[6,140]{1,0:T(8,128)(4,1)S(1)} %get-tuple-element.45), kind=kOutput, calls=%fused_computation | convolution fusion | flops 65000080 | bytes 3585680 | tf_op jit(solution)/shard_map/dot_general | solution.py:183
  55.0 1.8 %fusion.19 = f32[49,26,138]{2,1,0:T(8,128)S(1)} fusion(f32[100,32,140]{2,1,0:T(8,128)S(1)} %bitcast.115), kind=kLoop, calls=%fused_computation.32 | loop fusion | flops 703248 | bytes 3516240 | tf_op jit(solution)/shard_map/mul | solution.py:99
  56.8 3.8 %fusion.6 = f32[50,26,138]{2,1,0:T(8,128)S(1)} fusion(f32[100,32,140]{2,1,0:T(8,128)S(1)} %bitcast.116, f32[49,26,138]{2,1,0:T(8,128)S(1)} %fusion.19, pred[26,138]{1,0:T(8,128)(4,1)S(1)} %slice.508), kind=kLoop, calls=%fused_computation.8 | loop fusion | flops 4305600 | bytes 8600436 | tf_op jit(solution)/shard_map/jit(_where)/select_n | solution.py:212
  61.9 3.1 %fusion.75 = f32[50,24,136]{2,1,0:T(8,128)S(1)} fusion(f32[50,26,138]{2,1,0:T(8,128)S(1)} %fusion.6, f32[100,32,140]{2,1,0:T(8,128)S(1)} %bitcast.118, f32[49,24,136]{2,1,0:T(8,128)S(1)} %fusion.91, pred[24,136]{1,0:T(8,128)(4,1)S(1)} %slice.507), kind=kLoop, calls=%fused_computation.114 | loop fusion | flops 3916800 | bytes 7823808 | tf_op jit(solution)/shard_map/jit(_where)/select_n | solution.py:212
  65.0 1.3 %fusion.89 = f32[49,22,134]{2,1,0:T(8,128)S(1)} fusion(f32[50,24,136]{2,1,0:T(8,128)S(1)} %fusion.75, f32[100,32,140]{2,1,0:T(8,128)S(1)} %bitcast.119), kind=kLoop, calls=%fused_computation.140 | loop fusion | flops 577808 | bytes 2889040 | tf_op jit(solution)/shard_map/mul | solution.py:99
  66.3 3.1 %fusion.59 = f32[50,22,134]{2,1,0:T(8,128)S(1)} fusion(f32[50,24,136]{2,1,0:T(8,128)S(1)} %fusion.75, f32[100,32,140]{2,1,0:T(8,128)S(1)} %bitcast.120, f32[49,22,134]{2,1,0:T(8,128)S(1)} %fusion.89, pred[22,134]{1,0:T(8,128)(4,1)S(1)} %slice.506), kind=kLoop, calls=%fused_computation.90 | loop fusion | flops 3537600 | bytes 7066356 | tf_op jit(solution)/shard_map/jit(_where)/select_n | solution.py:212
  69.5 1.3 %fusion.87 = f32[49,20,132]{2,1,0:T(8,128)S(1)} fusion(f32[50,22,134]{2,1,0:T(8,128)S(1)} %fusion.59, f32[100,32,140]{2,1,0:T(8,128)S(1)} %bitcast.121), kind=kLoop, calls=%fused_computation.136 | loop fusion | flops 517440 | bytes 2587200 | tf_op jit(solution)/shard_map/mul | solution.py:99
  70.8 3.1 %fusion.43 = f32[50,20,132]{2,1,0:T(8,128)S(1)} fusion(f32[50,22,134]{2,1,0:T(8,128)S(1)} %fusion.59, f32[100,32,140]{2,1,0:T(8,128)S(1)} %bitcast.122, f32[49,20,132]{2,1,0:T(8,128)S(1)} %fusion.87, pred[20,132]{1,0:T(8,128)(4,1)S(1)} %slice.505), kind=kLoop, calls=%fused_computation.66 | loop fusion | flops 3168000 | bytes 6328080 | tf_op jit(solution)/shard_map/jit(_where)/select_n | solution.py:212
  73.9 1.3 %fusion.85 = f32[49,18,130]{2,1,0:T(8,128)S(1)} fusion(f32[50,20,132]{2,1,0:T(8,128)S(1)} %fusion.43, f32[100,32,140]{2,1,0:T(8,128)S(1)} %bitcast.123), kind=kLoop, calls=%fused_computation.132 | loop fusion | flops 458640 | bytes 2293200 | tf_op jit(solution)/shard_map/mul | solution.py:99
  75.2 3.3 %fusion.27 = f32[50,18,130]{2,1,0:T(8,128)S(1)} fusion(f32[50,20,132]{2,1,0:T(8,128)S(1)} %fusion.43, f32[100,32,140]{2,1,0:T(8,128)S(1)} %bitcast.124, f32[49,18,130]{2,1,0:T(8,128)S(1)} %fusion.85, pred[18,130]{1,0:T(8,128)(4,1)S(1)} %slice.504), kind=kLoop, calls=%fused_computation.42 | loop fusion | flops 2808000 | bytes 5608980 | tf_op jit(solution)/shard_map/jit(_where)/select_n | solution.py:212
  80.4 2.3 %collective-permute-start.7 = (f32[32,128]{1,0:T(8,128)S(1)}, f32[32,128]{1,0:T(8,128)S(1)}, u32[]{:S(2)}, u32[]{:S(2)}) collective-permute-start(f32[32,128]{1,0:T(8,128)S(1)} %get-tuple-element.39), channel_id=1, source_target_pairs={{0,3},{1,0},{2,1},{3,2},{4,7},{5,4},{6,5},{7,6},{8,11},{9,8},{10,9... | collective-permute-start | bytes 49160 | tf_op jit(solution)/shard_map/ppermute | solution.py:116
  82.7 4.9 %collective-permute-start.8 = (f32[32,128]{1,0:T(8,128)S(1)}, f32[32,128]{1,0:T(8,128)S(1)}, u32[]{:S(2)}, u32[]{:S(2)}) collective-permute-start(f32[32,128]{1,0:T(8,128)S(1)} %get-tuple-element.38), channel_id=1, source_target_pairs={{0,2},{1,3},{2,0},{3,1},{4,6},{5,7},{6,4},{7,5},{8,10},{9,11},{10,... | collective-permute-start | bytes 49160 | tf_op jit(solution)/shard_map/ppermute | solution.py:116
  87.6 1.9 %collective-permute-start.9 = (f32[32,128]{1,0:T(8,128)S(1)}, f32[32,128]{1,0:T(8,128)S(1)}, u32[]{:S(2)}, u32[]{:S(2)}) collective-permute-start(f32[32,128]{1,0:T(8,128)S(1)} %get-tuple-element.37), channel_id=1, source_target_pairs={{0,1},{1,2},{2,3},{3,0},{4,5},{5,6},{6,7},{7,4},{8,9},{9,10},{10,1... | collective-permute-start | bytes 49160 | tf_op jit(solution)/shard_map/ppermute | solution.py:116
  89.6 3.7 %collective-permute-done.9 = f32[32,128]{1,0:T(8,128)S(1)} collective-permute-done((f32[32,128]{1,0:T(8,128)S(1)}, f32[32,128]{1,0:T(8,128)S(1)}, u32[]{:S(2)}, u32[]{:S(2)}) %collective-permute-start.9) | collective-permute-done | bytes 16416 | tf_op jit(solution)/shard_map/ppermute | solution.py:116
  (69 shorter events, 17.7 us)
Async XLA Ops:
  0.6 3.2 %copy-start = (f32[64,20,128]{2,0,1:T(8,128)S(1)}, f32[64,20,128]{2,0,1:T(8,128)}, u32[]{:S(2)}) copy-start(f32[64,20,128]{2,0,1:T(8,128)} %param.11) | copy-start | bytes 1966084
  0.6 3.2 %copy-start.4 = (f32[64,20,128]{2,0,1:T(8,128)S(1)}, f32[64,20,128]{2,0,1:T(8,128)}, u32[]{:S(2)}) copy-start(f32[64,20,128]{2,0,1:T(8,128)} %param.12) | copy-start | bytes 1966084
  5.1 4.9 %copy-start.7 = (s32[64]{0:T(128)S(1)}, s32[64]{0:T(128)}, u32[]{:S(2)}) copy-start(s32[64]{0:T(128)} %param.17) | copy-start | bytes 772
  5.1 19.2 %copy-start.1 = (f32[50,16,128]{2,1,0:T(8,128)S(1)}, f32[50,16,128]{2,1,0:T(8,128)}, u32[]{:S(2)}) copy-start(f32[50,16,128]{2,1,0:T(8,128)} %param.14) | copy-start | bytes 1228804
  5.1 19.4 %copy-start.3 = (f32[50,16,128]{2,1,0:T(8,128)S(1)}, f32[50,16,128]{2,1,0:T(8,128)}, u32[]{:S(2)}) copy-start(f32[50,16,128]{2,1,0:T(8,128)} %param.15) | copy-start | bytes 1228804
  10.4 9.5 %collective-permute-start = (f32[33,128]{1,0:T(8,128)S(1)}, f32[33,128]{1,0:T(8,128)S(1)}, u32[]{:S(2)}, u32[]{:S(2)}) collective-permute-start(f32[33,128]{1,0:T(8,128)S(1)} %get-tuple-element.35), channel_id=1, source_target_pairs={{0,3},{1,0},{2,1},{3,2},{4,7},{5,4},{6,5},{7,6},{8,11},{9,8},{10,9... | collective-permute-start | bytes 50696 | tf_op jit(solution)/shard_map/ppermute | solution.py:116
  14.8 6.0 %collective-permute-start.1 = (f32[33,128]{1,0:T(8,128)S(1)}, f32[33,128]{1,0:T(8,128)S(1)}, u32[]{:S(2)}, u32[]{:S(2)}) collective-permute-start(f32[33,128]{1,0:T(8,128)S(1)} %get-tuple-element.36), channel_id=1, source_target_pairs={{0,2},{1,3},{2,0},{3,1},{4,6},{5,7},{6,4},{7,5},{8,10},{9,11},{10,... | collective-permute-start | bytes 50696 | tf_op jit(solution)/shard_map/ppermute | solution.py:116
  17.2 5.7 %collective-permute-start.2 = (f32[33,128]{1,0:T(8,128)S(1)}, f32[33,128]{1,0:T(8,128)S(1)}, u32[]{:S(2)}, u32[]{:S(2)}) collective-permute-start(f32[33,128]{1,0:T(8,128)S(1)} %get-tuple-element.34), channel_id=1, source_target_pairs={{0,1},{1,2},{2,3},{3,0},{4,5},{5,6},{6,7},{7,4},{8,9},{9,10},{10,1... | collective-permute-start | bytes 50696 | tf_op jit(solution)/shard_map/ppermute | solution.py:116
  24.5 11.6 %collective-permute-start.3 = (f32[100,6,128]{2,1,0:T(8,128)S(1)}, f32[100,6,128]{2,1,0:T(8,128)S(1)}, u32[]{:S(2)}, u32[]{:S(2)}) collective-permute-start(f32[100,6,128]{2,1,0:T(8,128)S(1)} %get-tuple-element.25), channel_id=1, source_target_pairs={{0,4},{4,8},{8,12},{12,16},{16,20},{20,24},{24,28},{28,32},{32,36}... | collective-permute-start | bytes 921608 | tf_op jit(solution)/shard_map/ppermute | solution.py:25
  31.2 12.6 %collective-permute-start.4 = (f32[100,6,128]{2,1,0:T(8,128)S(1)}, f32[100,6,128]{2,1,0:T(8,128)S(1)}, u32[]{:S(2)}, u32[]{:S(2)}) collective-permute-start(f32[100,6,128]{2,1,0:T(8,128)S(1)} %get-tuple-element.26), channel_id=1, source_target_pairs={{4,0},{8,4},{12,8},{16,12},{20,16},{24,20},{28,24},{32,28},{36,32}... | collective-permute-start | bytes 921608 | tf_op jit(solution)/shard_map/ppermute | solution.py:27
  45.9 3.1 %collective-permute-start.5 = (f32[6,3200]{1,0:T(8,128)S(1)}, f32[6,3200]{1,0:T(8,128)S(1)}, u32[]{:S(2)}, u32[]{:S(2)}) collective-permute-start(f32[6,3200]{1,0:T(8,128)S(1)} %fusion.174), channel_id=1, source_target_pairs={{0,1},{1,2},{2,3},{4,5},{5,6},{6,7},{8,9},{9,10},{10,11},{12,13},{... | collective-permute-start | bytes 230408 | tf_op jit(solution)/shard_map/ppermute | solution.py:179
  47.2 5.5 %collective-permute-start.6 = (f32[6,3200]{1,0:T(8,128)S(1)}, f32[6,3200]{1,0:T(8,128)S(1)}, u32[]{:S(2)}, u32[]{:S(2)}) collective-permute-start(f32[6,3200]{1,0:T(8,128)S(1)} %fusion.175), channel_id=1, source_target_pairs={{1,0},{2,1},{3,2},{5,4},{6,5},{7,6},{9,8},{10,9},{11,10},{13,12},{... | collective-permute-start | bytes 230408 | tf_op jit(solution)/shard_map/ppermute | solution.py:180
  80.1 14.4 %copy-start.5 = (f32[50,16,128]{2,1,0:T(8,128)}, f32[50,16,128]{2,1,0:T(8,128)S(1)}, u32[]{:S(2)}) copy-start(f32[50,16,128]{2,1,0:T(8,128)S(1)} %fusion.101) | copy-start | bytes 1228804
  80.1 13.2 %copy-start.2 = (f32[64,2560]{1,0:T(8,128)S(1)}, f32[64,2560]{1,0:T(8,128)}, u32[]{:S(2)}) copy-start(f32[64,2560]{1,0:T(8,128)} %shard_map.112) | copy-start | bytes 1966084
  80.1 13.5 %slice-start = ((f32[64,2560]{1,0:T(8,128)}), f32[64,2432]{1,0:T(8,128)S(1)}, s32[]{:S(2)}) async-start(f32[64,2560]{1,0:T(8,128)} %shard_map.112), calls=%async_computation | async-start | bytes 1245184 | tf_op jit(solution)/shard_map/slice | solution.py:221
  80.4 9.2 %collective-permute-start.7 = (f32[32,128]{1,0:T(8,128)S(1)}, f32[32,128]{1,0:T(8,128)S(1)}, u32[]{:S(2)}, u32[]{:S(2)}) collective-permute-start(f32[32,128]{1,0:T(8,128)S(1)} %get-tuple-element.39), channel_id=1, source_target_pairs={{0,3},{1,0},{2,1},{3,2},{4,7},{5,4},{6,5},{7,6},{8,11},{9,8},{10,9... | collective-permute-start | bytes 49160 | tf_op jit(solution)/shard_map/ppermute | solution.py:116
  82.7 6.9 %collective-permute-start.8 = (f32[32,128]{1,0:T(8,128)S(1)}, f32[32,128]{1,0:T(8,128)S(1)}, u32[]{:S(2)}, u32[]{:S(2)}) collective-permute-start(f32[32,128]{1,0:T(8,128)S(1)} %get-tuple-element.38), channel_id=1, source_target_pairs={{0,2},{1,3},{2,0},{3,1},{4,6},{5,7},{6,4},{7,5},{8,10},{9,11},{10,... | collective-permute-start | bytes 49160 | tf_op jit(solution)/shard_map/ppermute | solution.py:116
  87.6 5.7 %collective-permute-start.9 = (f32[32,128]{1,0:T(8,128)S(1)}, f32[32,128]{1,0:T(8,128)S(1)}, u32[]{:S(2)}, u32[]{:S(2)}) collective-permute-start(f32[32,128]{1,0:T(8,128)S(1)} %get-tuple-element.37), channel_id=1, source_target_pairs={{0,1},{1,2},{2,3},{3,0},{4,5},{5,6},{6,7},{7,4},{8,9},{9,10},{10,1... | collective-permute-start | bytes 49160 | tf_op jit(solution)/shard_map/ppermute | solution.py:116
  89.5 5.0 %copy-start.6 = (s32[64]{0:T(128)S(1)}, s32[64]{0:T(128)}, u32[]{:S(2)}) copy-start(s32[64]{0:T(128)} %param.18) | copy-start | bytes 772

commit v7 on v5

--- a/solution.py
+++ b/solution.py
@@ -32,54 +32,49 @@
 
 
 def column_kernel(moist_ref, diff_ref, rain_ref, wet_ref, ratio_ref):
-    lanes = rain_ref.shape[1]
-    depth = moist_ref.shape[1] // lanes
+    depth = moist_ref.shape[0]
     group = 8
-
-    def layer(ref, rows, k):
-        return ref[rows, k * lanes : (k + 1) * lanes]
 
     def body(g, carry):
         rows = pl.ds(pl.multiple_of(g * group, group), group)
         ratio = None
         carried = None
         for layer_k in range(depth):
-            lower_coef = layer(diff_ref, rows, layer_k)
-            source = layer(moist_ref, rows, layer_k)
+            lower_coef = diff_ref[layer_k, rows, :]
+            source = moist_ref[layer_k, rows, :]
             if layer_k == 0:
                 source = source + rain_ref[rows, :]
                 pivot = 1.0 + lower_coef
                 carried = source / pivot
             else:
-                upper_coef = layer(diff_ref, rows, layer_k - 1)
+                upper_coef = diff_ref[layer_k - 1, rows, :]
                 pivot = 1.0 + lower_coef + upper_coef - upper_coef * ratio
                 carried = (source + upper_coef * carried) / pivot
             ratio = lower_coef / pivot
-            ratio_ref[rows, layer_k * lanes : (layer_k + 1) * lanes] = ratio
-            wet_ref[rows, layer_k * lanes : (layer_k + 1) * lanes] = carried
+            ratio_ref[layer_k, rows, :] = ratio
+            wet_ref[layer_k, rows, :] = carried
         solved = carried
         for layer_k in range(depth - 2, -1, -1):
-            solved = layer(wet_ref, rows, layer_k) + layer(ratio_ref, rows, layer_k) * solved
-            wet_ref[rows, layer_k * lanes : (layer_k + 1) * lanes] = solved
+            solved = wet_ref[layer_k, rows, :] + ratio_ref[layer_k, rows, :] * solved
+            wet_ref[layer_k, rows, :] = solved
         return carry
 
-    lax.fori_loop(0, moist_ref.shape[0] // group, body, 0)
+    lax.fori_loop(0, moist_ref.shape[1] // group, body, 0)
 
 
 def column_solve(moisture, diffusivity, rain):
     blocks, depth, lanes = moisture.shape
-    flat = (blocks, depth * lanes)
-    wet = pl.pallas_call(
+    layered = (depth, blocks, lanes)
+    return pl.pallas_call(
         column_kernel,
-        out_shape=jax.ShapeDtypeStruct(flat, jnp.float32),
+        out_shape=jax.ShapeDtypeStruct(layered, jnp.float32),
         in_specs=[pl.BlockSpec(memory_space=pltpu.VMEM)] * 3,
         out_specs=pl.BlockSpec(memory_space=pltpu.VMEM),
-        scratch_shapes=[pltpu.VMEM(flat, jnp.float32)],
+        scratch_shapes=[pltpu.VMEM(layered, jnp.float32)],
         cost_estimate=pl.CostEstimate(
             flops=12 * blocks * depth * lanes, transcendentals=0, bytes_accessed=12 * blocks * depth * lanes
         ),
-    )(moisture.reshape(flat), diffusivity.reshape(flat), rain)
-    return wet
+    )(jnp.transpose(moisture, (1, 0, 2)), jnp.transpose(diffusivity, (1, 0, 2)), rain)
 
 
 def lateral_core(padded_head, padded_cond):
@@ -114,7 +109,7 @@
     tile_cols = head.shape[2]
     wet = column_solve(moisture, diffusivity, rain)
     depth = moisture.shape[1]
-    bottom = wet[:, (depth - 1) * tile_cols :]
+    bottom = wet[depth - 1]
     drain = diffusivity[:, -1, :] * bottom
     in_use = jnp.arange(block_count, dtype=jnp.int32) < counts[0]
     in_use_f = in_use.astype(jnp.float32)
@@ -198,9 +193,7 @@
     returned = lax.all_to_all(answered, "gy", split_axis=0, concat_axis=0, tiled=True)
     saturation = jnp.einsum("tcb,tcj->bj", placing, returned, precision=highest)
     new_bottom = bottom + capillary * (saturation - in_use_f[:, None] * bottom)
-    moisture_out = jnp.concatenate(
-        [wet[:, : (depth - 1) * tile_cols], new_bottom], axis=1
-    ).reshape(moisture.shape)
+    moisture_out = jnp.transpose(jnp.concatenate([wet[: depth - 1], new_bottom[None]]), (1, 0, 2))
     patch_hot = (patch_ids[None, :] == jnp.arange(PATCH_DEV, dtype=jnp.int32)[:, None]).astype(
         jnp.float32
     )

time: 87.1 us -> 85.8 us (0.985)
  local copies, waits for them, and re-layouts: 1.78 us -> 0.57 us
    reshape x1 -> x0, local copies, waits for them, and re-layouts: 1.2 us -> none  [column_solve(): diffusivity.reshape(flat)]
    unnamed x1 -> x0, other arithmetic: 0.91 us -> none
    transpose x0 -> x1, other arithmetic: none -> 0.88 us  [local(): jnp.transpose(jnp.concatenate([wet[:depth - 1], new_bottom[None]]), (1, 0...]
where the time goes in v7:
time: 85.8 us; the launch traced here: 85.3 us
  other arithmetic  29.5 us (34%)
  waiting for transfers between devices  23.2 us (27%)
  starting transfers between devices  19.1 us (22%)
  matrix products  7.41 us (9%)
  Pallas kernels  3.95 us (5%)
  between operations  1.61 us (2%)
    select_n x5, other arithmetic, local(): field = jnp.where(inside[None, edge:-edge, edge:-edge], field, 0.0)  16.4 us
    ppermute x1, waiting for transfers between devices, with_halo(): lax.ppermute(head, axis, [((i + 1) % count, i) for i in range(ends)])  7.72 us
    mul x6, other arithmetic, lateral_core(): 0.5 * (centre_cond[1:] + centre_cond[:-1]) * (centre[1:] - centre[:-1])  7.6 us
    ppermute x1, starting transfers between devices, with_halo(): lax.ppermute(tail, axis, [(i, (i + 1) % count) for i in range(ends)])  6.4 us
    all_to_all x1, waiting for transfers between devices, local(): lax.all_to_all(packed, 'gy', split_axis=0, concat_axis=0, tiled=True)  4.53 us
    all_to_all x1, waiting for transfers between devices, local(): lax.all_to_all(answered, 'gy', split_axis=0, concat_axis=0, tiled=True)  4.43 us
    all_to_all x1, starting transfers between devices, local(): lax.all_to_all(packed, 'gy', split_axis=0, concat_axis=0, tiled=True)  4.01 us
    pallas_call x1, Pallas kernels, column_solve(): pl.pallas_call(column_kernel, out_shape=jax.ShapeDtypeStruct(layered, jnp...  3.95 us
  transfers between devices with their start and end apart: 6, of which 5 were waited for; matrix products, arithmetic and copies ran while one was open for 1% of the time, Pallas kernels for 0%

profile of v7, /device:TPU:249, one launch (start us, length us, event | category | flops | bytes accessed | tf_op | source)
XLA Modules:
  0.0 85.3 jit_solution(6774416366107996974)
XLA Ops:
  3.7 3.9 %shard_map.112 = f32[20,64,128]{2,1,0:T(8,128)} custom-call(f32[20,64,128]{2,1,0:T(8,128)} %bitcast.70, f32[20,64,128]{2,1,0:T(8,128)} %bitcast.69, f32[64,128]{1,0:T(8,128)} %rain_ref.1), custom_call_target="tpu_custom_call" | custom-call | flops 1966080 | bytes 1966080 | tf_op jit(solution)/shard_map/pallas_call | solution.py:68
  9.7 4.0 %all-to-all-start = ((f32[4,33,128]{2,1,0:T(8,128)}), f32[4,33,128]{2,1,0:T(8,128)S(1)}, u32[]{:S(2)}, u32[]{:S(2)}) async-start(f32[4,33,128]{2,1,0:T(8,128)} %pad_maximum_fusion.1), calls=%async_computation | async-start | bytes 163840 | tf_op jit(solution)/shard_map/all_to_all | solution.py:130
  13.7 4.5 %all-to-all-done = f32[4,33,128]{2,1,0:T(8,128)S(1)} async-done(((f32[4,33,128]{2,1,0:T(8,128)}), f32[4,33,128]{2,1,0:T(8,128)S(1)}, u32[]{:S(2)}, u32[]{:S(2)}) %all-to-all-start) | async-done | bytes 67616 | tf_op jit(solution)/shard_map/all_to_all | solution.py:130
  18.6 6.4 %collective-permute-start = (f32[100,6,128]{2,1,0:T(8,128)S(1)}, f32[100,6,128]{2,1,0:T(8,128)S(1)}, u32[]{:S(2)}, u32[]{:S(2)}) collective-permute-start(f32[100,6,128]{2,1,0:T(8,128)S(1)} %get-tuple-element.15), channel_id=1, source_target_pairs={{0,4},{4,8},{8,12},{12,16},{16,20},{20,24},{24,28},{28,32},{32,36}... | collective-permute-start | bytes 921608 | tf_op jit(solution)/shard_map/ppermute | solution.py:25
  25.0 1.9 %collective-permute-start.1 = (f32[100,6,128]{2,1,0:T(8,128)S(1)}, f32[100,6,128]{2,1,0:T(8,128)S(1)}, u32[]{:S(2)}, u32[]{:S(2)}) collective-permute-start(f32[100,6,128]{2,1,0:T(8,128)S(1)} %get-tuple-element.16), channel_id=1, source_target_pairs={{4,0},{8,4},{12,8},{16,12},{20,16},{24,20},{28,24},{32,28},{36,32}... | collective-permute-start | bytes 921608 | tf_op jit(solution)/shard_map/ppermute | solution.py:27
  27.0 2.9 %collective-permute-done = f32[100,6,128]{2,1,0:T(8,128)S(1)} collective-permute-done((f32[100,6,128]{2,1,0:T(8,128)S(1)}, f32[100,6,128]{2,1,0:T(8,128)S(1)}, u32[]{:S(2)}, u32[]{:S(2)}) %collective-permute-start) | collective-permute-done | bytes 307232 | tf_op jit(solution)/shard_map/ppermute | solution.py:25
  29.9 7.7 %collective-permute-done.1 = f32[100,6,128]{2,1,0:T(8,128)S(1)} collective-permute-done((f32[100,6,128]{2,1,0:T(8,128)S(1)}, f32[100,6,128]{2,1,0:T(8,128)S(1)}, u32[]{:S(2)}, u32[]{:S(2)}) %collective-permute-start.1) | collective-permute-done | bytes 307232 | tf_op jit(solution)/shard_map/ppermute | solution.py:27
  39.6 2.2 %collective-permute-start.2 = (f32[6,3200]{1,0:T(8,128)S(1)}, f32[6,3200]{1,0:T(8,128)S(1)}, u32[]{:S(2)}, u32[]{:S(2)}) collective-permute-start(f32[6,3200]{1,0:T(8,128)S(1)} %fusion.146), channel_id=1, source_target_pairs={{0,1},{1,2},{2,3},{4,5},{5,6},{6,7},{8,9},{9,10},{10,11},{12,13},{... | collective-permute-start | bytes 230408 | tf_op jit(solution)/shard_map/ppermute | solution.py:155
  41.9 1.3 %collective-permute-start.3 = (f32[6,3200]{1,0:T(8,128)S(1)}, f32[6,3200]{1,0:T(8,128)S(1)}, u32[]{:S(2)}, u32[]{:S(2)}) collective-permute-start(f32[6,3200]{1,0:T(8,128)S(1)} %fusion.147), channel_id=1, source_target_pairs={{1,0},{2,1},{3,2},{5,4},{6,5},{7,6},{9,8},{10,9},{11,10},{13,12},{... | collective-permute-start | bytes 230408 | tf_op jit(solution)/shard_map/ppermute | solution.py:156
  43.6 3.6 %collective-permute-done.3 = f32[6,3200]{1,0:T(8,128)S(1)} collective-permute-done((f32[6,3200]{1,0:T(8,128)S(1)}, f32[6,3200]{1,0:T(8,128)S(1)}, u32[]{:S(2)}, u32[]{:S(2)}) %collective-permute-start.3) | collective-permute-done | bytes 76832 | tf_op jit(solution)/shard_map/ppermute | solution.py:156
  47.3 2.3 %pad_add_fusion = f32[3200,140]{1,0:T(8,128)S(1)} fusion(f32[3200,128]{1,0:T(8,128)S(1)} %bitcast.68, f32[6,3200]{1,0:T(8,128)S(1)} %collective-permute-done.3, f32[6,3200]{1,0:T(8,128)S(1)} %collective-permute-done.2, pred[6,140]{1,0:T(8,128)(4,1)S(1)} %get-tuple-element.19, pred[6,140]{1,0:T(8,128)(4,1)S(1)} %get-tuple-element.20), kind=kOutput, calls=%fused_computation | convolution fusion | flops 65000080 | bytes 3585680 | tf_op jit(solution)/shard_map/dot_general | solution.py:159
  49.6 1.8 %fusion.19 = f32[49,26,138]{2,1,0:T(8,128)S(1)} fusion(f32[100,32,140]{2,1,0:T(8,128)S(1)} %bitcast.54), kind=kLoop, calls=%fused_computation.32 | loop fusion | flops 703248 | bytes 3516240 | tf_op jit(solution)/shard_map/mul | solution.py:94
  51.4 3.8 %fusion.6 = f32[50,26,138]{2,1,0:T(8,128)S(1)} fusion(f32[100,32,140]{2,1,0:T(8,128)S(1)} %bitcast.55, f32[49,26,138]{2,1,0:T(8,128)S(1)} %fusion.19, pred[26,138]{1,0:T(8,128)(4,1)S(1)} %slice.484), kind=kLoop, calls=%fused_computation.8 | loop fusion | flops 4305600 | bytes 8600436 | tf_op jit(solution)/shard_map/jit(_where)/select_n | solution.py:188
  55.2 1.3 %fusion.91 = f32[49,24,136]{2,1,0:T(8,128)S(1)} fusion(f32[50,26,138]{2,1,0:T(8,128)S(1)} %fusion.6, f32[100,32,140]{2,1,0:T(8,128)S(1)} %bitcast.56), kind=kLoop, calls=%fused_computation.144 | loop fusion | flops 639744 | bytes 3198720 | tf_op jit(solution)/shard_map/mul | solution.py:94
  56.5 3.1 %fusion.75 = f32[50,24,136]{2,1,0:T(8,128)S(1)} fusion(f32[50,26,138]{2,1,0:T(8,128)S(1)} %fusion.6, f32[100,32,140]{2,1,0:T(8,128)S(1)} %bitcast.57, f32[49,24,136]{2,1,0:T(8,128)S(1)} %fusion.91, pred[24,136]{1,0:T(8,128)(4,1)S(1)} %slice.483), kind=kLoop, calls=%fused_computation.114 | loop fusion | flops 3916800 | bytes 7823808 | tf_op jit(solution)/shard_map/jit(_where)/select_n | solution.py:188
  59.6 1.3 %fusion.89 = f32[49,22,134]{2,1,0:T(8,128)S(1)} fusion(f32[50,24,136]{2,1,0:T(8,128)S(1)} %fusion.75, f32[100,32,140]{2,1,0:T(8,128)S(1)} %bitcast.58), kind=kLoop, calls=%fused_computation.140 | loop fusion | flops 577808 | bytes 2889040 | tf_op jit(solution)/shard_map/mul | solution.py:94
  60.9 3.1 %fusion.59 = f32[50,22,134]{2,1,0:T(8,128)S(1)} fusion(f32[50,24,136]{2,1,0:T(8,128)S(1)} %fusion.75, f32[100,32,140]{2,1,0:T(8,128)S(1)} %bitcast.59, f32[49,22,134]{2,1,0:T(8,128)S(1)} %fusion.89, pred[22,134]{1,0:T(8,128)(4,1)S(1)} %slice.482), kind=kLoop, calls=%fused_computation.90 | loop fusion | flops 3537600 | bytes 7066356 | tf_op jit(solution)/shard_map/jit(_where)/select_n | solution.py:188
  64.1 1.3 %fusion.87 = f32[49,20,132]{2,1,0:T(8,128)S(1)} fusion(f32[50,22,134]{2,1,0:T(8,128)S(1)} %fusion.59, f32[100,32,140]{2,1,0:T(8,128)S(1)} %bitcast.60), kind=kLoop, calls=%fused_computation.136 | loop fusion | flops 517440 | bytes 2587200 | tf_op jit(solution)/shard_map/mul | solution.py:94
  65.4 3.1 %fusion.43 = f32[50,20,132]{2,1,0:T(8,128)S(1)} fusion(f32[50,22,134]{2,1,0:T(8,128)S(1)} %fusion.59, f32[100,32,140]{2,1,0:T(8,128)S(1)} %bitcast.61, f32[49,20,132]{2,1,0:T(8,128)S(1)} %fusion.87, pred[20,132]{1,0:T(8,128)(4,1)S(1)} %slice.481), kind=kLoop, calls=%fused_computation.66 | loop fusion | flops 3168000 | bytes 6328080 | tf_op jit(solution)/shard_map/jit(_where)/select_n | solution.py:188
  68.5 1.3 %fusion.85 = f32[49,18,130]{2,1,0:T(8,128)S(1)} fusion(f32[50,20,132]{2,1,0:T(8,128)S(1)} %fusion.43, f32[100,32,140]{2,1,0:T(8,128)S(1)} %bitcast.62), kind=kLoop, calls=%fused_computation.132 | loop fusion | flops 458640 | bytes 2293200 | tf_op jit(solution)/shard_map/mul | solution.py:94
  69.9 3.3 %fusion.27 = f32[50,18,130]{2,1,0:T(8,128)S(1)} fusion(f32[50,20,132]{2,1,0:T(8,128)S(1)} %fusion.43, f32[100,32,140]{2,1,0:T(8,128)S(1)} %bitcast.63, f32[49,18,130]{2,1,0:T(8,128)S(1)} %fusion.85, pred[18,130]{1,0:T(8,128)(4,1)S(1)} %slice.480), kind=kLoop, calls=%fused_computation.42 | loop fusion | flops 2808000 | bytes 5608980 | tf_op jit(solution)/shard_map/jit(_where)/select_n | solution.py:188
  73.6 1.0 %fusion.101 = f32[50,16,128]{2,1,0:T(8,128)S(1)} fusion(f32[50,18,130]{2,1,0:T(8,128)S(1)} %fusion.27, f32[100,32,140]{2,1,0:T(8,128)S(1)} %bitcast.65, f32[49,16,128]{2,1,0:T(8,128)S(1)} %fusion.111), kind=kLoop, calls=%fused_computation.161 | loop fusion | flops 2355200 | bytes 4907008 | tf_op jit(solution)/shard_map/add | solution.py:100
  75.6 3.3 %all-to-all-start.1 = ((f32[4,32,128]{2,1,0:T(8,128)}), f32[4,32,128]{2,1,0:T(8,128)S(1)}, u32[]{:S(2)}, u32[]{:S(2)}) async-start(f32[4,32,128]{2,1,0:T(8,128)} %fusion.138), calls=%async_computation.1 | async-start | bytes 131072 | tf_op jit(solution)/shard_map/all_to_all | solution.py:193
  78.9 4.4 %all-to-all-done.1 = f32[4,32,128]{2,1,0:T(8,128)S(1)} async-done(((f32[4,32,128]{2,1,0:T(8,128)}), f32[4,32,128]{2,1,0:T(8,128)S(1)}, u32[]{:S(2)}, u32[]{:S(2)}) %all-to-all-start.1) | async-done | bytes 65568 | tf_op jit(solution)/shard_map/all_to_all | solution.py:193
  (52 shorter events, 10.6 us)
Async XLA Ops:
  0.6 8.0 %copy-start.5 = (s32[64]{0:T(128)S(1)}, s32[64]{0:T(128)}, u32[]{:S(2)}) copy-start(s32[64]{0:T(128)} %param.17) | copy-start | bytes 772
  3.7 14.7 %copy-start = (f32[50,16,128]{2,1,0:T(8,128)S(1)}, f32[50,16,128]{2,1,0:T(8,128)}, u32[]{:S(2)}) copy-start(f32[50,16,128]{2,1,0:T(8,128)} %param.14) | copy-start | bytes 1228804
  3.7 14.8 %copy-start.2 = (f32[50,16,128]{2,1,0:T(8,128)S(1)}, f32[50,16,128]{2,1,0:T(8,128)}, u32[]{:S(2)}) copy-start(f32[50,16,128]{2,1,0:T(8,128)} %param.15) | copy-start | bytes 1228804
  9.7 8.6 %all-to-all-start = ((f32[4,33,128]{2,1,0:T(8,128)}), f32[4,33,128]{2,1,0:T(8,128)S(1)}, u32[]{:S(2)}, u32[]{:S(2)}) async-start(f32[4,33,128]{2,1,0:T(8,128)} %pad_maximum_fusion.1), calls=%async_computation | async-start | bytes 163840 | tf_op jit(solution)/shard_map/all_to_all | solution.py:130
  18.6 11.3 %collective-permute-start = (f32[100,6,128]{2,1,0:T(8,128)S(1)}, f32[100,6,128]{2,1,0:T(8,128)S(1)}, u32[]{:S(2)}, u32[]{:S(2)}) collective-permute-start(f32[100,6,128]{2,1,0:T(8,128)S(1)} %get-tuple-element.15), channel_id=1, source_target_pairs={{0,4},{4,8},{8,12},{12,16},{16,20},{20,24},{24,28},{28,32},{32,36}... | collective-permute-start | bytes 921608 | tf_op jit(solution)/shard_map/ppermute | solution.py:25
  25.0 12.6 %collective-permute-start.1 = (f32[100,6,128]{2,1,0:T(8,128)S(1)}, f32[100,6,128]{2,1,0:T(8,128)S(1)}, u32[]{:S(2)}, u32[]{:S(2)}) collective-permute-start(f32[100,6,128]{2,1,0:T(8,128)S(1)} %get-tuple-element.16), channel_id=1, source_target_pairs={{4,0},{8,4},{12,8},{16,12},{20,16},{24,20},{28,24},{32,28},{36,32}... | collective-permute-start | bytes 921608 | tf_op jit(solution)/shard_map/ppermute | solution.py:27
  39.6 4.0 %collective-permute-start.2 = (f32[6,3200]{1,0:T(8,128)S(1)}, f32[6,3200]{1,0:T(8,128)S(1)}, u32[]{:S(2)}, u32[]{:S(2)}) collective-permute-start(f32[6,3200]{1,0:T(8,128)S(1)} %fusion.146), channel_id=1, source_target_pairs={{0,1},{1,2},{2,3},{4,5},{5,6},{6,7},{8,9},{9,10},{10,11},{12,13},{... | collective-permute-start | bytes 230408 | tf_op jit(solution)/shard_map/ppermute | solution.py:155
  41.9 5.4 %collective-permute-start.3 = (f32[6,3200]{1,0:T(8,128)S(1)}, f32[6,3200]{1,0:T(8,128)S(1)}, u32[]{:S(2)}, u32[]{:S(2)}) collective-permute-start(f32[6,3200]{1,0:T(8,128)S(1)} %fusion.147), channel_id=1, source_target_pairs={{1,0},{2,1},{3,2},{5,4},{6,5},{7,6},{9,8},{10,9},{11,10},{13,12},{... | collective-permute-start | bytes 230408 | tf_op jit(solution)/shard_map/ppermute | solution.py:156
  74.7 10.6 %copy-start.3 = (f32[50,16,128]{2,1,0:T(8,128)}, f32[50,16,128]{2,1,0:T(8,128)S(1)}, u32[]{:S(2)}) copy-start(f32[50,16,128]{2,1,0:T(8,128)S(1)} %fusion.101) | copy-start | bytes 1228804
  74.7 8.9 %copy-start.1 = (f32[20,64,128]{2,1,0:T(8,128)S(1)}, f32[20,64,128]{2,1,0:T(8,128)}, u32[]{:S(2)}) copy-start(f32[20,64,128]{2,1,0:T(8,128)} %shard_map.112) | copy-start | bytes 1966084
  74.7 9.0 %copy-start.4 = (s32[64]{0:T(128)S(1)}, s32[64]{0:T(128)}, u32[]{:S(2)}) copy-start(s32[64]{0:T(128)} %param.18) | copy-start | bytes 772
  74.7 9.7 %slice-start = ((f32[20,64,128]{2,1,0:T(8,128)}), f32[19,64,128]{2,1,0:T(8,128)S(1)}, s32[]{:S(2)}) async-start(f32[20,64,128]{2,1,0:T(8,128)} %shard_map.112), calls=%async_computation.2 | async-start | bytes 1245184 | tf_op jit(solution)/shard_map/slice | solution.py:196
  75.6 7.7 %all-to-all-start.1 = ((f32[4,32,128]{2,1,0:T(8,128)}), f32[4,32,128]{2,1,0:T(8,128)S(1)}, u32[]{:S(2)}, u32[]{:S(2)}) async-start(f32[4,32,128]{2,1,0:T(8,128)} %fusion.138), calls=%async_computation.1 | async-start | bytes 131072 | tf_op jit(solution)/shard_map/all_to_all | solution.py:193

commit v8 on v7

--- a/solution.py
+++ b/solution.py
@@ -33,10 +33,9 @@
 
 def column_kernel(moist_ref, diff_ref, rain_ref, wet_ref, ratio_ref):
     depth = moist_ref.shape[0]
-    group = 8
 
     def body(g, carry):
-        rows = pl.ds(pl.multiple_of(g * group, group), group)
+        rows = pl.ds(0, moist_ref.shape[1])
         ratio = None
         carried = None
         for layer_k in range(depth):
@@ -59,7 +58,7 @@
             wet_ref[layer_k, rows, :] = solved
         return carry
 
-    lax.fori_loop(0, moist_ref.shape[1] // group, body, 0)
+    body(0, 0)
 
 
 def column_solve(moisture, diffusivity, rain):

time: 85.8 us -> 84.4 us (0.984)
  Pallas kernels: 3.95 us -> 2.48 us
    pallas_call x1, Pallas kernels: 3.95 us -> 2.48 us  [column_solve(): pl.pallas_call(column_kernel, out_shape=jax.ShapeDtypeStruct(layered, jnp...]
where the time goes in v8:
time: 84.4 us; the launch traced here: 83.8 us
  other arithmetic  29.5 us (35%)
  waiting for transfers between devices  23.2 us (27%)
  starting transfers between devices  19.1 us (23%)
  matrix products  7.41 us (9%)
  Pallas kernels  2.48 us (3%)
  between operations  1.61 us (2%)
    select_n x5, other arithmetic, local(): field = jnp.where(inside[None, edge:-edge, edge:-edge], field, 0.0)  16.4 us
    ppermute x1, waiting for transfers between devices, with_halo(): lax.ppermute(head, axis, [((i + 1) % count, i) for i in range(ends)])  7.72 us
    mul x6, other arithmetic, lateral_core(): 0.5 * (centre_cond[1:] + centre_cond[:-1]) * (centre[1:] - centre[:-1])  7.6 us
    ppermute x1, starting transfers between devices, with_halo(): lax.ppermute(tail, axis, [(i, (i + 1) % count) for i in range(ends)])  6.41 us
    all_to_all x1, waiting for transfers between devices, local(): lax.all_to_all(packed, 'gy', split_axis=0, concat_axis=0, tiled=True)  4.53 us
    all_to_all x1, waiting for transfers between devices, local(): lax.all_to_all(answered, 'gy', split_axis=0, concat_axis=0, tiled=True)  4.43 us
    all_to_all x1, starting transfers between devices, local(): lax.all_to_all(packed, 'gy', split_axis=0, concat_axis=0, tiled=True)  4.01 us
    ppermute x1, waiting for transfers between devices, local(): lax.ppermute(left_strip, 'gy', [(i + 1, i) for i in range(ends)])  3.62 us
  transfers between devices with their start and end apart: 6, of which 5 were waited for; matrix products, arithmetic and copies ran while one was open for 1% of the time, Pallas kernels for 0%

profile of v8, /device:TPU:249, one launch (start us, length us, event | category | flops | bytes accessed | tf_op | source)
XLA Modules:
  0.0 83.8 jit_solution(17326332004531397618)
XLA Ops:
  3.7 2.5 %shard_map.112 = f32[20,64,128]{2,1,0:T(8,128)} custom-call(f32[20,64,128]{2,1,0:T(8,128)} %bitcast.70, f32[20,64,128]{2,1,0:T(8,128)} %bitcast.69, f32[64,128]{1,0:T(8,128)} %rain_ref.1), custom_call_target="tpu_custom_call" | custom-call | flops 1966080 | bytes 1966080 | tf_op jit(solution)/shard_map/pallas_call | solution.py:67
  8.2 4.0 %all-to-all-start = ((f32[4,33,128]{2,1,0:T(8,128)}), f32[4,33,128]{2,1,0:T(8,128)S(1)}, u32[]{:S(2)}, u32[]{:S(2)}) async-start(f32[4,33,128]{2,1,0:T(8,128)} %pad_maximum_fusion.1), calls=%async_computation | async-start | bytes 163840 | tf_op jit(solution)/shard_map/all_to_all | solution.py:129
  12.2 4.5 %all-to-all-done = f32[4,33,128]{2,1,0:T(8,128)S(1)} async-done(((f32[4,33,128]{2,1,0:T(8,128)}), f32[4,33,128]{2,1,0:T(8,128)S(1)}, u32[]{:S(2)}, u32[]{:S(2)}) %all-to-all-start) | async-done | bytes 67616 | tf_op jit(solution)/shard_map/all_to_all | solution.py:129
  17.1 6.4 %collective-permute-start = (f32[100,6,128]{2,1,0:T(8,128)S(1)}, f32[100,6,128]{2,1,0:T(8,128)S(1)}, u32[]{:S(2)}, u32[]{:S(2)}) collective-permute-start(f32[100,6,128]{2,1,0:T(8,128)S(1)} %get-tuple-element.15), channel_id=1, source_target_pairs={{0,4},{4,8},{8,12},{12,16},{16,20},{20,24},{24,28},{28,32},{32,36}... | collective-permute-start | bytes 921608 | tf_op jit(solution)/shard_map/ppermute | solution.py:25
  23.5 1.9 %collective-permute-start.1 = (f32[100,6,128]{2,1,0:T(8,128)S(1)}, f32[100,6,128]{2,1,0:T(8,128)S(1)}, u32[]{:S(2)}, u32[]{:S(2)}) collective-permute-start(f32[100,6,128]{2,1,0:T(8,128)S(1)} %get-tuple-element.16), channel_id=1, source_target_pairs={{4,0},{8,4},{12,8},{16,12},{20,16},{24,20},{28,24},{32,28},{36,32}... | collective-permute-start | bytes 921608 | tf_op jit(solution)/shard_map/ppermute | solution.py:27
  25.6 2.9 %collective-permute-done = f32[100,6,128]{2,1,0:T(8,128)S(1)} collective-permute-done((f32[100,6,128]{2,1,0:T(8,128)S(1)}, f32[100,6,128]{2,1,0:T(8,128)S(1)}, u32[]{:S(2)}, u32[]{:S(2)}) %collective-permute-start) | collective-permute-done | bytes 307232 | tf_op jit(solution)/shard_map/ppermute | solution.py:25
  28.4 7.7 %collective-permute-done.1 = f32[100,6,128]{2,1,0:T(8,128)S(1)} collective-permute-done((f32[100,6,128]{2,1,0:T(8,128)S(1)}, f32[100,6,128]{2,1,0:T(8,128)S(1)}, u32[]{:S(2)}, u32[]{:S(2)}) %collective-permute-start.1) | collective-permute-done | bytes 307232 | tf_op jit(solution)/shard_map/ppermute | solution.py:27
  38.2 2.2 %collective-permute-start.2 = (f32[6,3200]{1,0:T(8,128)S(1)}, f32[6,3200]{1,0:T(8,128)S(1)}, u32[]{:S(2)}, u32[]{:S(2)}) collective-permute-start(f32[6,3200]{1,0:T(8,128)S(1)} %fusion.146), channel_id=1, source_target_pairs={{0,1},{1,2},{2,3},{4,5},{5,6},{6,7},{8,9},{9,10},{10,11},{12,13},{... | collective-permute-start | bytes 230408 | tf_op jit(solution)/shard_map/ppermute | solution.py:154
  40.4 1.3 %collective-permute-start.3 = (f32[6,3200]{1,0:T(8,128)S(1)}, f32[6,3200]{1,0:T(8,128)S(1)}, u32[]{:S(2)}, u32[]{:S(2)}) collective-permute-start(f32[6,3200]{1,0:T(8,128)S(1)} %fusion.147), channel_id=1, source_target_pairs={{1,0},{2,1},{3,2},{5,4},{6,5},{7,6},{9,8},{10,9},{11,10},{13,12},{... | collective-permute-start | bytes 230408 | tf_op jit(solution)/shard_map/ppermute | solution.py:155
  42.2 3.6 %collective-permute-done.3 = f32[6,3200]{1,0:T(8,128)S(1)} collective-permute-done((f32[6,3200]{1,0:T(8,128)S(1)}, f32[6,3200]{1,0:T(8,128)S(1)}, u32[]{:S(2)}, u32[]{:S(2)}) %collective-permute-start.3) | collective-permute-done | bytes 76832 | tf_op jit(solution)/shard_map/ppermute | solution.py:155
  45.8 2.3 %pad_add_fusion = f32[3200,140]{1,0:T(8,128)S(1)} fusion(f32[3200,128]{1,0:T(8,128)S(1)} %bitcast.68, f32[6,3200]{1,0:T(8,128)S(1)} %collective-permute-done.3, f32[6,3200]{1,0:T(8,128)S(1)} %collective-permute-done.2, pred[6,140]{1,0:T(8,128)(4,1)S(1)} %get-tuple-element.19, pred[6,140]{1,0:T(8,128)(4,1)S(1)} %get-tuple-element.20), kind=kOutput, calls=%fused_computation | convolution fusion | flops 65000080 | bytes 3585680 | tf_op jit(solution)/shard_map/dot_general | solution.py:158
  48.1 1.8 %fusion.19 = f32[49,26,138]{2,1,0:T(8,128)S(1)} fusion(f32[100,32,140]{2,1,0:T(8,128)S(1)} %bitcast.54), kind=kLoop, calls=%fused_computation.32 | loop fusion | flops 703248 | bytes 3516240 | tf_op jit(solution)/shard_map/mul | solution.py:93
  49.9 3.8 %fusion.6 = f32[50,26,138]{2,1,0:T(8,128)S(1)} fusion(f32[100,32,140]{2,1,0:T(8,128)S(1)} %bitcast.55, f32[49,26,138]{2,1,0:T(8,128)S(1)} %fusion.19, pred[26,138]{1,0:T(8,128)(4,1)S(1)} %slice.484), kind=kLoop, calls=%fused_computation.8 | loop fusion | flops 4305600 | bytes 8600436 | tf_op jit(solution)/shard_map/jit(_where)/select_n | solution.py:187
  53.7 1.3 %fusion.91 = f32[49,24,136]{2,1,0:T(8,128)S(1)} fusion(f32[50,26,138]{2,1,0:T(8,128)S(1)} %fusion.6, f32[100,32,140]{2,1,0:T(8,128)S(1)} %bitcast.56), kind=kLoop, calls=%fused_computation.144 | loop fusion | flops 639744 | bytes 3198720 | tf_op jit(solution)/shard_map/mul | solution.py:93
  55.1 3.1 %fusion.75 = f32[50,24,136]{2,1,0:T(8,128)S(1)} fusion(f32[50,26,138]{2,1,0:T(8,128)S(1)} %fusion.6, f32[100,32,140]{2,1,0:T(8,128)S(1)} %bitcast.57, f32[49,24,136]{2,1,0:T(8,128)S(1)} %fusion.91, pred[24,136]{1,0:T(8,128)(4,1)S(1)} %slice.483), kind=kLoop, calls=%fused_computation.114 | loop fusion | flops 3916800 | bytes 7823808 | tf_op jit(solution)/shard_map/jit(_where)/select_n | solution.py:187
  58.2 1.3 %fusion.89 = f32[49,22,134]{2,1,0:T(8,128)S(1)} fusion(f32[50,24,136]{2,1,0:T(8,128)S(1)} %fusion.75, f32[100,32,140]{2,1,0:T(8,128)S(1)} %bitcast.58), kind=kLoop, calls=%fused_computation.140 | loop fusion | flops 577808 | bytes 2889040 | tf_op jit(solution)/shard_map/mul | solution.py:93
  59.5 3.1 %fusion.59 = f32[50,22,134]{2,1,0:T(8,128)S(1)} fusion(f32[50,24,136]{2,1,0:T(8,128)S(1)} %fusion.75, f32[100,32,140]{2,1,0:T(8,128)S(1)} %bitcast.59, f32[49,22,134]{2,1,0:T(8,128)S(1)} %fusion.89, pred[22,134]{1,0:T(8,128)(4,1)S(1)} %slice.482), kind=kLoop, calls=%fused_computation.90 | loop fusion | flops 3537600 | bytes 7066356 | tf_op jit(solution)/shard_map/jit(_where)/select_n | solution.py:187
  62.6 1.3 %fusion.87 = f32[49,20,132]{2,1,0:T(8,128)S(1)} fusion(f32[50,22,134]{2,1,0:T(8,128)S(1)} %fusion.59, f32[100,32,140]{2,1,0:T(8,128)S(1)} %bitcast.60), kind=kLoop, calls=%fused_computation.136 | loop fusion | flops 517440 | bytes 2587200 | tf_op jit(solution)/shard_map/mul | solution.py:93
  64.0 3.1 %fusion.43 = f32[50,20,132]{2,1,0:T(8,128)S(1)} fusion(f32[50,22,134]{2,1,0:T(8,128)S(1)} %fusion.59, f32[100,32,140]{2,1,0:T(8,128)S(1)} %bitcast.61, f32[49,20,132]{2,1,0:T(8,128)S(1)} %fusion.87, pred[20,132]{1,0:T(8,128)(4,1)S(1)} %slice.481), kind=kLoop, calls=%fused_computation.66 | loop fusion | flops 3168000 | bytes 6328080 | tf_op jit(solution)/shard_map/jit(_where)/select_n | solution.py:187
  67.0 1.3 %fusion.85 = f32[49,18,130]{2,1,0:T(8,128)S(1)} fusion(f32[50,20,132]{2,1,0:T(8,128)S(1)} %fusion.43, f32[100,32,140]{2,1,0:T(8,128)S(1)} %bitcast.62), kind=kLoop, calls=%fused_computation.132 | loop fusion | flops 458640 | bytes 2293200 | tf_op jit(solution)/shard_map/mul | solution.py:93
  68.4 3.3 %fusion.27 = f32[50,18,130]{2,1,0:T(8,128)S(1)} fusion(f32[50,20,132]{2,1,0:T(8,128)S(1)} %fusion.43, f32[100,32,140]{2,1,0:T(8,128)S(1)} %bitcast.63, f32[49,18,130]{2,1,0:T(8,128)S(1)} %fusion.85, pred[18,130]{1,0:T(8,128)(4,1)S(1)} %slice.480), kind=kLoop, calls=%fused_computation.42 | loop fusion | flops 2808000 | bytes 5608980 | tf_op jit(solution)/shard_map/jit(_where)/select_n | solution.py:187
  72.2 1.0 %fusion.101 = f32[50,16,128]{2,1,0:T(8,128)S(1)} fusion(f32[50,18,130]{2,1,0:T(8,128)S(1)} %fusion.27, f32[100,32,140]{2,1,0:T(8,128)S(1)} %bitcast.65, f32[49,16,128]{2,1,0:T(8,128)S(1)} %fusion.111), kind=kLoop, calls=%fused_computation.161 | loop fusion | flops 2355200 | bytes 4907008 | tf_op jit(solution)/shard_map/add | solution.py:99
  74.1 3.3 %all-to-all-start.1 = ((f32[4,32,128]{2,1,0:T(8,128)}), f32[4,32,128]{2,1,0:T(8,128)S(1)}, u32[]{:S(2)}, u32[]{:S(2)}) async-start(f32[4,32,128]{2,1,0:T(8,128)} %fusion.138), calls=%async_computation.1 | async-start | bytes 131072 | tf_op jit(solution)/shard_map/all_to_all | solution.py:192
  77.4 4.4 %all-to-all-done.1 = f32[4,32,128]{2,1,0:T(8,128)S(1)} async-done(((f32[4,32,128]{2,1,0:T(8,128)}), f32[4,32,128]{2,1,0:T(8,128)S(1)}, u32[]{:S(2)}, u32[]{:S(2)}) %all-to-all-start.1) | async-done | bytes 65568 | tf_op jit(solution)/shard_map/all_to_all | solution.py:192
  (52 shorter events, 10.6 us)
Async XLA Ops:
  0.6 6.5 %copy-start.5 = (s32[64]{0:T(128)S(1)}, s32[64]{0:T(128)}, u32[]{:S(2)}) copy-start(s32[64]{0:T(128)} %param.17) | copy-start | bytes 772
  3.7 13.2 %copy-start = (f32[50,16,128]{2,1,0:T(8,128)S(1)}, f32[50,16,128]{2,1,0:T(8,128)}, u32[]{:S(2)}) copy-start(f32[50,16,128]{2,1,0:T(8,128)} %param.14) | copy-start | bytes 1228804
  3.7 13.4 %copy-start.2 = (f32[50,16,128]{2,1,0:T(8,128)S(1)}, f32[50,16,128]{2,1,0:T(8,128)}, u32[]{:S(2)}) copy-start(f32[50,16,128]{2,1,0:T(8,128)} %param.15) | copy-start | bytes 1228804
  8.2 8.6 %all-to-all-start = ((f32[4,33,128]{2,1,0:T(8,128)}), f32[4,33,128]{2,1,0:T(8,128)S(1)}, u32[]{:S(2)}, u32[]{:S(2)}) async-start(f32[4,33,128]{2,1,0:T(8,128)} %pad_maximum_fusion.1), calls=%async_computation | async-start | bytes 163840 | tf_op jit(solution)/shard_map/all_to_all | solution.py:129
  17.1 11.3 %collective-permute-start = (f32[100,6,128]{2,1,0:T(8,128)S(1)}, f32[100,6,128]{2,1,0:T(8,128)S(1)}, u32[]{:S(2)}, u32[]{:S(2)}) collective-permute-start(f32[100,6,128]{2,1,0:T(8,128)S(1)} %get-tuple-element.15), channel_id=1, source_target_pairs={{0,4},{4,8},{8,12},{12,16},{16,20},{20,24},{24,28},{28,32},{32,36}... | collective-permute-start | bytes 921608 | tf_op jit(solution)/shard_map/ppermute | solution.py:25
  23.5 12.6 %collective-permute-start.1 = (f32[100,6,128]{2,1,0:T(8,128)S(1)}, f32[100,6,128]{2,1,0:T(8,128)S(1)}, u32[]{:S(2)}, u32[]{:S(2)}) collective-permute-start(f32[100,6,128]{2,1,0:T(8,128)S(1)} %get-tuple-element.16), channel_id=1, source_target_pairs={{4,0},{8,4},{12,8},{16,12},{20,16},{24,20},{28,24},{32,28},{36,32}... | collective-permute-start | bytes 921608 | tf_op jit(solution)/shard_map/ppermute | solution.py:27
  38.2 4.0 %collective-permute-start.2 = (f32[6,3200]{1,0:T(8,128)S(1)}, f32[6,3200]{1,0:T(8,128)S(1)}, u32[]{:S(2)}, u32[]{:S(2)}) collective-permute-start(f32[6,3200]{1,0:T(8,128)S(1)} %fusion.146), channel_id=1, source_target_pairs={{0,1},{1,2},{2,3},{4,5},{5,6},{6,7},{8,9},{9,10},{10,11},{12,13},{... | collective-permute-start | bytes 230408 | tf_op jit(solution)/shard_map/ppermute | solution.py:154
  40.4 5.4 %collective-permute-start.3 = (f32[6,3200]{1,0:T(8,128)S(1)}, f32[6,3200]{1,0:T(8,128)S(1)}, u32[]{:S(2)}, u32[]{:S(2)}) collective-permute-start(f32[6,3200]{1,0:T(8,128)S(1)} %fusion.147), channel_id=1, source_target_pairs={{1,0},{2,1},{3,2},{5,4},{6,5},{7,6},{9,8},{10,9},{11,10},{13,12},{... | collective-permute-start | bytes 230408 | tf_op jit(solution)/shard_map/ppermute | solution.py:155
  73.2 10.6 %copy-start.3 = (f32[50,16,128]{2,1,0:T(8,128)}, f32[50,16,128]{2,1,0:T(8,128)S(1)}, u32[]{:S(2)}) copy-start(f32[50,16,128]{2,1,0:T(8,128)S(1)} %fusion.101) | copy-start | bytes 1228804
  73.2 8.9 %copy-start.1 = (f32[20,64,128]{2,1,0:T(8,128)S(1)}, f32[20,64,128]{2,1,0:T(8,128)}, u32[]{:S(2)}) copy-start(f32[20,64,128]{2,1,0:T(8,128)} %shard_map.112) | copy-start | bytes 1966084
  73.2 9.0 %copy-start.4 = (s32[64]{0:T(128)S(1)}, s32[64]{0:T(128)}, u32[]{:S(2)}) copy-start(s32[64]{0:T(128)} %param.18) | copy-start | bytes 772
  73.2 9.7 %slice-start = ((f32[20,64,128]{2,1,0:T(8,128)}), f32[19,64,128]{2,1,0:T(8,128)S(1)}, s32[]{:S(2)}) async-start(f32[20,64,128]{2,1,0:T(8,128)} %shard_map.112), calls=%async_computation.2 | async-start | bytes 1245184 | tf_op jit(solution)/shard_map/slice | solution.py:195
  74.1 7.7 %all-to-all-start.1 = ((f32[4,32,128]{2,1,0:T(8,128)}), f32[4,32,128]{2,1,0:T(8,128)S(1)}, u32[]{:S(2)}, u32[]{:S(2)}) async-start(f32[4,32,128]{2,1,0:T(8,128)} %fusion.138), calls=%async_computation.1 | async-start | bytes 131072 | tf_op jit(solution)/shard_map/all_to_all | solution.py:192

commit v9 on v8

--- a/solution.py
+++ b/solution.py
@@ -76,21 +76,34 @@
     )(jnp.transpose(moisture, (1, 0, 2)), jnp.transpose(diffusivity, (1, 0, 2)), rain)
 
 
-def lateral_core(padded_head, padded_cond):
+SHIFTS = ((0, 1), (2, 1), (1, 0), (1, 2))
+
+
+def conductances(padded_cond):
+    inner_rows = padded_cond.shape[1] - 2
+    inner_cols = padded_cond.shape[2] - 2
+    centre_cond = padded_cond[:, 1:-1, 1:-1]
+    sides = []
+    for row_shift, col_shift in SHIFTS:
+        beside_cond = padded_cond[
+            :, row_shift : row_shift + inner_rows, col_shift : col_shift + inner_cols
+        ]
+        sides.append(0.5 * (centre_cond + beside_cond))
+    sides.append(0.5 * (centre_cond[1:] + centre_cond[:-1]))
+    return sides
+
+
+def lateral_core(padded_head, sides):
     inner_rows = padded_head.shape[1] - 2
     inner_cols = padded_head.shape[2] - 2
     centre = padded_head[:, 1:-1, 1:-1]
-    centre_cond = padded_cond[:, 1:-1, 1:-1]
     flux_total = jnp.zeros_like(centre)
-    for row_shift, col_shift in ((0, 1), (2, 1), (1, 0), (1, 2)):
+    for (row_shift, col_shift), side in zip(SHIFTS, sides):
         beside = padded_head[
             :, row_shift : row_shift + inner_rows, col_shift : col_shift + inner_cols
         ]
-        beside_cond = padded_cond[
-            :, row_shift : row_shift + inner_rows, col_shift : col_shift + inner_cols
-        ]
-        flux_total = flux_total + 0.5 * (centre_cond + beside_cond) * (beside - centre)
-    vertical = 0.5 * (centre_cond[1:] + centre_cond[:-1]) * (centre[1:] - centre[:-1])
+        flux_total = flux_total + side * (beside - centre)
+    vertical = sides[4] * (centre[1:] - centre[:-1])
     flux_total = (
         flux_total
         + jnp.pad(vertical, ((0, 1), (0, 0), (0, 0)))
@@ -179,9 +192,13 @@
         & (col_at >= 0)
         & (col_at < tile_cols * tile_count)
     )
+    sides = conductances(padded_cond)
     for sweep_k in range(SWEEPS):
-        field = lateral_core(field, padded_cond)
-        padded_cond = padded_cond[:, 1:-1, 1:-1]
+        window = [
+            side[:, sweep_k : side.shape[1] - sweep_k, sweep_k : side.shape[2] - sweep_k]
+            for side in sides
+        ]
+        field = lateral_core(field, window)
         if sweep_k < SWEEPS - 1:
             edge = sweep_k + 1
             field = jnp.where(inside[None, edge:-edge, edge:-edge], field, 0.0)

time: 84.4 us -> 81.4 us (0.964)
  other arithmetic: 29.5 us -> 26.6 us
    select_n x5, other arithmetic: 16.4 us -> 14.5 us  [local(): field = jnp.where(inside[None, edge:-edge, edge:-edge], field, 0.0)]
    mul x6, other arithmetic: 7.6 us -> 6.54 us  [lateral_core(): vertical = sides[4] * (centre[1:] - centre[:-1])]
where the time goes in v9:
time: 81.4 us; the launch traced here: 80.9 us
  other arithmetic  26.6 us (33%)
  waiting for transfers between devices  23.2 us (29%)
  starting transfers between devices  19.1 us (23%)
  matrix products  7.41 us (9%)
  Pallas kernels  2.48 us (3%)
  between operations  1.61 us (2%)
    select_n x5, other arithmetic, local(): field = jnp.where(inside[None, edge:-edge, edge:-edge], field, 0.0)  14.5 us
    ppermute x1, waiting for transfers between devices, with_halo(): lax.ppermute(head, axis, [((i + 1) % count, i) for i in range(ends)])  7.72 us
    mul x6, other arithmetic, lateral_core(): vertical = sides[4] * (centre[1:] - centre[:-1])  6.54 us
    ppermute x1, starting transfers between devices, with_halo(): lax.ppermute(tail, axis, [(i, (i + 1) % count) for i in range(ends)])  6.41 us
    all_to_all x1, waiting for transfers between devices, local(): lax.all_to_all(packed, 'gy', split_axis=0, concat_axis=0, tiled=True)  4.53 us
    all_to_all x1, waiting for transfers between devices, local(): lax.all_to_all(answered, 'gy', split_axis=0, concat_axis=0, tiled=True)  4.43 us
    all_to_all x1, starting transfers between devices, local(): lax.all_to_all(packed, 'gy', split_axis=0, concat_axis=0, tiled=True)  4.01 us
    ppermute x1, waiting for transfers between devices, local(): lax.ppermute(left_strip, 'gy', [(i + 1, i) for i in range(ends)])  3.62 us
  transfers between devices with their start and end apart: 6, of which 5 were waited for; matrix products, arithmetic and copies ran while one was open for 1% of the time, Pallas kernels for 0%

profile of v9, /device:TPU:249, one launch (start us, length us, event | category | flops | bytes accessed | tf_op | source)
XLA Modules:
  0.0 80.9 jit_solution(4882297779835330958)
XLA Ops:
  3.7 2.5 %shard_map.112 = f32[20,64,128]{2,1,0:T(8,128)} custom-call(f32[20,64,128]{2,1,0:T(8,128)} %bitcast.60, f32[20,64,128]{2,1,0:T(8,128)} %bitcast.59, f32[64,128]{1,0:T(8,128)} %rain_ref.1), custom_call_target="tpu_custom_call" | custom-call | flops 1966080 | bytes 1966080 | tf_op jit(solution)/shard_map/pallas_call | solution.py:67
  8.2 4.0 %all-to-all-start = ((f32[4,33,128]{2,1,0:T(8,128)}), f32[4,33,128]{2,1,0:T(8,128)S(1)}, u32[]{:S(2)}, u32[]{:S(2)}) async-start(f32[4,33,128]{2,1,0:T(8,128)} %pad_maximum_fusion.1), calls=%async_computation | async-start | bytes 163840 | tf_op jit(solution)/shard_map/all_to_all | solution.py:142
  12.2 4.5 %all-to-all-done = f32[4,33,128]{2,1,0:T(8,128)S(1)} async-done(((f32[4,33,128]{2,1,0:T(8,128)}), f32[4,33,128]{2,1,0:T(8,128)S(1)}, u32[]{:S(2)}, u32[]{:S(2)}) %all-to-all-start) | async-done | bytes 67616 | tf_op jit(solution)/shard_map/all_to_all | solution.py:142
  17.1 6.4 %collective-permute-start = (f32[100,6,128]{2,1,0:T(8,128)S(1)}, f32[100,6,128]{2,1,0:T(8,128)S(1)}, u32[]{:S(2)}, u32[]{:S(2)}) collective-permute-start(f32[100,6,128]{2,1,0:T(8,128)S(1)} %get-tuple-element.22), channel_id=1, source_target_pairs={{0,4},{4,8},{8,12},{12,16},{16,20},{20,24},{24,28},{28,32},{32,36}... | collective-permute-start | bytes 921608 | tf_op jit(solution)/shard_map/ppermute | solution.py:25
  23.5 1.9 %collective-permute-start.1 = (f32[100,6,128]{2,1,0:T(8,128)S(1)}, f32[100,6,128]{2,1,0:T(8,128)S(1)}, u32[]{:S(2)}, u32[]{:S(2)}) collective-permute-start(f32[100,6,128]{2,1,0:T(8,128)S(1)} %get-tuple-element.23), channel_id=1, source_target_pairs={{4,0},{8,4},{12,8},{16,12},{20,16},{24,20},{28,24},{32,28},{36,32}... | collective-permute-start | bytes 921608 | tf_op jit(solution)/shard_map/ppermute | solution.py:27
  25.6 2.9 %collective-permute-done = f32[100,6,128]{2,1,0:T(8,128)S(1)} collective-permute-done((f32[100,6,128]{2,1,0:T(8,128)S(1)}, f32[100,6,128]{2,1,0:T(8,128)S(1)}, u32[]{:S(2)}, u32[]{:S(2)}) %collective-permute-start) | collective-permute-done | bytes 307232 | tf_op jit(solution)/shard_map/ppermute | solution.py:25
  28.4 7.7 %collective-permute-done.1 = f32[100,6,128]{2,1,0:T(8,128)S(1)} collective-permute-done((f32[100,6,128]{2,1,0:T(8,128)S(1)}, f32[100,6,128]{2,1,0:T(8,128)S(1)}, u32[]{:S(2)}, u32[]{:S(2)}) %collective-permute-start.1) | collective-permute-done | bytes 307232 | tf_op jit(solution)/shard_map/ppermute | solution.py:27
  38.2 2.2 %collective-permute-start.2 = (f32[6,3200]{1,0:T(8,128)S(1)}, f32[6,3200]{1,0:T(8,128)S(1)}, u32[]{:S(2)}, u32[]{:S(2)}) collective-permute-start(f32[6,3200]{1,0:T(8,128)S(1)} %fusion.121), channel_id=1, source_target_pairs={{0,1},{1,2},{2,3},{4,5},{5,6},{6,7},{8,9},{9,10},{10,11},{12,13},{... | collective-permute-start | bytes 230408 | tf_op jit(solution)/shard_map/ppermute | solution.py:167
  40.4 1.3 %collective-permute-start.3 = (f32[6,3200]{1,0:T(8,128)S(1)}, f32[6,3200]{1,0:T(8,128)S(1)}, u32[]{:S(2)}, u32[]{:S(2)}) collective-permute-start(f32[6,3200]{1,0:T(8,128)S(1)} %fusion.122), channel_id=1, source_target_pairs={{1,0},{2,1},{3,2},{5,4},{6,5},{7,6},{9,8},{10,9},{11,10},{13,12},{... | collective-permute-start | bytes 230408 | tf_op jit(solution)/shard_map/ppermute | solution.py:168
  42.2 3.6 %collective-permute-done.3 = f32[6,3200]{1,0:T(8,128)S(1)} collective-permute-done((f32[6,3200]{1,0:T(8,128)S(1)}, f32[6,3200]{1,0:T(8,128)S(1)}, u32[]{:S(2)}, u32[]{:S(2)}) %collective-permute-start.3) | collective-permute-done | bytes 76832 | tf_op jit(solution)/shard_map/ppermute | solution.py:168
  45.8 2.3 %pad_add_fusion = f32[3200,140]{1,0:T(8,128)S(1)} fusion(f32[3200,128]{1,0:T(8,128)S(1)} %bitcast.58, f32[6,3200]{1,0:T(8,128)S(1)} %collective-permute-done.3, f32[6,3200]{1,0:T(8,128)S(1)} %collective-permute-done.2, pred[6,140]{1,0:T(8,128)(4,1)S(1)} %get-tuple-element.26, pred[6,140]{1,0:T(8,128)(4,1)S(1)} %get-tuple-element.27), kind=kOutput, calls=%fused_computation | convolution fusion | flops 65000080 | bytes 3585680 | tf_op jit(solution)/shard_map/dot_general | solution.py:171
  48.1 1.7 %fusion.19 = (f32[49,26,138]{2,1,0:T(8,128)S(1)}, f32[49,26,138]{2,1,0:T(8,128)S(1)}) fusion(f32[100,32,140]{2,1,0:T(8,128)S(1)} %bitcast.54), kind=kLoop, calls=%fused_computation.32 | loop fusion | flops 703248 | bytes 4219488 | tf_op jit(solution)/shard_map/mul | solution.py:106
  49.9 3.8 %fusion.6 = (f32[50,26,138]{2,1,0:T(8,128)S(1)}, f32[50,26,138]{2,1,0:T(8,128)S(1)}, f32[50,26,138]{2,1,0:T(8,128)S(1)}, f32[50,26,138]{2,1,0:T(8,128)S(1)}, f32[50,26,138]{2,1,0:T(8,128)S(1)}) fusion(f32[100,32,140]{2,1,0:T(8,128)S(1)} %bitcast.55, f32[49,26,138]{2,1,0:T(8,128)S(1)} %get-tuple-element.20, pred[26,138]{1,0:T(8,128)(4,1)S(1)} %slice.404), kind=kLoop, calls=%fused_computation.8 | loop fusion | flops 4305600 | bytes 11470836 | tf_op jit(solution)/shard_map/jit(_where)/select_n | solution.py:204
  53.7 1.0 %fusion.72 = f32[49,24,136]{2,1,0:T(8,128)S(1)} fusion(f32[50,26,138]{2,1,0:T(8,128)S(1)} %get-tuple-element.15, f32[49,26,138]{2,1,0:T(8,128)S(1)} %get-tuple-element.21), kind=kLoop, calls=%fused_computation.106 | loop fusion | flops 319872 | bytes 2558976 | tf_op jit(solution)/shard_map/mul | solution.py:106
  54.7 2.6 %fusion.63 = f32[50,24,136]{2,1,0:T(8,128)S(1)} fusion(f32[50,26,138]{2,1,0:T(8,128)S(1)} %get-tuple-element.15, f32[50,26,138]{2,1,0:T(8,128)S(1)} %get-tuple-element.19, f32[50,26,138]{2,1,0:T(8,128)S(1)} %get-tuple-element.18, f32[50,26,138]{2,1,0:T(8,128)S(1)} %get-tuple-element.17, f32[50,26,138]{2,1,0:T(8,128)S(1)} %get-tuple-element.16, ...), kind=kLoop, calls=%fused_computation.90 | loop fusion | flops 2611200 | bytes 7171008 | tf_op jit(solution)/shard_map/jit(_where)/select_n | solution.py:204
  57.4 1.0 %fusion.71 = f32[49,22,134]{2,1,0:T(8,128)S(1)} fusion(f32[50,24,136]{2,1,0:T(8,128)S(1)} %fusion.63, f32[49,26,138]{2,1,0:T(8,128)S(1)} %get-tuple-element.21), kind=kLoop, calls=%fused_computation.104 | loop fusion | flops 288904 | bytes 2311232 | tf_op jit(solution)/shard_map/mul | solution.py:106
  58.4 2.6 %fusion.51 = f32[50,22,134]{2,1,0:T(8,128)S(1)} fusion(f32[50,24,136]{2,1,0:T(8,128)S(1)} %fusion.63, f32[50,26,138]{2,1,0:T(8,128)S(1)} %get-tuple-element.19, f32[50,26,138]{2,1,0:T(8,128)S(1)} %get-tuple-element.18, f32[50,26,138]{2,1,0:T(8,128)S(1)} %get-tuple-element.17, f32[50,26,138]{2,1,0:T(8,128)S(1)} %get-tuple-element.16, ...), kind=kLoop, calls=%fused_computation.74 | loop fusion | flops 2358400 | bytes 6476756 | tf_op jit(solution)/shard_map/jit(_where)/select_n | solution.py:204
  61.0 1.1 %fusion.70 = f32[49,20,132]{2,1,0:T(8,128)S(1)} fusion(f32[50,22,134]{2,1,0:T(8,128)S(1)} %fusion.51, f32[49,26,138]{2,1,0:T(8,128)S(1)} %get-tuple-element.21), kind=kLoop, calls=%fused_computation.102 | loop fusion | flops 258720 | bytes 2069760 | tf_op jit(solution)/shard_map/mul | solution.py:106
  62.1 2.7 %fusion.39 = f32[50,20,132]{2,1,0:T(8,128)S(1)} fusion(f32[50,22,134]{2,1,0:T(8,128)S(1)} %fusion.51, f32[50,26,138]{2,1,0:T(8,128)S(1)} %get-tuple-element.19, f32[50,26,138]{2,1,0:T(8,128)S(1)} %get-tuple-element.18, f32[50,26,138]{2,1,0:T(8,128)S(1)} %get-tuple-element.17, f32[50,26,138]{2,1,0:T(8,128)S(1)} %get-tuple-element.16, ...), kind=kLoop, calls=%fused_computation.58 | loop fusion | flops 2112000 | bytes 5800080 | tf_op jit(solution)/shard_map/jit(_where)/select_n | solution.py:204
  64.8 1.3 %fusion.69 = f32[49,18,130]{2,1,0:T(8,128)S(1)} fusion(f32[50,20,132]{2,1,0:T(8,128)S(1)} %fusion.39, f32[49,26,138]{2,1,0:T(8,128)S(1)} %get-tuple-element.21), kind=kLoop, calls=%fused_computation.100 | loop fusion | flops 229320 | bytes 1834560 | tf_op jit(solution)/shard_map/mul | solution.py:106
  66.1 2.7 %fusion.27 = f32[50,18,130]{2,1,0:T(8,128)S(1)} fusion(f32[50,20,132]{2,1,0:T(8,128)S(1)} %fusion.39, f32[50,26,138]{2,1,0:T(8,128)S(1)} %get-tuple-element.19, f32[50,26,138]{2,1,0:T(8,128)S(1)} %get-tuple-element.18, f32[50,26,138]{2,1,0:T(8,128)S(1)} %get-tuple-element.17, f32[50,26,138]{2,1,0:T(8,128)S(1)} %get-tuple-element.16, ...), kind=kLoop, calls=%fused_computation.42 | loop fusion | flops 1872000 | bytes 5140980 | tf_op jit(solution)/shard_map/jit(_where)/select_n | solution.py:204
  69.3 1.0 %fusion.81 = f32[50,16,128]{2,1,0:T(8,128)S(1)} fusion(f32[50,18,130]{2,1,0:T(8,128)S(1)} %fusion.27, f32[50,26,138]{2,1,0:T(8,128)S(1)} %get-tuple-element.19, f32[50,26,138]{2,1,0:T(8,128)S(1)} %get-tuple-element.18, f32[50,26,138]{2,1,0:T(8,128)S(1)} %get-tuple-element.17, f32[50,26,138]{2,1,0:T(8,128)S(1)} %get-tuple-element.16, ...), kind=kLoop, calls=%fused_computation.121 | loop fusion | flops 1536000 | bytes 4497408 | tf_op jit(solution)/shard_map/add | solution.py:112
  71.2 3.3 %all-to-all-start.1 = ((f32[4,32,128]{2,1,0:T(8,128)}), f32[4,32,128]{2,1,0:T(8,128)S(1)}, u32[]{:S(2)}, u32[]{:S(2)}) async-start(f32[4,32,128]{2,1,0:T(8,128)} %fusion.113), calls=%async_computation.1 | async-start | bytes 131072 | tf_op jit(solution)/shard_map/all_to_all | solution.py:209
  74.5 4.4 %all-to-all-done.1 = f32[4,32,128]{2,1,0:T(8,128)S(1)} async-done(((f32[4,32,128]{2,1,0:T(8,128)}), f32[4,32,128]{2,1,0:T(8,128)S(1)}, u32[]{:S(2)}, u32[]{:S(2)}) %all-to-all-start.1) | async-done | bytes 65568 | tf_op jit(solution)/shard_map/all_to_all | solution.py:209
  (52 shorter events, 10.6 us)
Async XLA Ops:
  0.6 6.5 %copy-start.5 = (s32[64]{0:T(128)S(1)}, s32[64]{0:T(128)}, u32[]{:S(2)}) copy-start(s32[64]{0:T(128)} %param.17) | copy-start | bytes 772
  3.7 13.2 %copy-start = (f32[50,16,128]{2,1,0:T(8,128)S(1)}, f32[50,16,128]{2,1,0:T(8,128)}, u32[]{:S(2)}) copy-start(f32[50,16,128]{2,1,0:T(8,128)} %param.14) | copy-start | bytes 1228804
  3.7 13.4 %copy-start.2 = (f32[50,16,128]{2,1,0:T(8,128)S(1)}, f32[50,16,128]{2,1,0:T(8,128)}, u32[]{:S(2)}) copy-start(f32[50,16,128]{2,1,0:T(8,128)} %param.15) | copy-start | bytes 1228804
  8.2 8.6 %all-to-all-start = ((f32[4,33,128]{2,1,0:T(8,128)}), f32[4,33,128]{2,1,0:T(8,128)S(1)}, u32[]{:S(2)}, u32[]{:S(2)}) async-start(f32[4,33,128]{2,1,0:T(8,128)} %pad_maximum_fusion.1), calls=%async_computation | async-start | bytes 163840 | tf_op jit(solution)/shard_map/all_to_all | solution.py:142
  17.1 11.3 %collective-permute-start = (f32[100,6,128]{2,1,0:T(8,128)S(1)}, f32[100,6,128]{2,1,0:T(8,128)S(1)}, u32[]{:S(2)}, u32[]{:S(2)}) collective-permute-start(f32[100,6,128]{2,1,0:T(8,128)S(1)} %get-tuple-element.22), channel_id=1, source_target_pairs={{0,4},{4,8},{8,12},{12,16},{16,20},{20,24},{24,28},{28,32},{32,36}... | collective-permute-start | bytes 921608 | tf_op jit(solution)/shard_map/ppermute | solution.py:25
  23.5 12.6 %collective-permute-start.1 = (f32[100,6,128]{2,1,0:T(8,128)S(1)}, f32[100,6,128]{2,1,0:T(8,128)S(1)}, u32[]{:S(2)}, u32[]{:S(2)}) collective-permute-start(f32[100,6,128]{2,1,0:T(8,128)S(1)} %get-tuple-element.23), channel_id=1, source_target_pairs={{4,0},{8,4},{12,8},{16,12},{20,16},{24,20},{28,24},{32,28},{36,32}... | collective-permute-start | bytes 921608 | tf_op jit(solution)/shard_map/ppermute | solution.py:27
  38.2 4.0 %collective-permute-start.2 = (f32[6,3200]{1,0:T(8,128)S(1)}, f32[6,3200]{1,0:T(8,128)S(1)}, u32[]{:S(2)}, u32[]{:S(2)}) collective-permute-start(f32[6,3200]{1,0:T(8,128)S(1)} %fusion.121), channel_id=1, source_target_pairs={{0,1},{1,2},{2,3},{4,5},{5,6},{6,7},{8,9},{9,10},{10,11},{12,13},{... | collective-permute-start | bytes 230408 | tf_op jit(solution)/shard_map/ppermute | solution.py:167
  40.4 5.4 %collective-permute-start.3 = (f32[6,3200]{1,0:T(8,128)S(1)}, f32[6,3200]{1,0:T(8,128)S(1)}, u32[]{:S(2)}, u32[]{:S(2)}) collective-permute-start(f32[6,3200]{1,0:T(8,128)S(1)} %fusion.122), channel_id=1, source_target_pairs={{1,0},{2,1},{3,2},{5,4},{6,5},{7,6},{9,8},{10,9},{11,10},{13,12},{... | collective-permute-start | bytes 230408 | tf_op jit(solution)/shard_map/ppermute | solution.py:168
  70.3 10.6 %copy-start.3 = (f32[50,16,128]{2,1,0:T(8,128)}, f32[50,16,128]{2,1,0:T(8,128)S(1)}, u32[]{:S(2)}) copy-start(f32[50,16,128]{2,1,0:T(8,128)S(1)} %fusion.81) | copy-start | bytes 1228804
  70.3 8.9 %copy-start.1 = (f32[20,64,128]{2,1,0:T(8,128)S(1)}, f32[20,64,128]{2,1,0:T(8,128)}, u32[]{:S(2)}) copy-start(f32[20,64,128]{2,1,0:T(8,128)} %shard_map.112) | copy-start | bytes 1966084
  70.3 9.0 %copy-start.4 = (s32[64]{0:T(128)S(1)}, s32[64]{0:T(128)}, u32[]{:S(2)}) copy-start(s32[64]{0:T(128)} %param.18) | copy-start | bytes 772
  70.3 9.7 %slice-start = ((f32[20,64,128]{2,1,0:T(8,128)}), f32[19,64,128]{2,1,0:T(8,128)S(1)}, s32[]{:S(2)}) async-start(f32[20,64,128]{2,1,0:T(8,128)} %shard_map.112), calls=%async_computation.2 | async-start | bytes 1245184 | tf_op jit(solution)/shard_map/slice | solution.py:212
  71.2 7.7 %all-to-all-start.1 = ((f32[4,32,128]{2,1,0:T(8,128)}), f32[4,32,128]{2,1,0:T(8,128)S(1)}, u32[]{:S(2)}, u32[]{:S(2)}) async-start(f32[4,32,128]{2,1,0:T(8,128)} %fusion.113), calls=%async_computation.1 | async-start | bytes 131072 | tf_op jit(solution)/shard_map/all_to_all | solution.py:209

commit v10 on v9

--- a/solution.py
+++ b/solution.py
@@ -128,7 +128,11 @@
     to_tile = (
         (tile_ids[:, None] == jnp.arange(tile_count, dtype=jnp.int32)[None, :]) & in_use[:, None]
     ).astype(jnp.int32)
-    before = jnp.cumsum(to_tile, axis=0) - to_tile
+    earlier = (
+        jnp.arange(block_count, dtype=jnp.int32)[None, :]
+        < jnp.arange(block_count, dtype=jnp.int32)[:, None]
+    ).astype(jnp.float32)
+    before = jnp.dot(earlier, to_tile.astype(jnp.float32), precision=highest).astype(jnp.int32)
     slot_of = jnp.sum(before * to_tile, axis=1)
     slot_match = slot_of[None, None, :] == jnp.arange(capacity, dtype=jnp.int32)[None, :, None]
     placing = (to_tile.T[:, None, :] * slot_match).astype(jnp.float32)
@@ -209,7 +213,7 @@
     returned = lax.all_to_all(answered, "gy", split_axis=0, concat_axis=0, tiled=True)
     saturation = jnp.einsum("tcb,tcj->bj", placing, returned, precision=highest)
     new_bottom = bottom + capillary * (saturation - in_use_f[:, None] * bottom)
-    moisture_out = jnp.transpose(jnp.concatenate([wet[: depth - 1], new_bottom[None]]), (1, 0, 2))
+    moisture_out = jnp.transpose(wet.at[depth - 1].set(new_bottom), (1, 0, 2))
     patch_hot = (patch_ids[None, :] == jnp.arange(PATCH_DEV, dtype=jnp.int32)[:, None]).astype(
         jnp.float32
     )

time: 81.4 us -> 80.3 us (0.986)
  other arithmetic: 26.6 us -> 24 us
  matrix products: 7.41 us -> 8.92 us
    dot_general x0 -> x1, matrix products: none -> 0.89 us  [local(): jnp.dot(earlier, to_tile.astype(jnp.float32), precision=highest)]
    transpose x1 -> x0, other arithmetic: 0.88 us -> none  [local(): jnp.transpose(jnp.concatenate([wet[:depth - 1], new_bottom[None]]), (1, 0...]
    reduce_sum x1 -> x0, other arithmetic: 0.84 us -> none  [local(): slot_of = jnp.sum(before * to_tile, axis=1)]
  transfers between devices with their start and end apart: 6 -> 6, of which waited for: 5 -> 5; matrix products, arithmetic and copies ran while one was open for 1% -> 2% of each run, Pallas kernels for 0% -> 0%
where the time goes in v10:
time: 80.3 us; the launch traced here: 79.8 us
  other arithmetic  24 us (30%)
  waiting for transfers between devices  22.4 us (28%)
  starting transfers between devices  19.1 us (24%)
  matrix products  8.92 us (11%)
  Pallas kernels  2.48 us (3%)
  between operations  1.55 us (2%)
  local copies, waits for them, and re-layouts  1.33 us (2%)
    select_n x5, other arithmetic, local(): field = jnp.where(inside[None, edge:-edge, edge:-edge], field, 0.0)  14.5 us
    ppermute x1, waiting for transfers between devices, with_halo(): lax.ppermute(head, axis, [((i + 1) % count, i) for i in range(ends)])  7.72 us
    mul x6, other arithmetic, lateral_core(): vertical = sides[4] * (centre[1:] - centre[:-1])  6.54 us
    ppermute x1, starting transfers between devices, with_halo(): lax.ppermute(tail, axis, [(i, (i + 1) % count) for i in range(ends)])  6.41 us
    all_to_all x1, waiting for transfers between devices, local(): lax.all_to_all(packed, 'gy', split_axis=0, concat_axis=0, tiled=True)  4.46 us
    all_to_all x1, waiting for transfers between devices, local(): lax.all_to_all(answered, 'gy', split_axis=0, concat_axis=0, tiled=True)  4.43 us
    all_to_all x1, starting transfers between devices, local(): lax.all_to_all(packed, 'gy', split_axis=0, concat_axis=0, tiled=True)  4.01 us
    ppermute x1, waiting for transfers between devices, local(): lax.ppermute(left_strip, 'gy', [(i + 1, i) for i in range(ends)])  3.62 us
  transfers between devices with their start and end apart: 6, of which 5 were waited for; matrix products, arithmetic and copies ran while one was open for 2% of the time, Pallas kernels for 0%

profile of v10, /device:TPU:249, one launch (start us, length us, event | category | flops | bytes accessed | tf_op | source)
XLA Modules:
  0.0 79.8 jit_solution(2515648957814328140)
XLA Ops:
  2.9 2.5 %shard_map.112 = f32[20,64,128]{2,1,0:T(8,128)} custom-call(f32[20,64,128]{2,1,0:T(8,128)} %bitcast.58, f32[20,64,128]{2,1,0:T(8,128)} %bitcast.57, f32[64,128]{1,0:T(8,128)} %rain_ref.1), custom_call_target="tpu_custom_call" | custom-call | flops 1966080 | bytes 1966080 | tf_op jit(solution)/shard_map/pallas_call | solution.py:67
  7.4 4.0 %all-to-all-start = ((f32[4,33,128]{2,1,0:T(8,128)}), f32[4,33,128]{2,1,0:T(8,128)S(1)}, u32[]{:S(2)}, u32[]{:S(2)}) async-start(f32[4,33,128]{2,1,0:T(8,128)} %pad_maximum_fusion.1), calls=%async_computation | async-start | bytes 163840 | tf_op jit(solution)/shard_map/all_to_all | solution.py:146
  11.5 4.5 %all-to-all-done = f32[4,33,128]{2,1,0:T(8,128)S(1)} async-done(((f32[4,33,128]{2,1,0:T(8,128)}), f32[4,33,128]{2,1,0:T(8,128)S(1)}, u32[]{:S(2)}, u32[]{:S(2)}) %all-to-all-start) | async-done | bytes 67616 | tf_op jit(solution)/shard_map/all_to_all | solution.py:146
  16.3 6.4 %collective-permute-start = (f32[100,6,128]{2,1,0:T(8,128)S(1)}, f32[100,6,128]{2,1,0:T(8,128)S(1)}, u32[]{:S(2)}, u32[]{:S(2)}) collective-permute-start(f32[100,6,128]{2,1,0:T(8,128)S(1)} %get-tuple-element.34), channel_id=1, source_target_pairs={{0,4},{4,8},{8,12},{12,16},{16,20},{20,24},{24,28},{28,32},{32,36}... | collective-permute-start | bytes 921608 | tf_op jit(solution)/shard_map/ppermute | solution.py:25
  22.7 1.9 %collective-permute-start.1 = (f32[100,6,128]{2,1,0:T(8,128)S(1)}, f32[100,6,128]{2,1,0:T(8,128)S(1)}, u32[]{:S(2)}, u32[]{:S(2)}) collective-permute-start(f32[100,6,128]{2,1,0:T(8,128)S(1)} %get-tuple-element.35), channel_id=1, source_target_pairs={{4,0},{8,4},{12,8},{16,12},{20,16},{24,20},{28,24},{32,28},{36,32}... | collective-permute-start | bytes 921608 | tf_op jit(solution)/shard_map/ppermute | solution.py:27
  25.4 2.2 %collective-permute-done = f32[100,6,128]{2,1,0:T(8,128)S(1)} collective-permute-done((f32[100,6,128]{2,1,0:T(8,128)S(1)}, f32[100,6,128]{2,1,0:T(8,128)S(1)}, u32[]{:S(2)}, u32[]{:S(2)}) %collective-permute-start) | collective-permute-done | bytes 307232 | tf_op jit(solution)/shard_map/ppermute | solution.py:25
  27.6 7.7 %collective-permute-done.1 = f32[100,6,128]{2,1,0:T(8,128)S(1)} collective-permute-done((f32[100,6,128]{2,1,0:T(8,128)S(1)}, f32[100,6,128]{2,1,0:T(8,128)S(1)}, u32[]{:S(2)}, u32[]{:S(2)}) %collective-permute-start.1) | collective-permute-done | bytes 307232 | tf_op jit(solution)/shard_map/ppermute | solution.py:27
  37.4 2.2 %collective-permute-start.2 = (f32[6,3200]{1,0:T(8,128)S(1)}, f32[6,3200]{1,0:T(8,128)S(1)}, u32[]{:S(2)}, u32[]{:S(2)}) collective-permute-start(f32[6,3200]{1,0:T(8,128)S(1)} %fusion.121), channel_id=1, source_target_pairs={{0,1},{1,2},{2,3},{4,5},{5,6},{6,7},{8,9},{9,10},{10,11},{12,13},{... | collective-permute-start | bytes 230408 | tf_op jit(solution)/shard_map/ppermute | solution.py:171
  39.6 1.3 %collective-permute-start.3 = (f32[6,3200]{1,0:T(8,128)S(1)}, f32[6,3200]{1,0:T(8,128)S(1)}, u32[]{:S(2)}, u32[]{:S(2)}) collective-permute-start(f32[6,3200]{1,0:T(8,128)S(1)} %fusion.122), channel_id=1, source_target_pairs={{1,0},{2,1},{3,2},{5,4},{6,5},{7,6},{9,8},{10,9},{11,10},{13,12},{... | collective-permute-start | bytes 230408 | tf_op jit(solution)/shard_map/ppermute | solution.py:172
  41.4 3.6 %collective-permute-done.3 = f32[6,3200]{1,0:T(8,128)S(1)} collective-permute-done((f32[6,3200]{1,0:T(8,128)S(1)}, f32[6,3200]{1,0:T(8,128)S(1)}, u32[]{:S(2)}, u32[]{:S(2)}) %collective-permute-start.3) | collective-permute-done | bytes 76832 | tf_op jit(solution)/shard_map/ppermute | solution.py:172
  45.0 2.3 %pad_add_fusion = f32[3200,140]{1,0:T(8,128)S(1)} fusion(f32[3200,128]{1,0:T(8,128)S(1)} %bitcast.55, f32[6,3200]{1,0:T(8,128)S(1)} %collective-permute-done.3, f32[6,3200]{1,0:T(8,128)S(1)} %collective-permute-done.2, pred[6,140]{1,0:T(8,128)(4,1)S(1)} %get-tuple-element.40, pred[6,140]{1,0:T(8,128)(4,1)S(1)} %get-tuple-element.41), kind=kOutput, calls=%fused_computation | convolution fusion | flops 65000080 | bytes 3585680 | tf_op jit(solution)/shard_map/dot_general | solution.py:175
  47.3 1.7 %fusion.19 = (f32[49,26,138]{2,1,0:T(8,128)S(1)}, f32[49,26,138]{2,1,0:T(8,128)S(1)}) fusion(f32[100,32,140]{2,1,0:T(8,128)S(1)} %bitcast.51), kind=kLoop, calls=%fused_computation.32 | loop fusion | flops 703248 | bytes 4219488 | tf_op jit(solution)/shard_map/mul | solution.py:106
  49.1 3.8 %fusion.6 = (f32[50,26,138]{2,1,0:T(8,128)S(1)}, f32[50,26,138]{2,1,0:T(8,128)S(1)}, f32[50,26,138]{2,1,0:T(8,128)S(1)}, f32[50,26,138]{2,1,0:T(8,128)S(1)}, f32[50,26,138]{2,1,0:T(8,128)S(1)}) fusion(f32[100,32,140]{2,1,0:T(8,128)S(1)} %bitcast.52, f32[49,26,138]{2,1,0:T(8,128)S(1)} %get-tuple-element.32, pred[26,138]{1,0:T(8,128)(4,1)S(1)} %slice.420), kind=kLoop, calls=%fused_computation.8 | loop fusion | flops 4305600 | bytes 11470836 | tf_op jit(solution)/shard_map/jit(_where)/select_n | solution.py:208
  52.9 1.0 %fusion.72 = f32[49,24,136]{2,1,0:T(8,128)S(1)} fusion(f32[50,26,138]{2,1,0:T(8,128)S(1)} %get-tuple-element.27, f32[49,26,138]{2,1,0:T(8,128)S(1)} %get-tuple-element.33), kind=kLoop, calls=%fused_computation.106 | loop fusion | flops 319872 | bytes 2558976 | tf_op jit(solution)/shard_map/mul | solution.py:106
  54.0 2.6 %fusion.63 = f32[50,24,136]{2,1,0:T(8,128)S(1)} fusion(f32[50,26,138]{2,1,0:T(8,128)S(1)} %get-tuple-element.27, f32[50,26,138]{2,1,0:T(8,128)S(1)} %get-tuple-element.31, f32[50,26,138]{2,1,0:T(8,128)S(1)} %get-tuple-element.30, f32[50,26,138]{2,1,0:T(8,128)S(1)} %get-tuple-element.29, f32[50,26,138]{2,1,0:T(8,128)S(1)} %get-tuple-element.28, ...), kind=kLoop, calls=%fused_computation.90 | loop fusion | flops 2611200 | bytes 7171008 | tf_op jit(solution)/shard_map/jit(_where)/select_n | solution.py:208
  56.6 1.0 %fusion.71 = f32[49,22,134]{2,1,0:T(8,128)S(1)} fusion(f32[50,24,136]{2,1,0:T(8,128)S(1)} %fusion.63, f32[49,26,138]{2,1,0:T(8,128)S(1)} %get-tuple-element.33), kind=kLoop, calls=%fused_computation.104 | loop fusion | flops 288904 | bytes 2311232 | tf_op jit(solution)/shard_map/mul | solution.py:106
  57.6 2.6 %fusion.51 = f32[50,22,134]{2,1,0:T(8,128)S(1)} fusion(f32[50,24,136]{2,1,0:T(8,128)S(1)} %fusion.63, f32[50,26,138]{2,1,0:T(8,128)S(1)} %get-tuple-element.31, f32[50,26,138]{2,1,0:T(8,128)S(1)} %get-tuple-element.30, f32[50,26,138]{2,1,0:T(8,128)S(1)} %get-tuple-element.29, f32[50,26,138]{2,1,0:T(8,128)S(1)} %get-tuple-element.28, ...), kind=kLoop, calls=%fused_computation.74 | loop fusion | flops 2358400 | bytes 6476756 | tf_op jit(solution)/shard_map/jit(_where)/select_n | solution.py:208
  60.2 1.1 %fusion.70 = f32[49,20,132]{2,1,0:T(8,128)S(1)} fusion(f32[50,22,134]{2,1,0:T(8,128)S(1)} %fusion.51, f32[49,26,138]{2,1,0:T(8,128)S(1)} %get-tuple-element.33), kind=kLoop, calls=%fused_computation.102 | loop fusion | flops 258720 | bytes 2069760 | tf_op jit(solution)/shard_map/mul | solution.py:106
  61.3 2.7 %fusion.39 = f32[50,20,132]{2,1,0:T(8,128)S(1)} fusion(f32[50,22,134]{2,1,0:T(8,128)S(1)} %fusion.51, f32[50,26,138]{2,1,0:T(8,128)S(1)} %get-tuple-element.31, f32[50,26,138]{2,1,0:T(8,128)S(1)} %get-tuple-element.30, f32[50,26,138]{2,1,0:T(8,128)S(1)} %get-tuple-element.29, f32[50,26,138]{2,1,0:T(8,128)S(1)} %get-tuple-element.28, ...), kind=kLoop, calls=%fused_computation.58 | loop fusion | flops 2112000 | bytes 5800080 | tf_op jit(solution)/shard_map/jit(_where)/select_n | solution.py:208
  64.0 1.3 %fusion.69 = f32[49,18,130]{2,1,0:T(8,128)S(1)} fusion(f32[50,20,132]{2,1,0:T(8,128)S(1)} %fusion.39, f32[49,26,138]{2,1,0:T(8,128)S(1)} %get-tuple-element.33), kind=kLoop, calls=%fused_computation.100 | loop fusion | flops 229320 | bytes 1834560 | tf_op jit(solution)/shard_map/mul | solution.py:106
  65.3 2.7 %fusion.27 = f32[50,18,130]{2,1,0:T(8,128)S(1)} fusion(f32[50,20,132]{2,1,0:T(8,128)S(1)} %fusion.39, f32[50,26,138]{2,1,0:T(8,128)S(1)} %get-tuple-element.31, f32[50,26,138]{2,1,0:T(8,128)S(1)} %get-tuple-element.30, f32[50,26,138]{2,1,0:T(8,128)S(1)} %get-tuple-element.29, f32[50,26,138]{2,1,0:T(8,128)S(1)} %get-tuple-element.28, ...), kind=kLoop, calls=%fused_computation.42 | loop fusion | flops 1872000 | bytes 5140980 | tf_op jit(solution)/shard_map/jit(_where)/select_n | solution.py:208
  68.5 1.0 %fusion.83 = f32[50,16,128]{2,1,0:T(8,128)S(1)} fusion(f32[50,18,130]{2,1,0:T(8,128)S(1)} %fusion.27, f32[50,26,138]{2,1,0:T(8,128)S(1)} %get-tuple-element.31, f32[50,26,138]{2,1,0:T(8,128)S(1)} %get-tuple-element.30, f32[50,26,138]{2,1,0:T(8,128)S(1)} %get-tuple-element.29, f32[50,26,138]{2,1,0:T(8,128)S(1)} %get-tuple-element.28, ...), kind=kLoop, calls=%fused_computation.123 | loop fusion | flops 1536000 | bytes 4497408 | tf_op jit(solution)/shard_map/add | solution.py:112
  70.4 3.3 %all-to-all-start.1 = ((f32[4,32,128]{2,1,0:T(8,128)}), f32[4,32,128]{2,1,0:T(8,128)S(1)}, u32[]{:S(2)}, u32[]{:S(2)}) async-start(f32[4,32,128]{2,1,0:T(8,128)} %fusion.113), calls=%async_computation.1 | async-start | bytes 131072 | tf_op jit(solution)/shard_map/all_to_all | solution.py:213
  73.7 4.4 %all-to-all-done.1 = f32[4,32,128]{2,1,0:T(8,128)S(1)} async-done(((f32[4,32,128]{2,1,0:T(8,128)}), f32[4,32,128]{2,1,0:T(8,128)S(1)}, u32[]{:S(2)}, u32[]{:S(2)}) %all-to-all-start.1) | async-done | bytes 65568 | tf_op jit(solution)/shard_map/all_to_all | solution.py:213
  (45 shorter events, 10.2 us)
Async XLA Ops:
  0.6 5.7 %copy-start.4 = (s32[64]{0:T(128)S(1)}, s32[64]{0:T(128)}, u32[]{:S(2)}) copy-start(s32[64]{0:T(128)} %param.19) | copy-start | bytes 772
  2.9 13.2 %copy-start = (f32[50,16,128]{2,1,0:T(8,128)S(1)}, f32[50,16,128]{2,1,0:T(8,128)}, u32[]{:S(2)}) copy-start(f32[50,16,128]{2,1,0:T(8,128)} %param.16) | copy-start | bytes 1228804
  2.9 13.4 %copy-start.1 = (f32[50,16,128]{2,1,0:T(8,128)S(1)}, f32[50,16,128]{2,1,0:T(8,128)}, u32[]{:S(2)}) copy-start(f32[50,16,128]{2,1,0:T(8,128)} %param.17) | copy-start | bytes 1228804
  7.4 8.6 %all-to-all-start = ((f32[4,33,128]{2,1,0:T(8,128)}), f32[4,33,128]{2,1,0:T(8,128)S(1)}, u32[]{:S(2)}, u32[]{:S(2)}) async-start(f32[4,33,128]{2,1,0:T(8,128)} %pad_maximum_fusion.1), calls=%async_computation | async-start | bytes 163840 | tf_op jit(solution)/shard_map/all_to_all | solution.py:146
  16.3 11.3 %collective-permute-start = (f32[100,6,128]{2,1,0:T(8,128)S(1)}, f32[100,6,128]{2,1,0:T(8,128)S(1)}, u32[]{:S(2)}, u32[]{:S(2)}) collective-permute-start(f32[100,6,128]{2,1,0:T(8,128)S(1)} %get-tuple-element.34), channel_id=1, source_target_pairs={{0,4},{4,8},{8,12},{12,16},{16,20},{20,24},{24,28},{28,32},{32,36}... | collective-permute-start | bytes 921608 | tf_op jit(solution)/shard_map/ppermute | solution.py:25
  22.7 12.6 %collective-permute-start.1 = (f32[100,6,128]{2,1,0:T(8,128)S(1)}, f32[100,6,128]{2,1,0:T(8,128)S(1)}, u32[]{:S(2)}, u32[]{:S(2)}) collective-permute-start(f32[100,6,128]{2,1,0:T(8,128)S(1)} %get-tuple-element.35), channel_id=1, source_target_pairs={{4,0},{8,4},{12,8},{16,12},{20,16},{24,20},{28,24},{32,28},{36,32}... | collective-permute-start | bytes 921608 | tf_op jit(solution)/shard_map/ppermute | solution.py:27
  37.4 4.0 %collective-permute-start.2 = (f32[6,3200]{1,0:T(8,128)S(1)}, f32[6,3200]{1,0:T(8,128)S(1)}, u32[]{:S(2)}, u32[]{:S(2)}) collective-permute-start(f32[6,3200]{1,0:T(8,128)S(1)} %fusion.121), channel_id=1, source_target_pairs={{0,1},{1,2},{2,3},{4,5},{5,6},{6,7},{8,9},{9,10},{10,11},{12,13},{... | collective-permute-start | bytes 230408 | tf_op jit(solution)/shard_map/ppermute | solution.py:171
  39.6 5.4 %collective-permute-start.3 = (f32[6,3200]{1,0:T(8,128)S(1)}, f32[6,3200]{1,0:T(8,128)S(1)}, u32[]{:S(2)}, u32[]{:S(2)}) collective-permute-start(f32[6,3200]{1,0:T(8,128)S(1)} %fusion.122), channel_id=1, source_target_pairs={{1,0},{2,1},{3,2},{5,4},{6,5},{7,6},{9,8},{10,9},{11,10},{13,12},{... | collective-permute-start | bytes 230408 | tf_op jit(solution)/shard_map/ppermute | solution.py:172
  68.5 10.5 %copy-start.3 = (s32[64]{0:T(128)S(1)}, s32[64]{0:T(128)}, u32[]{:S(2)}) copy-start(s32[64]{0:T(128)} %param.20) | copy-start | bytes 772
  69.5 10.2 %copy-start.2 = (f32[50,16,128]{2,1,0:T(8,128)}, f32[50,16,128]{2,1,0:T(8,128)S(1)}, u32[]{:S(2)}) copy-start(f32[50,16,128]{2,1,0:T(8,128)S(1)} %fusion.83) | copy-start | bytes 1228804
  70.4 7.7 %all-to-all-start.1 = ((f32[4,32,128]{2,1,0:T(8,128)}), f32[4,32,128]{2,1,0:T(8,128)S(1)}, u32[]{:S(2)}, u32[]{:S(2)}) async-start(f32[4,32,128]{2,1,0:T(8,128)} %fusion.113), calls=%async_computation.1 | async-start | bytes 131072 | tf_op jit(solution)/shard_map/all_to_all | solution.py:213

commit v11 on v10

--- a/solution.py
+++ b/solution.py
@@ -161,12 +161,14 @@
     picks = jnp.arange(SWEEPS, dtype=jnp.int32)[:, None]
     lanes = jnp.arange(tile_cols, dtype=jnp.int32)[None, :]
     by_lane = (((1,), (1,)), ((), ()))
-    left_strip = lax.dot_general(
-        (lanes == picks).astype(jnp.float32), flat, by_lane, precision=highest
-    )
-    right_strip = lax.dot_general(
-        (lanes == tile_cols - SWEEPS + picks).astype(jnp.float32), flat, by_lane, precision=highest
-    )
+    spare = jnp.zeros((8 - SWEEPS % 8) % 8, jnp.int32)[:, None] - 1
+    choose = jnp.concatenate(
+        [lanes == jnp.concatenate([picks, spare]), lanes == tile_cols - SWEEPS + picks], axis=0
+    ).astype(jnp.float32)
+    strips = lax.dot_general(choose, flat, by_lane, precision=highest)
+    gap = SWEEPS + spare.shape[0]
+    left_strip = strips[:SWEEPS]
+    right_strip = strips[gap : gap + SWEEPS]
     ends = tile_count - 1
     from_left = lax.ppermute(right_strip, "gy", [(i, i + 1) for i in range(ends)])
     from_right = lax.ppermute(left_strip, "gy", [(i + 1, i) for i in range(ends)])

time: 80.3 us -> 79.5 us (0.990)
  matrix products: 8.92 us -> 8.04 us
    dot_general x2 -> x1, matrix products: 1.76 us -> 0.88 us  [local(): strips = lax.dot_general(choose, flat, by_lane, precision=highest)]
where the time goes in v11:
time: 79.5 us; the launch traced here: 78.9 us
  other arithmetic  24.1 us (30%)
  waiting for transfers between devices  22.2 us (28%)
  starting transfers between devices  19.1 us (24%)
  matrix products  8.04 us (10%)
  Pallas kernels  2.48 us (3%)
  between operations  1.57 us (2%)
  local copies, waits for them, and re-layouts  1.36 us (2%)
    select_n x5, other arithmetic, local(): field = jnp.where(inside[None, edge:-edge, edge:-edge], field, 0.0)  14.5 us
    ppermute x1, waiting for transfers between devices, with_halo(): lax.ppermute(head, axis, [((i + 1) % count, i) for i in range(ends)])  7.72 us
    mul x6, other arithmetic, lateral_core(): vertical = sides[4] * (centre[1:] - centre[:-1])  6.54 us
    ppermute x1, starting transfers between devices, with_halo(): lax.ppermute(tail, axis, [(i, (i + 1) % count) for i in range(ends)])  6.41 us
    all_to_all x1, waiting for transfers between devices, local(): lax.all_to_all(answered, 'gy', split_axis=0, concat_axis=0, tiled=True)  4.43 us
    all_to_all x1, waiting for transfers between devices, local(): lax.all_to_all(packed, 'gy', split_axis=0, concat_axis=0, tiled=True)  4.31 us
    all_to_all x1, starting transfers between devices, local(): lax.all_to_all(packed, 'gy', split_axis=0, concat_axis=0, tiled=True)  4.01 us
    ppermute x1, waiting for transfers between devices, local(): lax.ppermute(left_strip, 'gy', [(i + 1, i) for i in range(ends)])  3.62 us
  transfers between devices with their start and end apart: 6, of which 5 were waited for; matrix products, arithmetic and copies ran while one was open for 2% of the time, Pallas kernels for 0%

profile of v11, /device:TPU:249, one launch (start us, length us, event | category | flops | bytes accessed | tf_op | source)
XLA Modules:
  0.0 78.9 jit_solution(1902765545408487837)
XLA Ops:
  2.9 2.5 %shard_map.112 = f32[20,64,128]{2,1,0:T(8,128)} custom-call(f32[20,64,128]{2,1,0:T(8,128)} %bitcast.56, f32[20,64,128]{2,1,0:T(8,128)} %bitcast.55, f32[64,128]{1,0:T(8,128)} %rain_ref.1), custom_call_target="tpu_custom_call" | custom-call | flops 1966080 | bytes 1966080 | tf_op jit(solution)/shard_map/pallas_call | solution.py:67
  7.4 4.0 %all-to-all-start = ((f32[4,33,128]{2,1,0:T(8,128)}), f32[4,33,128]{2,1,0:T(8,128)S(1)}, u32[]{:S(2)}, u32[]{:S(2)}) async-start(f32[4,33,128]{2,1,0:T(8,128)} %pad_maximum_fusion.1), calls=%async_computation | async-start | bytes 163840 | tf_op jit(solution)/shard_map/all_to_all | solution.py:146
  11.7 4.3 %all-to-all-done = f32[4,33,128]{2,1,0:T(8,128)S(1)} async-done(((f32[4,33,128]{2,1,0:T(8,128)}), f32[4,33,128]{2,1,0:T(8,128)S(1)}, u32[]{:S(2)}, u32[]{:S(2)}) %all-to-all-start) | async-done | bytes 67616 | tf_op jit(solution)/shard_map/all_to_all | solution.py:146
  16.3 6.4 %collective-permute-start = (f32[100,6,128]{2,1,0:T(8,128)S(1)}, f32[100,6,128]{2,1,0:T(8,128)S(1)}, u32[]{:S(2)}, u32[]{:S(2)}) collective-permute-start(f32[100,6,128]{2,1,0:T(8,128)S(1)} %get-tuple-element.34), channel_id=1, source_target_pairs={{0,4},{4,8},{8,12},{12,16},{16,20},{20,24},{24,28},{28,32},{32,36}... | collective-permute-start | bytes 921608 | tf_op jit(solution)/shard_map/ppermute | solution.py:25
  22.8 1.9 %collective-permute-start.1 = (f32[100,6,128]{2,1,0:T(8,128)S(1)}, f32[100,6,128]{2,1,0:T(8,128)S(1)}, u32[]{:S(2)}, u32[]{:S(2)}) collective-permute-start(f32[100,6,128]{2,1,0:T(8,128)S(1)} %get-tuple-element.35), channel_id=1, source_target_pairs={{4,0},{8,4},{12,8},{16,12},{20,16},{24,20},{28,24},{32,28},{36,32}... | collective-permute-start | bytes 921608 | tf_op jit(solution)/shard_map/ppermute | solution.py:27
  25.5 2.2 %collective-permute-done = f32[100,6,128]{2,1,0:T(8,128)S(1)} collective-permute-done((f32[100,6,128]{2,1,0:T(8,128)S(1)}, f32[100,6,128]{2,1,0:T(8,128)S(1)}, u32[]{:S(2)}, u32[]{:S(2)}) %collective-permute-start) | collective-permute-done | bytes 307232 | tf_op jit(solution)/shard_map/ppermute | solution.py:25
  27.6 7.7 %collective-permute-done.1 = f32[100,6,128]{2,1,0:T(8,128)S(1)} collective-permute-done((f32[100,6,128]{2,1,0:T(8,128)S(1)}, f32[100,6,128]{2,1,0:T(8,128)S(1)}, u32[]{:S(2)}, u32[]{:S(2)}) %collective-permute-start.1) | collective-permute-done | bytes 307232 | tf_op jit(solution)/shard_map/ppermute | solution.py:27
  36.6 2.2 %collective-permute-start.2 = (f32[6,3200]{1,0:T(8,128)S(1)}, f32[6,3200]{1,0:T(8,128)S(1)}, u32[]{:S(2)}, u32[]{:S(2)}) collective-permute-start(f32[6,3200]{1,0:T(8,128)S(1)} %get-tuple-element.36), channel_id=1, source_target_pairs={{0,1},{1,2},{2,3},{4,5},{5,6},{6,7},{8,9},{9,10},{10,11},{12,13},{... | collective-permute-start | bytes 230408 | tf_op jit(solution)/shard_map/ppermute | solution.py:173
  38.8 1.3 %collective-permute-start.3 = (f32[6,3200]{1,0:T(8,128)S(1)}, f32[6,3200]{1,0:T(8,128)S(1)}, u32[]{:S(2)}, u32[]{:S(2)}) collective-permute-start(f32[6,3200]{1,0:T(8,128)S(1)} %get-tuple-element.37), channel_id=1, source_target_pairs={{1,0},{2,1},{3,2},{5,4},{6,5},{7,6},{9,8},{10,9},{11,10},{13,12},{... | collective-permute-start | bytes 230408 | tf_op jit(solution)/shard_map/ppermute | solution.py:174
  40.5 3.6 %collective-permute-done.3 = f32[6,3200]{1,0:T(8,128)S(1)} collective-permute-done((f32[6,3200]{1,0:T(8,128)S(1)}, f32[6,3200]{1,0:T(8,128)S(1)}, u32[]{:S(2)}, u32[]{:S(2)}) %collective-permute-start.3) | collective-permute-done | bytes 76832 | tf_op jit(solution)/shard_map/ppermute | solution.py:174
  44.2 2.3 %pad_add_fusion = f32[3200,140]{1,0:T(8,128)S(1)} fusion(f32[3200,128]{1,0:T(8,128)S(1)} %bitcast.53, f32[6,3200]{1,0:T(8,128)S(1)} %collective-permute-done.3, f32[6,3200]{1,0:T(8,128)S(1)} %collective-permute-done.2, pred[6,140]{1,0:T(8,128)(4,1)S(1)} %get-tuple-element.42, pred[6,140]{1,0:T(8,128)(4,1)S(1)} %get-tuple-element.43), kind=kOutput, calls=%fused_computation | convolution fusion | flops 65000080 | bytes 3585680 | tf_op jit(solution)/shard_map/dot_general | solution.py:177
  46.5 1.7 %fusion.19 = (f32[49,26,138]{2,1,0:T(8,128)S(1)}, f32[49,26,138]{2,1,0:T(8,128)S(1)}) fusion(f32[100,32,140]{2,1,0:T(8,128)S(1)} %bitcast.50), kind=kLoop, calls=%fused_computation.32 | loop fusion | flops 703248 | bytes 4219488 | tf_op jit(solution)/shard_map/mul | solution.py:106
  48.3 3.8 %fusion.6 = (f32[50,26,138]{2,1,0:T(8,128)S(1)}, f32[50,26,138]{2,1,0:T(8,128)S(1)}, f32[50,26,138]{2,1,0:T(8,128)S(1)}, f32[50,26,138]{2,1,0:T(8,128)S(1)}, f32[50,26,138]{2,1,0:T(8,128)S(1)}) fusion(f32[100,32,140]{2,1,0:T(8,128)S(1)} %bitcast.51, f32[49,26,138]{2,1,0:T(8,128)S(1)} %get-tuple-element.32, pred[26,138]{1,0:T(8,128)(4,1)S(1)} %slice.428), kind=kLoop, calls=%fused_computation.8 | loop fusion | flops 4305600 | bytes 11470836 | tf_op jit(solution)/shard_map/jit(_where)/select_n | solution.py:210
  52.1 1.0 %fusion.72 = f32[49,24,136]{2,1,0:T(8,128)S(1)} fusion(f32[50,26,138]{2,1,0:T(8,128)S(1)} %get-tuple-element.27, f32[49,26,138]{2,1,0:T(8,128)S(1)} %get-tuple-element.33), kind=kLoop, calls=%fused_computation.106 | loop fusion | flops 319872 | bytes 2558976 | tf_op jit(solution)/shard_map/mul | solution.py:106
  53.1 2.6 %fusion.63 = f32[50,24,136]{2,1,0:T(8,128)S(1)} fusion(f32[50,26,138]{2,1,0:T(8,128)S(1)} %get-tuple-element.27, f32[50,26,138]{2,1,0:T(8,128)S(1)} %get-tuple-element.31, f32[50,26,138]{2,1,0:T(8,128)S(1)} %get-tuple-element.30, f32[50,26,138]{2,1,0:T(8,128)S(1)} %get-tuple-element.29, f32[50,26,138]{2,1,0:T(8,128)S(1)} %get-tuple-element.28, ...), kind=kLoop, calls=%fused_computation.90 | loop fusion | flops 2611200 | bytes 7171008 | tf_op jit(solution)/shard_map/jit(_where)/select_n | solution.py:210
  55.7 1.0 %fusion.71 = f32[49,22,134]{2,1,0:T(8,128)S(1)} fusion(f32[50,24,136]{2,1,0:T(8,128)S(1)} %fusion.63, f32[49,26,138]{2,1,0:T(8,128)S(1)} %get-tuple-element.33), kind=kLoop, calls=%fused_computation.104 | loop fusion | flops 288904 | bytes 2311232 | tf_op jit(solution)/shard_map/mul | solution.py:106
  56.7 2.6 %fusion.51 = f32[50,22,134]{2,1,0:T(8,128)S(1)} fusion(f32[50,24,136]{2,1,0:T(8,128)S(1)} %fusion.63, f32[50,26,138]{2,1,0:T(8,128)S(1)} %get-tuple-element.31, f32[50,26,138]{2,1,0:T(8,128)S(1)} %get-tuple-element.30, f32[50,26,138]{2,1,0:T(8,128)S(1)} %get-tuple-element.29, f32[50,26,138]{2,1,0:T(8,128)S(1)} %get-tuple-element.28, ...), kind=kLoop, calls=%fused_computation.74 | loop fusion | flops 2358400 | bytes 6476756 | tf_op jit(solution)/shard_map/jit(_where)/select_n | solution.py:210
  59.4 1.1 %fusion.70 = f32[49,20,132]{2,1,0:T(8,128)S(1)} fusion(f32[50,22,134]{2,1,0:T(8,128)S(1)} %fusion.51, f32[49,26,138]{2,1,0:T(8,128)S(1)} %get-tuple-element.33), kind=kLoop, calls=%fused_computation.102 | loop fusion | flops 258720 | bytes 2069760 | tf_op jit(solution)/shard_map/mul | solution.py:106
  60.4 2.7 %fusion.39 = f32[50,20,132]{2,1,0:T(8,128)S(1)} fusion(f32[50,22,134]{2,1,0:T(8,128)S(1)} %fusion.51, f32[50,26,138]{2,1,0:T(8,128)S(1)} %get-tuple-element.31, f32[50,26,138]{2,1,0:T(8,128)S(1)} %get-tuple-element.30, f32[50,26,138]{2,1,0:T(8,128)S(1)} %get-tuple-element.29, f32[50,26,138]{2,1,0:T(8,128)S(1)} %get-tuple-element.28, ...), kind=kLoop, calls=%fused_computation.58 | loop fusion | flops 2112000 | bytes 5800080 | tf_op jit(solution)/shard_map/jit(_where)/select_n | solution.py:210
  63.2 1.3 %fusion.69 = f32[49,18,130]{2,1,0:T(8,128)S(1)} fusion(f32[50,20,132]{2,1,0:T(8,128)S(1)} %fusion.39, f32[49,26,138]{2,1,0:T(8,128)S(1)} %get-tuple-element.33), kind=kLoop, calls=%fused_computation.100 | loop fusion | flops 229320 | bytes 1834560 | tf_op jit(solution)/shard_map/mul | solution.py:106
  64.5 2.7 %fusion.27 = f32[50,18,130]{2,1,0:T(8,128)S(1)} fusion(f32[50,20,132]{2,1,0:T(8,128)S(1)} %fusion.39, f32[50,26,138]{2,1,0:T(8,128)S(1)} %get-tuple-element.31, f32[50,26,138]{2,1,0:T(8,128)S(1)} %get-tuple-element.30, f32[50,26,138]{2,1,0:T(8,128)S(1)} %get-tuple-element.29, f32[50,26,138]{2,1,0:T(8,128)S(1)} %get-tuple-element.28, ...), kind=kLoop, calls=%fused_computation.42 | loop fusion | flops 1872000 | bytes 5140980 | tf_op jit(solution)/shard_map/jit(_where)/select_n | solution.py:210
  67.6 1.0 %fusion.83 = f32[50,16,128]{2,1,0:T(8,128)S(1)} fusion(f32[50,18,130]{2,1,0:T(8,128)S(1)} %fusion.27, f32[50,26,138]{2,1,0:T(8,128)S(1)} %get-tuple-element.31, f32[50,26,138]{2,1,0:T(8,128)S(1)} %get-tuple-element.30, f32[50,26,138]{2,1,0:T(8,128)S(1)} %get-tuple-element.29, f32[50,26,138]{2,1,0:T(8,128)S(1)} %get-tuple-element.28, ...), kind=kLoop, calls=%fused_computation.123 | loop fusion | flops 1536000 | bytes 4497408 | tf_op jit(solution)/shard_map/add | solution.py:112
  69.6 3.3 %all-to-all-start.1 = ((f32[4,32,128]{2,1,0:T(8,128)}), f32[4,32,128]{2,1,0:T(8,128)S(1)}, u32[]{:S(2)}, u32[]{:S(2)}) async-start(f32[4,32,128]{2,1,0:T(8,128)} %fusion.113), calls=%async_computation.1 | async-start | bytes 131072 | tf_op jit(solution)/shard_map/all_to_all | solution.py:215
  72.9 4.4 %all-to-all-done.1 = f32[4,32,128]{2,1,0:T(8,128)S(1)} async-done(((f32[4,32,128]{2,1,0:T(8,128)}), f32[4,32,128]{2,1,0:T(8,128)S(1)}, u32[]{:S(2)}, u32[]{:S(2)}) %all-to-all-start.1) | async-done | bytes 65568 | tf_op jit(solution)/shard_map/all_to_all | solution.py:215
  (49 shorter events, 9.5 us)
Async XLA Ops:
  0.6 5.8 %copy-start.4 = (s32[64]{0:T(128)S(1)}, s32[64]{0:T(128)}, u32[]{:S(2)}) copy-start(s32[64]{0:T(128)} %param.19) | copy-start | bytes 772
  2.9 8.7 %copy-start.5 = (s32[8]{0:T(128)S(1)}, s32[8]{0:T(128)}, u32[]{:S(2)}) copy-start(s32[8]{0:T(128)} %constant.100.clone.1) | copy-start | bytes 100
  2.9 13.2 %copy-start = (f32[50,16,128]{2,1,0:T(8,128)S(1)}, f32[50,16,128]{2,1,0:T(8,128)}, u32[]{:S(2)}) copy-start(f32[50,16,128]{2,1,0:T(8,128)} %param.16) | copy-start | bytes 1228804
  2.9 13.4 %copy-start.1 = (f32[50,16,128]{2,1,0:T(8,128)S(1)}, f32[50,16,128]{2,1,0:T(8,128)}, u32[]{:S(2)}) copy-start(f32[50,16,128]{2,1,0:T(8,128)} %param.17) | copy-start | bytes 1228804
  7.4 8.6 %all-to-all-start = ((f32[4,33,128]{2,1,0:T(8,128)}), f32[4,33,128]{2,1,0:T(8,128)S(1)}, u32[]{:S(2)}, u32[]{:S(2)}) async-start(f32[4,33,128]{2,1,0:T(8,128)} %pad_maximum_fusion.1), calls=%async_computation | async-start | bytes 163840 | tf_op jit(solution)/shard_map/all_to_all | solution.py:146
  16.3 11.3 %collective-permute-start = (f32[100,6,128]{2,1,0:T(8,128)S(1)}, f32[100,6,128]{2,1,0:T(8,128)S(1)}, u32[]{:S(2)}, u32[]{:S(2)}) collective-permute-start(f32[100,6,128]{2,1,0:T(8,128)S(1)} %get-tuple-element.34), channel_id=1, source_target_pairs={{0,4},{4,8},{8,12},{12,16},{16,20},{20,24},{24,28},{28,32},{32,36}... | collective-permute-start | bytes 921608 | tf_op jit(solution)/shard_map/ppermute | solution.py:25
  22.8 12.6 %collective-permute-start.1 = (f32[100,6,128]{2,1,0:T(8,128)S(1)}, f32[100,6,128]{2,1,0:T(8,128)S(1)}, u32[]{:S(2)}, u32[]{:S(2)}) collective-permute-start(f32[100,6,128]{2,1,0:T(8,128)S(1)} %get-tuple-element.35), channel_id=1, source_target_pairs={{4,0},{8,4},{12,8},{16,12},{20,16},{24,20},{28,24},{32,28},{36,32}... | collective-permute-start | bytes 921608 | tf_op jit(solution)/shard_map/ppermute | solution.py:27
  36.6 4.0 %collective-permute-start.2 = (f32[6,3200]{1,0:T(8,128)S(1)}, f32[6,3200]{1,0:T(8,128)S(1)}, u32[]{:S(2)}, u32[]{:S(2)}) collective-permute-start(f32[6,3200]{1,0:T(8,128)S(1)} %get-tuple-element.36), channel_id=1, source_target_pairs={{0,1},{1,2},{2,3},{4,5},{5,6},{6,7},{8,9},{9,10},{10,11},{12,13},{... | collective-permute-start | bytes 230408 | tf_op jit(solution)/shard_map/ppermute | solution.py:173
  38.8 5.4 %collective-permute-start.3 = (f32[6,3200]{1,0:T(8,128)S(1)}, f32[6,3200]{1,0:T(8,128)S(1)}, u32[]{:S(2)}, u32[]{:S(2)}) collective-permute-start(f32[6,3200]{1,0:T(8,128)S(1)} %get-tuple-element.37), channel_id=1, source_target_pairs={{1,0},{2,1},{3,2},{5,4},{6,5},{7,6},{9,8},{10,9},{11,10},{13,12},{... | collective-permute-start | bytes 230408 | tf_op jit(solution)/shard_map/ppermute | solution.py:174
  67.6 10.6 %copy-start.3 = (s32[64]{0:T(128)S(1)}, s32[64]{0:T(128)}, u32[]{:S(2)}) copy-start(s32[64]{0:T(128)} %param.20) | copy-start | bytes 772
  68.7 10.2 %copy-start.2 = (f32[50,16,128]{2,1,0:T(8,128)}, f32[50,16,128]{2,1,0:T(8,128)S(1)}, u32[]{:S(2)}) copy-start(f32[50,16,128]{2,1,0:T(8,128)S(1)} %fusion.83) | copy-start | bytes 1228804
  69.6 7.7 %all-to-all-start.1 = ((f32[4,32,128]{2,1,0:T(8,128)}), f32[4,32,128]{2,1,0:T(8,128)S(1)}, u32[]{:S(2)}, u32[]{:S(2)}) async-start(f32[4,32,128]{2,1,0:T(8,128)} %fusion.113), calls=%async_computation.1 | async-start | bytes 131072 | tf_op jit(solution)/shard_map/all_to_all | solution.py:215

commit v12 on v11

--- a/solution.py
+++ b/solution.py
@@ -116,7 +116,6 @@
     highest = lax.Precision.HIGHEST
     block_count = moisture.shape[0]
     tile_count = lax.axis_size("gy")
-    capacity = block_count // 2
     tile_rows = head.shape[1]
     tile_cols = head.shape[2]
     wet = column_solve(moisture, diffusivity, rain)
@@ -125,28 +124,18 @@
     drain = diffusivity[:, -1, :] * bottom
     in_use = jnp.arange(block_count, dtype=jnp.int32) < counts[0]
     in_use_f = in_use.astype(jnp.float32)
-    to_tile = (
-        (tile_ids[:, None] == jnp.arange(tile_count, dtype=jnp.int32)[None, :]) & in_use[:, None]
-    ).astype(jnp.int32)
-    earlier = (
-        jnp.arange(block_count, dtype=jnp.int32)[None, :]
-        < jnp.arange(block_count, dtype=jnp.int32)[:, None]
-    ).astype(jnp.float32)
-    before = jnp.dot(earlier, to_tile.astype(jnp.float32), precision=highest).astype(jnp.int32)
-    slot_of = jnp.sum(before * to_tile, axis=1)
-    slot_match = slot_of[None, None, :] == jnp.arange(capacity, dtype=jnp.int32)[None, :, None]
-    placing = (to_tile.T[:, None, :] * slot_match).astype(jnp.float32)
-    outgoing = jnp.einsum("tcb,bj->tcj", placing, drain, precision=highest)
-    out_rows = (
-        jnp.einsum("tcb,b->tc", placing, (offsets + 1).astype(jnp.float32), precision=highest) - 1.0
-    )
+    tiles = jnp.arange(tile_count, dtype=jnp.int32)
+    sent = (tile_ids[None, :] == tiles[:, None]) & in_use[None, :]
+    outgoing = jnp.where(sent[:, :, None], drain[None], 0.0)
+    out_rows = jnp.where(sent, offsets[None, :].astype(jnp.float32), -1.0)
     packed = jnp.concatenate(
-        [outgoing, jnp.pad(out_rows, ((0, 0), (0, tile_cols - capacity)))[:, None, :]], axis=1
+        [outgoing, jnp.pad(out_rows, ((0, 0), (0, tile_cols - block_count)), constant_values=-1.0)[:, None, :]],
+        axis=1,
     )
     arrived = lax.all_to_all(packed, "gy", split_axis=0, concat_axis=0, tiled=True)
-    incoming = arrived[:, :capacity, :]
-    in_rows = arrived[:, capacity, :capacity]
-    slot_total = tile_count * capacity
+    incoming = arrived[:, :block_count, :]
+    in_rows = arrived[:, block_count, :block_count]
+    slot_total = tile_count * block_count
     landing = (
         in_rows.reshape(1, slot_total) == jnp.arange(tile_rows, dtype=jnp.float32)[:, None]
     ).astype(jnp.float32)
@@ -210,10 +199,12 @@
             field = jnp.where(inside[None, edge:-edge, edge:-edge], field, 0.0)
     surface = field[0]
     answered = jnp.dot(landing.T, surface, precision=highest).reshape(
-        tile_count, capacity, tile_cols
+        tile_count, block_count, tile_cols
     )
     returned = lax.all_to_all(answered, "gy", split_axis=0, concat_axis=0, tiled=True)
-    saturation = jnp.einsum("tcb,tcj->bj", placing, returned, precision=highest)
+    saturation = jnp.zeros_like(drain)
+    for tile in range(tile_count):
+        saturation = jnp.where(sent[tile][:, None], returned[tile], saturation)
     new_bottom = bottom + capillary * (saturation - in_use_f[:, None] * bottom)
     moisture_out = jnp.transpose(wet.at[depth - 1].set(new_bottom), (1, 0, 2))
     patch_hot = (patch_ids[None, :] == jnp.arange(PATCH_DEV, dtype=jnp.int32)[:, None]).astype(

time: 79.5 us -> 79.6 us (level)
  matrix products: 8.04 us -> 5.14 us
  other arithmetic: 24.1 us -> 26.5 us
  waiting for transfers between devices: 22.2 us -> 23.7 us
    dot_general x4 -> x0, matrix products: 3.09 us -> none  [the longest x1 0.97 us: local(): outgoing = jnp.einsum('tcb,bj->tcj', placing, drain, precision=highest)]
    scatter x0 -> x1, other arithmetic: none -> 1.49 us  [local(): moisture_out = jnp.transpose(wet.at[depth - 1].set(new_bottom), (1, 0, 2))]
  transfers between devices with their start and end apart: 6 -> 6, of which waited for: 5 -> 5; matrix products, arithmetic and copies ran while one was open for 2% -> 1% of each run, Pallas kernels for 0% -> 0%
where the time goes in v12:
time: 79.6 us; the launch traced here: 79.1 us
  other arithmetic  26.5 us (33%)
  waiting for transfers between devices  23.7 us (30%)
  starting transfers between devices  19.1 us (24%)
  matrix products  5.14 us (6%)
  Pallas kernels  2.49 us (3%)
  between operations  1.55 us (2%)
    select_n x5, other arithmetic, local(): field = jnp.where(inside[None, edge:-edge, edge:-edge], field, 0.0)  14.5 us
    ppermute x1, waiting for transfers between devices, with_halo(): lax.ppermute(head, axis, [((i + 1) % count, i) for i in range(ends)])  7.72 us
    mul x6, other arithmetic, lateral_core(): vertical = sides[4] * (centre[1:] - centre[:-1])  6.54 us
    ppermute x1, starting transfers between devices, with_halo(): lax.ppermute(tail, axis, [(i, (i + 1) % count) for i in range(ends)])  6.41 us
    all_to_all x1, waiting for transfers between devices, local(): lax.all_to_all(answered, 'gy', split_axis=0, concat_axis=0, tiled=True)  4.78 us
    all_to_all x1, waiting for transfers between devices, local(): lax.all_to_all(packed, 'gy', split_axis=0, concat_axis=0, tiled=True)  4.68 us
    all_to_all x1, starting transfers between devices, local(): lax.all_to_all(packed, 'gy', split_axis=0, concat_axis=0, tiled=True)  4.01 us
    ppermute x1, waiting for transfers between devices, local(): lax.ppermute(left_strip, 'gy', [(i + 1, i) for i in range(ends)])  3.67 us
  transfers between devices with their start and end apart: 6, of which 5 were waited for; matrix products, arithmetic and copies ran while one was open for 1% of the time, Pallas kernels for 0%

profile of v12, /device:TPU:249, one launch (start us, length us, event | category | flops | bytes accessed | tf_op | source)
XLA Modules:
  0.0 79.1 jit_solution(18395912342653984336)
XLA Ops:
  2.0 2.5 %shard_map.112 = f32[20,64,128]{2,1,0:T(8,128)} custom-call(f32[20,64,128]{2,1,0:T(8,128)} %bitcast.70, f32[20,64,128]{2,1,0:T(8,128)} %bitcast.69, f32[64,128]{1,0:T(8,128)} %rain_ref.1), custom_call_target="tpu_custom_call" | custom-call | flops 1966080 | bytes 1966080 | tf_op jit(solution)/shard_map/pallas_call | solution.py:67
  6.1 4.0 %all-to-all-start = ((f32[4,65,128]{2,1,0:T(8,128)}), f32[4,65,128]{2,1,0:T(8,128)S(1)}, u32[]{:S(2)}, u32[]{:S(2)}) async-start(f32[4,65,128]{2,1,0:T(8,128)} %pad_maximum_fusion.1), calls=%async_computation | async-start | bytes 294912 | tf_op jit(solution)/shard_map/all_to_all | solution.py:135
  10.3 4.7 %all-to-all-done = f32[4,65,128]{2,1,0:T(8,128)S(1)} async-done(((f32[4,65,128]{2,1,0:T(8,128)}), f32[4,65,128]{2,1,0:T(8,128)S(1)}, u32[]{:S(2)}, u32[]{:S(2)}) %all-to-all-start) | async-done | bytes 133152 | tf_op jit(solution)/shard_map/all_to_all | solution.py:135
  15.3 6.4 %collective-permute-start = (f32[100,6,128]{2,1,0:T(8,128)S(1)}, f32[100,6,128]{2,1,0:T(8,128)S(1)}, u32[]{:S(2)}, u32[]{:S(2)}) collective-permute-start(f32[100,6,128]{2,1,0:T(8,128)S(1)} %get-tuple-element.36), channel_id=1, source_target_pairs={{0,4},{4,8},{8,12},{12,16},{16,20},{20,24},{24,28},{28,32},{32,36}... | collective-permute-start | bytes 921608 | tf_op jit(solution)/shard_map/ppermute | solution.py:25
  21.8 1.9 %collective-permute-start.1 = (f32[100,6,128]{2,1,0:T(8,128)S(1)}, f32[100,6,128]{2,1,0:T(8,128)S(1)}, u32[]{:S(2)}, u32[]{:S(2)}) collective-permute-start(f32[100,6,128]{2,1,0:T(8,128)S(1)} %get-tuple-element.37), channel_id=1, source_target_pairs={{4,0},{8,4},{12,8},{16,12},{20,16},{24,20},{28,24},{32,28},{36,32}... | collective-permute-start | bytes 921608 | tf_op jit(solution)/shard_map/ppermute | solution.py:27
  23.8 2.9 %collective-permute-done = f32[100,6,128]{2,1,0:T(8,128)S(1)} collective-permute-done((f32[100,6,128]{2,1,0:T(8,128)S(1)}, f32[100,6,128]{2,1,0:T(8,128)S(1)}, u32[]{:S(2)}, u32[]{:S(2)}) %collective-permute-start) | collective-permute-done | bytes 307232 | tf_op jit(solution)/shard_map/ppermute | solution.py:25
  26.6 7.7 %collective-permute-done.1 = f32[100,6,128]{2,1,0:T(8,128)S(1)} collective-permute-done((f32[100,6,128]{2,1,0:T(8,128)S(1)}, f32[100,6,128]{2,1,0:T(8,128)S(1)}, u32[]{:S(2)}, u32[]{:S(2)}) %collective-permute-start.1) | collective-permute-done | bytes 307232 | tf_op jit(solution)/shard_map/ppermute | solution.py:27
  35.6 2.2 %collective-permute-start.2 = (f32[6,3200]{1,0:T(8,128)S(1)}, f32[6,3200]{1,0:T(8,128)S(1)}, u32[]{:S(2)}, u32[]{:S(2)}) collective-permute-start(f32[6,3200]{1,0:T(8,128)S(1)} %get-tuple-element.38), channel_id=1, source_target_pairs={{0,1},{1,2},{2,3},{4,5},{5,6},{6,7},{8,9},{9,10},{10,11},{12,13},{... | collective-permute-start | bytes 230408 | tf_op jit(solution)/shard_map/ppermute | solution.py:162
  37.8 1.3 %collective-permute-start.3 = (f32[6,3200]{1,0:T(8,128)S(1)}, f32[6,3200]{1,0:T(8,128)S(1)}, u32[]{:S(2)}, u32[]{:S(2)}) collective-permute-start(f32[6,3200]{1,0:T(8,128)S(1)} %get-tuple-element.39), channel_id=1, source_target_pairs={{1,0},{2,1},{3,2},{5,4},{6,5},{7,6},{9,8},{10,9},{11,10},{13,12},{... | collective-permute-start | bytes 230408 | tf_op jit(solution)/shard_map/ppermute | solution.py:163
  39.5 3.7 %collective-permute-done.3 = f32[6,3200]{1,0:T(8,128)S(1)} collective-permute-done((f32[6,3200]{1,0:T(8,128)S(1)}, f32[6,3200]{1,0:T(8,128)S(1)}, u32[]{:S(2)}, u32[]{:S(2)}) %collective-permute-start.3) | collective-permute-done | bytes 76832 | tf_op jit(solution)/shard_map/ppermute | solution.py:163
  43.2 2.3 %pad_add_fusion = f32[3200,140]{1,0:T(8,128)S(1)} fusion(f32[3200,128]{1,0:T(8,128)S(1)} %bitcast.67, f32[6,3200]{1,0:T(8,128)S(1)} %collective-permute-done.3, f32[6,3200]{1,0:T(8,128)S(1)} %collective-permute-done.2, pred[6,140]{1,0:T(8,128)(4,1)S(1)} %get-tuple-element.46, pred[6,140]{1,0:T(8,128)(4,1)S(1)} %get-tuple-element.47), kind=kOutput, calls=%fused_computation | convolution fusion | flops 65000080 | bytes 3585680 | tf_op jit(solution)/shard_map/dot_general | solution.py:166
  45.5 1.7 %fusion.19 = (f32[49,26,138]{2,1,0:T(8,128)S(1)}, f32[49,26,138]{2,1,0:T(8,128)S(1)}) fusion(f32[100,32,140]{2,1,0:T(8,128)S(1)} %bitcast.64), kind=kLoop, calls=%fused_computation.32 | loop fusion | flops 703248 | bytes 4219488 | tf_op jit(solution)/shard_map/mul | solution.py:106
  47.2 3.8 %fusion.6 = (f32[50,26,138]{2,1,0:T(8,128)S(1)}, f32[50,26,138]{2,1,0:T(8,128)S(1)}, f32[50,26,138]{2,1,0:T(8,128)S(1)}, f32[50,26,138]{2,1,0:T(8,128)S(1)}, f32[50,26,138]{2,1,0:T(8,128)S(1)}) fusion(f32[100,32,140]{2,1,0:T(8,128)S(1)} %bitcast.65, f32[49,26,138]{2,1,0:T(8,128)S(1)} %get-tuple-element.32, pred[26,138]{1,0:T(8,128)(4,1)S(1)} %slice.472), kind=kLoop, calls=%fused_computation.8 | loop fusion | flops 4305600 | bytes 11470836 | tf_op jit(solution)/shard_map/jit(_where)/select_n | solution.py:199
  51.1 1.0 %fusion.72 = f32[49,24,136]{2,1,0:T(8,128)S(1)} fusion(f32[50,26,138]{2,1,0:T(8,128)S(1)} %get-tuple-element.27, f32[49,26,138]{2,1,0:T(8,128)S(1)} %get-tuple-element.33), kind=kLoop, calls=%fused_computation.106 | loop fusion | flops 319872 | bytes 2558976 | tf_op jit(solution)/shard_map/mul | solution.py:106
  52.1 2.6 %fusion.63 = f32[50,24,136]{2,1,0:T(8,128)S(1)} fusion(f32[50,26,138]{2,1,0:T(8,128)S(1)} %get-tuple-element.27, f32[50,26,138]{2,1,0:T(8,128)S(1)} %get-tuple-element.31, f32[50,26,138]{2,1,0:T(8,128)S(1)} %get-tuple-element.30, f32[50,26,138]{2,1,0:T(8,128)S(1)} %get-tuple-element.29, f32[50,26,138]{2,1,0:T(8,128)S(1)} %get-tuple-element.28, ...), kind=kLoop, calls=%fused_computation.90 | loop fusion | flops 2611200 | bytes 7171008 | tf_op jit(solution)/shard_map/jit(_where)/select_n | solution.py:199
  55.7 2.6 %fusion.51 = f32[50,22,134]{2,1,0:T(8,128)S(1)} fusion(f32[50,24,136]{2,1,0:T(8,128)S(1)} %fusion.63, f32[50,26,138]{2,1,0:T(8,128)S(1)} %get-tuple-element.31, f32[50,26,138]{2,1,0:T(8,128)S(1)} %get-tuple-element.30, f32[50,26,138]{2,1,0:T(8,128)S(1)} %get-tuple-element.29, f32[50,26,138]{2,1,0:T(8,128)S(1)} %get-tuple-element.28, ...), kind=kLoop, calls=%fused_computation.74 | loop fusion | flops 2358400 | bytes 6476756 | tf_op jit(solution)/shard_map/jit(_where)/select_n | solution.py:199
  58.4 1.1 %fusion.70 = f32[49,20,132]{2,1,0:T(8,128)S(1)} fusion(f32[50,22,134]{2,1,0:T(8,128)S(1)} %fusion.51, f32[49,26,138]{2,1,0:T(8,128)S(1)} %get-tuple-element.33), kind=kLoop, calls=%fused_computation.102 | loop fusion | flops 258720 | bytes 2069760 | tf_op jit(solution)/shard_map/mul | solution.py:106
  59.4 2.7 %fusion.39 = f32[50,20,132]{2,1,0:T(8,128)S(1)} fusion(f32[50,22,134]{2,1,0:T(8,128)S(1)} %fusion.51, f32[50,26,138]{2,1,0:T(8,128)S(1)} %get-tuple-element.31, f32[50,26,138]{2,1,0:T(8,128)S(1)} %get-tuple-element.30, f32[50,26,138]{2,1,0:T(8,128)S(1)} %get-tuple-element.29, f32[50,26,138]{2,1,0:T(8,128)S(1)} %get-tuple-element.28, ...), kind=kLoop, calls=%fused_computation.58 | loop fusion | flops 2112000 | bytes 5800080 | tf_op jit(solution)/shard_map/jit(_where)/select_n | solution.py:199
  62.2 1.3 %fusion.69 = f32[49,18,130]{2,1,0:T(8,128)S(1)} fusion(f32[50,20,132]{2,1,0:T(8,128)S(1)} %fusion.39, f32[49,26,138]{2,1,0:T(8,128)S(1)} %get-tuple-element.33), kind=kLoop, calls=%fused_computation.100 | loop fusion | flops 229320 | bytes 1834560 | tf_op jit(solution)/shard_map/mul | solution.py:106
  63.5 2.7 %fusion.27 = f32[50,18,130]{2,1,0:T(8,128)S(1)} fusion(f32[50,20,132]{2,1,0:T(8,128)S(1)} %fusion.39, f32[50,26,138]{2,1,0:T(8,128)S(1)} %get-tuple-element.31, f32[50,26,138]{2,1,0:T(8,128)S(1)} %get-tuple-element.30, f32[50,26,138]{2,1,0:T(8,128)S(1)} %get-tuple-element.29, f32[50,26,138]{2,1,0:T(8,128)S(1)} %get-tuple-element.28, ...), kind=kLoop, calls=%fused_computation.42 | loop fusion | flops 1872000 | bytes 5140980 | tf_op jit(solution)/shard_map/jit(_where)/select_n | solution.py:199
  66.6 1.0 %fusion.81 = f32[50,16,128]{2,1,0:T(8,128)S(1)} fusion(f32[50,18,130]{2,1,0:T(8,128)S(1)} %fusion.27, f32[50,26,138]{2,1,0:T(8,128)S(1)} %get-tuple-element.31, f32[50,26,138]{2,1,0:T(8,128)S(1)} %get-tuple-element.30, f32[50,26,138]{2,1,0:T(8,128)S(1)} %get-tuple-element.29, f32[50,26,138]{2,1,0:T(8,128)S(1)} %get-tuple-element.28, ...), kind=kLoop, calls=%fused_computation.119 | loop fusion | flops 1536000 | bytes 4497408 | tf_op jit(solution)/shard_map/add | solution.py:112
  68.6 3.3 %all-to-all-start.1 = ((f32[4,64,128]{2,1,0:T(8,128)}), f32[4,64,128]{2,1,0:T(8,128)S(1)}, u32[]{:S(2)}, u32[]{:S(2)}) async-start(f32[4,64,128]{2,1,0:T(8,128)} %fusion.104), calls=%async_computation.1 | async-start | bytes 262144 | tf_op jit(solution)/shard_map/all_to_all | solution.py:204
  72.0 4.8 %all-to-all-done.1 = f32[4,64,128]{2,1,0:T(8,128)S(1)} async-done(((f32[4,64,128]{2,1,0:T(8,128)}), f32[4,64,128]{2,1,0:T(8,128)S(1)}, u32[]{:S(2)}, u32[]{:S(2)}) %all-to-all-start.1) | async-done | bytes 131104 | tf_op jit(solution)/shard_map/all_to_all | solution.py:204
  76.7 1.5 %add_dynamic-update-slice_fusion = f32[20,64,128]{2,1,0:T(8,128)} fusion(f32[20,64,128]{2,1,0:T(8,128)} %shard_map.112, f32[4,64,128]{2,1,0:T(8,128)S(1)} %all-to-all-done.1, f32[64]{0:T(128)S(1)} %fusion.132, pred[64]{0:T(512)(128)(4,1)S(1)} %get-tuple-element.45, pred[64]{0:T(512)(128)(4,1)S(1)} %get-tuple-element.43, ...), kind=kLoop, calls=%fused_computation.147 | loop fusion | flops 65536 | bytes 197120 | tf_op jit(solution)/shard_map/scatter | solution.py:209
  (47 shorter events, 7.7 us)
Async XLA Ops:
  0.6 4.6 %copy-start.3 = (s32[64]{0:T(128)S(1)}, s32[64]{0:T(128)}, u32[]{:S(2)}) copy-start(s32[64]{0:T(128)} %param.18) | copy-start | bytes 772
  2.0 8.2 %copy-start.5 = (s32[8]{0:T(128)S(1)}, s32[8]{0:T(128)}, u32[]{:S(2)}) copy-start(s32[8]{0:T(128)} %constant.97.clone.1) | copy-start | bytes 100
  2.0 13.1 %copy-start = (f32[50,16,128]{2,1,0:T(8,128)S(1)}, f32[50,16,128]{2,1,0:T(8,128)}, u32[]{:S(2)}) copy-start(f32[50,16,128]{2,1,0:T(8,128)} %param.16) | copy-start | bytes 1228804
  2.0 13.3 %copy-start.1 = (f32[50,16,128]{2,1,0:T(8,128)S(1)}, f32[50,16,128]{2,1,0:T(8,128)}, u32[]{:S(2)}) copy-start(f32[50,16,128]{2,1,0:T(8,128)} %param.17) | copy-start | bytes 1228804
  6.1 8.9 %all-to-all-start = ((f32[4,65,128]{2,1,0:T(8,128)}), f32[4,65,128]{2,1,0:T(8,128)S(1)}, u32[]{:S(2)}, u32[]{:S(2)}) async-start(f32[4,65,128]{2,1,0:T(8,128)} %pad_maximum_fusion.1), calls=%async_computation | async-start | bytes 294912 | tf_op jit(solution)/shard_map/all_to_all | solution.py:135
  15.3 11.3 %collective-permute-start = (f32[100,6,128]{2,1,0:T(8,128)S(1)}, f32[100,6,128]{2,1,0:T(8,128)S(1)}, u32[]{:S(2)}, u32[]{:S(2)}) collective-permute-start(f32[100,6,128]{2,1,0:T(8,128)S(1)} %get-tuple-element.36), channel_id=1, source_target_pairs={{0,4},{4,8},{8,12},{12,16},{16,20},{20,24},{24,28},{28,32},{32,36}... | collective-permute-start | bytes 921608 | tf_op jit(solution)/shard_map/ppermute | solution.py:25
  21.8 12.6 %collective-permute-start.1 = (f32[100,6,128]{2,1,0:T(8,128)S(1)}, f32[100,6,128]{2,1,0:T(8,128)S(1)}, u32[]{:S(2)}, u32[]{:S(2)}) collective-permute-start(f32[100,6,128]{2,1,0:T(8,128)S(1)} %get-tuple-element.37), channel_id=1, source_target_pairs={{4,0},{8,4},{12,8},{16,12},{20,16},{24,20},{28,24},{32,28},{36,32}... | collective-permute-start | bytes 921608 | tf_op jit(solution)/shard_map/ppermute | solution.py:27
  35.6 3.9 %collective-permute-start.2 = (f32[6,3200]{1,0:T(8,128)S(1)}, f32[6,3200]{1,0:T(8,128)S(1)}, u32[]{:S(2)}, u32[]{:S(2)}) collective-permute-start(f32[6,3200]{1,0:T(8,128)S(1)} %get-tuple-element.38), channel_id=1, source_target_pairs={{0,1},{1,2},{2,3},{4,5},{5,6},{6,7},{8,9},{9,10},{10,11},{12,13},{... | collective-permute-start | bytes 230408 | tf_op jit(solution)/shard_map/ppermute | solution.py:162
  37.8 5.4 %collective-permute-start.3 = (f32[6,3200]{1,0:T(8,128)S(1)}, f32[6,3200]{1,0:T(8,128)S(1)}, u32[]{:S(2)}, u32[]{:S(2)}) collective-permute-start(f32[6,3200]{1,0:T(8,128)S(1)} %get-tuple-element.39), channel_id=1, source_target_pairs={{1,0},{2,1},{3,2},{5,4},{6,5},{7,6},{9,8},{10,9},{11,10},{13,12},{... | collective-permute-start | bytes 230408 | tf_op jit(solution)/shard_map/ppermute | solution.py:163
  66.6 11.6 %copy-start.4 = (s32[64]{0:T(128)S(1)}, s32[64]{0:T(128)}, u32[]{:S(2)}) copy-start(s32[64]{0:T(128)} %param.20) | copy-start | bytes 772
  67.7 11.4 %copy-start.2 = (f32[50,16,128]{2,1,0:T(8,128)}, f32[50,16,128]{2,1,0:T(8,128)S(1)}, u32[]{:S(2)}) copy-start(f32[50,16,128]{2,1,0:T(8,128)S(1)} %fusion.81) | copy-start | bytes 1228804
  68.6 8.1 %all-to-all-start.1 = ((f32[4,64,128]{2,1,0:T(8,128)}), f32[4,64,128]{2,1,0:T(8,128)S(1)}, u32[]{:S(2)}, u32[]{:S(2)}) async-start(f32[4,64,128]{2,1,0:T(8,128)} %fusion.104), calls=%async_computation.1 | async-start | bytes 262144 | tf_op jit(solution)/shard_map/all_to_all | solution.py:204

commit v13 on v11

--- a/solution.py
+++ b/solution.py
@@ -154,7 +154,21 @@
     field = head.at[0].add(recharge)
     layers = field.shape[0]
     stacked = jnp.concatenate([field, conductivity], axis=0)
-    rowed = with_halo(stacked, (("gx", 1),), SWEEPS)
+    rows_count = lax.axis_size("gx")
+    rows_end = rows_count - 1
+    dense = (stacked.shape[0] * SWEEPS, tile_cols)
+    from_above = lax.ppermute(
+        stacked[:, tile_rows - SWEEPS :, :].reshape(dense),
+        "gx",
+        [(i, i + 1) for i in range(rows_end)],
+    )
+    from_below = lax.ppermute(
+        stacked[:, :SWEEPS, :].reshape(dense), "gx", [(i + 1, i) for i in range(rows_end)]
+    )
+    halo_shape = (stacked.shape[0], SWEEPS, tile_cols)
+    rowed = jnp.concatenate(
+        [from_above.reshape(halo_shape), stacked, from_below.reshape(halo_shape)], axis=1
+    )
     halo_rows = rowed.shape[1]
     tiled_rows = -(-halo_rows // 8) * 8
     flat = jnp.pad(rowed, ((0, 0), (0, tiled_rows - halo_rows), (0, 0))).reshape(-1, tile_cols)

time: 79.5 us -> 78.5 us (0.987)
  waiting for transfers between devices: 22.2 us -> 21.1 us
    ppermute x2, waiting for transfers between devices: 9.89 us -> 8.75 us  [the longest x1 7.72 us: local(): lax.ppermute(stacked[:, :SWEEPS, :].reshape(dense), 'gx', [(i + 1, i) for...]
where the time goes in v13:
time: 78.5 us; the launch traced here: 77.9 us
  other arithmetic  24.1 us (31%)
  waiting for transfers between devices  21.1 us (27%)
  starting transfers between devices  19.1 us (24%)
  matrix products  8.04 us (10%)
  Pallas kernels  2.48 us (3%)
  between operations  1.59 us (2%)
  local copies, waits for them, and re-layouts  1.51 us (2%)
    select_n x5, other arithmetic, local(): field = jnp.where(inside[None, edge:-edge, edge:-edge], field, 0.0)  14.5 us
    ppermute x1, waiting for transfers between devices, local(): lax.ppermute(stacked[:, :SWEEPS, :].reshape(dense), 'gx', [(i + 1, i) for...  7.72 us
    mul x6, other arithmetic, lateral_core(): vertical = sides[4] * (centre[1:] - centre[:-1])  6.54 us
    ppermute x1, starting transfers between devices, local(): lax.ppermute(stacked[:, tile_rows - SWEEPS:, :].reshape(dense), 'gx', [(i...  6.41 us
    all_to_all x1, waiting for transfers between devices, local(): lax.all_to_all(answered, 'gy', split_axis=0, concat_axis=0, tiled=True)  4.43 us
    all_to_all x1, waiting for transfers between devices, local(): lax.all_to_all(packed, 'gy', split_axis=0, concat_axis=0, tiled=True)  4.31 us
    all_to_all x1, starting transfers between devices, local(): lax.all_to_all(packed, 'gy', split_axis=0, concat_axis=0, tiled=True)  4.01 us
    ppermute x1, waiting for transfers between devices, local(): lax.ppermute(left_strip, 'gy', [(i + 1, i) for i in range(ends)])  3.62 us
  transfers between devices with their start and end apart: 6, of which 5 were waited for; matrix products, arithmetic and copies ran while one was open for 2% of the time, Pallas kernels for 0%

profile of v13, /device:TPU:249, one launch (start us, length us, event | category | flops | bytes accessed | tf_op | source)
XLA Modules:
  0.0 77.9 jit_solution(11288906097746386240)
XLA Ops:
  2.9 2.5 %shard_map.112 = f32[20,64,128]{2,1,0:T(8,128)} custom-call(f32[20,64,128]{2,1,0:T(8,128)} %bitcast.56, f32[20,64,128]{2,1,0:T(8,128)} %bitcast.55, f32[64,128]{1,0:T(8,128)} %rain_ref.1), custom_call_target="tpu_custom_call" | custom-call | flops 1966080 | bytes 1966080 | tf_op jit(solution)/shard_map/pallas_call | solution.py:67
  7.4 4.0 %all-to-all-start = ((f32[4,33,128]{2,1,0:T(8,128)}), f32[4,33,128]{2,1,0:T(8,128)S(1)}, u32[]{:S(2)}, u32[]{:S(2)}) async-start(f32[4,33,128]{2,1,0:T(8,128)} %pad_maximum_fusion.1), calls=%async_computation | async-start | bytes 163840 | tf_op jit(solution)/shard_map/all_to_all | solution.py:146
  11.7 4.3 %all-to-all-done = f32[4,33,128]{2,1,0:T(8,128)S(1)} async-done(((f32[4,33,128]{2,1,0:T(8,128)}), f32[4,33,128]{2,1,0:T(8,128)S(1)}, u32[]{:S(2)}, u32[]{:S(2)}) %all-to-all-start) | async-done | bytes 67616 | tf_op jit(solution)/shard_map/all_to_all | solution.py:146
  16.4 6.4 %collective-permute-start = (f32[600,128]{1,0:T(8,128)S(1)}, f32[600,128]{1,0:T(8,128)S(1)}, u32[]{:S(2)}, u32[]{:S(2)}) collective-permute-start(f32[600,128]{1,0:T(8,128)S(1)} %reshape.212), channel_id=1, source_target_pairs={{0,4},{4,8},{8,12},{12,16},{16,20},{20,24},{24,28},{28,32},{32,36}... | collective-permute-start | bytes 921608 | tf_op jit(solution)/shard_map/ppermute | solution.py:160
  22.8 1.9 %collective-permute-start.1 = (f32[600,128]{1,0:T(8,128)S(1)}, f32[600,128]{1,0:T(8,128)S(1)}, u32[]{:S(2)}, u32[]{:S(2)}) collective-permute-start(f32[600,128]{1,0:T(8,128)S(1)} %reshape.214), channel_id=1, source_target_pairs={{4,0},{8,4},{12,8},{16,12},{20,16},{24,20},{28,24},{32,28},{36,32}... | collective-permute-start | bytes 921608 | tf_op jit(solution)/shard_map/ppermute | solution.py:165
  25.6 1.0 %collective-permute-done = f32[600,128]{1,0:T(8,128)S(1)} collective-permute-done((f32[600,128]{1,0:T(8,128)S(1)}, f32[600,128]{1,0:T(8,128)S(1)}, u32[]{:S(2)}, u32[]{:S(2)}) %collective-permute-start) | collective-permute-done | bytes 307232 | tf_op jit(solution)/shard_map/ppermute | solution.py:160
  26.6 7.7 %collective-permute-done.1 = f32[600,128]{1,0:T(8,128)S(1)} collective-permute-done((f32[600,128]{1,0:T(8,128)S(1)}, f32[600,128]{1,0:T(8,128)S(1)}, u32[]{:S(2)}, u32[]{:S(2)}) %collective-permute-start.1) | collective-permute-done | bytes 307232 | tf_op jit(solution)/shard_map/ppermute | solution.py:165
  35.6 2.2 %collective-permute-start.2 = (f32[6,3200]{1,0:T(8,128)S(1)}, f32[6,3200]{1,0:T(8,128)S(1)}, u32[]{:S(2)}, u32[]{:S(2)}) collective-permute-start(f32[6,3200]{1,0:T(8,128)S(1)} %get-tuple-element.36), channel_id=1, source_target_pairs={{0,1},{1,2},{2,3},{4,5},{5,6},{6,7},{8,9},{9,10},{10,11},{12,13},{... | collective-permute-start | bytes 230408 | tf_op jit(solution)/shard_map/ppermute | solution.py:187
  37.8 1.3 %collective-permute-start.3 = (f32[6,3200]{1,0:T(8,128)S(1)}, f32[6,3200]{1,0:T(8,128)S(1)}, u32[]{:S(2)}, u32[]{:S(2)}) collective-permute-start(f32[6,3200]{1,0:T(8,128)S(1)} %get-tuple-element.37), channel_id=1, source_target_pairs={{1,0},{2,1},{3,2},{5,4},{6,5},{7,6},{9,8},{10,9},{11,10},{13,12},{... | collective-permute-start | bytes 230408 | tf_op jit(solution)/shard_map/ppermute | solution.py:188
  39.6 3.6 %collective-permute-done.3 = f32[6,3200]{1,0:T(8,128)S(1)} collective-permute-done((f32[6,3200]{1,0:T(8,128)S(1)}, f32[6,3200]{1,0:T(8,128)S(1)}, u32[]{:S(2)}, u32[]{:S(2)}) %collective-permute-start.3) | collective-permute-done | bytes 76832 | tf_op jit(solution)/shard_map/ppermute | solution.py:188
  43.2 2.3 %convolution_add_fusion = f32[3200,140]{1,0:T(8,128)S(1)} fusion(f32[3200,128]{1,0:T(8,128)S(1)} %bitcast.53, f32[6,3200]{1,0:T(8,128)S(1)} %collective-permute-done.3, f32[6,3200]{1,0:T(8,128)S(1)} %collective-permute-done.2, pred[6,140]{1,0:T(8,128)(4,1)S(1)} %get-tuple-element.42, pred[6,140]{1,0:T(8,128)(4,1)S(1)} %get-tuple-element.43), kind=kOutput, calls=%fused_computation | convolution fusion | flops 65000080 | bytes 3585680 | tf_op jit(solution)/shard_map/dot_general | solution.py:191
  45.5 1.7 %fusion.19 = (f32[49,26,138]{2,1,0:T(8,128)S(1)}, f32[49,26,138]{2,1,0:T(8,128)S(1)}) fusion(f32[100,32,140]{2,1,0:T(8,128)S(1)} %bitcast.50), kind=kLoop, calls=%fused_computation.32 | loop fusion | flops 703248 | bytes 4219488 | tf_op jit(solution)/shard_map/mul | solution.py:106
  47.3 3.8 %fusion.6 = (f32[50,26,138]{2,1,0:T(8,128)S(1)}, f32[50,26,138]{2,1,0:T(8,128)S(1)}, f32[50,26,138]{2,1,0:T(8,128)S(1)}, f32[50,26,138]{2,1,0:T(8,128)S(1)}, f32[50,26,138]{2,1,0:T(8,128)S(1)}) fusion(f32[100,32,140]{2,1,0:T(8,128)S(1)} %bitcast.51, f32[49,26,138]{2,1,0:T(8,128)S(1)} %get-tuple-element.32, pred[26,138]{1,0:T(8,128)(4,1)S(1)} %slice.428), kind=kLoop, calls=%fused_computation.8 | loop fusion | flops 4305600 | bytes 11470836 | tf_op jit(solution)/shard_map/jit(_where)/select_n | solution.py:224
  51.1 1.0 %fusion.72 = f32[49,24,136]{2,1,0:T(8,128)S(1)} fusion(f32[50,26,138]{2,1,0:T(8,128)S(1)} %get-tuple-element.27, f32[49,26,138]{2,1,0:T(8,128)S(1)} %get-tuple-element.33), kind=kLoop, calls=%fused_computation.106 | loop fusion | flops 319872 | bytes 2558976 | tf_op jit(solution)/shard_map/mul | solution.py:106
  52.1 2.6 %fusion.63 = f32[50,24,136]{2,1,0:T(8,128)S(1)} fusion(f32[50,26,138]{2,1,0:T(8,128)S(1)} %get-tuple-element.27, f32[50,26,138]{2,1,0:T(8,128)S(1)} %get-tuple-element.31, f32[50,26,138]{2,1,0:T(8,128)S(1)} %get-tuple-element.30, f32[50,26,138]{2,1,0:T(8,128)S(1)} %get-tuple-element.29, f32[50,26,138]{2,1,0:T(8,128)S(1)} %get-tuple-element.28, ...), kind=kLoop, calls=%fused_computation.90 | loop fusion | flops 2611200 | bytes 7171008 | tf_op jit(solution)/shard_map/jit(_where)/select_n | solution.py:224
  54.7 1.0 %fusion.71 = f32[49,22,134]{2,1,0:T(8,128)S(1)} fusion(f32[50,24,136]{2,1,0:T(8,128)S(1)} %fusion.63, f32[49,26,138]{2,1,0:T(8,128)S(1)} %get-tuple-element.33), kind=kLoop, calls=%fused_computation.104 | loop fusion | flops 288904 | bytes 2311232 | tf_op jit(solution)/shard_map/mul | solution.py:106
  55.8 2.6 %fusion.51 = f32[50,22,134]{2,1,0:T(8,128)S(1)} fusion(f32[50,24,136]{2,1,0:T(8,128)S(1)} %fusion.63, f32[50,26,138]{2,1,0:T(8,128)S(1)} %get-tuple-element.31, f32[50,26,138]{2,1,0:T(8,128)S(1)} %get-tuple-element.30, f32[50,26,138]{2,1,0:T(8,128)S(1)} %get-tuple-element.29, f32[50,26,138]{2,1,0:T(8,128)S(1)} %get-tuple-element.28, ...), kind=kLoop, calls=%fused_computation.74 | loop fusion | flops 2358400 | bytes 6476756 | tf_op jit(solution)/shard_map/jit(_where)/select_n | solution.py:224
  58.4 1.1 %fusion.70 = f32[49,20,132]{2,1,0:T(8,128)S(1)} fusion(f32[50,22,134]{2,1,0:T(8,128)S(1)} %fusion.51, f32[49,26,138]{2,1,0:T(8,128)S(1)} %get-tuple-element.33), kind=kLoop, calls=%fused_computation.102 | loop fusion | flops 258720 | bytes 2069760 | tf_op jit(solution)/shard_map/mul | solution.py:106
  59.5 2.7 %fusion.39 = f32[50,20,132]{2,1,0:T(8,128)S(1)} fusion(f32[50,22,134]{2,1,0:T(8,128)S(1)} %fusion.51, f32[50,26,138]{2,1,0:T(8,128)S(1)} %get-tuple-element.31, f32[50,26,138]{2,1,0:T(8,128)S(1)} %get-tuple-element.30, f32[50,26,138]{2,1,0:T(8,128)S(1)} %get-tuple-element.29, f32[50,26,138]{2,1,0:T(8,128)S(1)} %get-tuple-element.28, ...), kind=kLoop, calls=%fused_computation.58 | loop fusion | flops 2112000 | bytes 5800080 | tf_op jit(solution)/shard_map/jit(_where)/select_n | solution.py:224
  62.2 1.3 %fusion.69 = f32[49,18,130]{2,1,0:T(8,128)S(1)} fusion(f32[50,20,132]{2,1,0:T(8,128)S(1)} %fusion.39, f32[49,26,138]{2,1,0:T(8,128)S(1)} %get-tuple-element.33), kind=kLoop, calls=%fused_computation.100 | loop fusion | flops 229320 | bytes 1834560 | tf_op jit(solution)/shard_map/mul | solution.py:106
  63.5 2.7 %fusion.27 = f32[50,18,130]{2,1,0:T(8,128)S(1)} fusion(f32[50,20,132]{2,1,0:T(8,128)S(1)} %fusion.39, f32[50,26,138]{2,1,0:T(8,128)S(1)} %get-tuple-element.31, f32[50,26,138]{2,1,0:T(8,128)S(1)} %get-tuple-element.30, f32[50,26,138]{2,1,0:T(8,128)S(1)} %get-tuple-element.29, f32[50,26,138]{2,1,0:T(8,128)S(1)} %get-tuple-element.28, ...), kind=kLoop, calls=%fused_computation.42 | loop fusion | flops 1872000 | bytes 5140980 | tf_op jit(solution)/shard_map/jit(_where)/select_n | solution.py:224
  66.7 1.0 %fusion.83 = f32[50,16,128]{2,1,0:T(8,128)S(1)} fusion(f32[50,18,130]{2,1,0:T(8,128)S(1)} %fusion.27, f32[50,26,138]{2,1,0:T(8,128)S(1)} %get-tuple-element.31, f32[50,26,138]{2,1,0:T(8,128)S(1)} %get-tuple-element.30, f32[50,26,138]{2,1,0:T(8,128)S(1)} %get-tuple-element.29, f32[50,26,138]{2,1,0:T(8,128)S(1)} %get-tuple-element.28, ...), kind=kLoop, calls=%fused_computation.123 | loop fusion | flops 1536000 | bytes 4497408 | tf_op jit(solution)/shard_map/add | solution.py:112
  68.6 3.3 %all-to-all-start.1 = ((f32[4,32,128]{2,1,0:T(8,128)}), f32[4,32,128]{2,1,0:T(8,128)S(1)}, u32[]{:S(2)}, u32[]{:S(2)}) async-start(f32[4,32,128]{2,1,0:T(8,128)} %fusion.110), calls=%async_computation.1 | async-start | bytes 131072 | tf_op jit(solution)/shard_map/all_to_all | solution.py:229
  71.9 4.4 %all-to-all-done.1 = f32[4,32,128]{2,1,0:T(8,128)S(1)} async-done(((f32[4,32,128]{2,1,0:T(8,128)}), f32[4,32,128]{2,1,0:T(8,128)S(1)}, u32[]{:S(2)}, u32[]{:S(2)}) %all-to-all-start.1) | async-done | bytes 65568 | tf_op jit(solution)/shard_map/all_to_all | solution.py:229
  (53 shorter events, 9.6 us)
Async XLA Ops:
  0.6 5.8 %copy-start.4 = (s32[64]{0:T(128)S(1)}, s32[64]{0:T(128)}, u32[]{:S(2)}) copy-start(s32[64]{0:T(128)} %param.19) | copy-start | bytes 772
  2.9 8.7 %copy-start.5 = (s32[8]{0:T(128)S(1)}, s32[8]{0:T(128)}, u32[]{:S(2)}) copy-start(s32[8]{0:T(128)} %constant.100.clone.1) | copy-start | bytes 100
  2.9 13.2 %copy-start = (f32[50,16,128]{2,1,0:T(8,128)S(1)}, f32[50,16,128]{2,1,0:T(8,128)}, u32[]{:S(2)}) copy-start(f32[50,16,128]{2,1,0:T(8,128)} %param.16) | copy-start | bytes 1228804
  2.9 13.4 %copy-start.1 = (f32[50,16,128]{2,1,0:T(8,128)S(1)}, f32[50,16,128]{2,1,0:T(8,128)}, u32[]{:S(2)}) copy-start(f32[50,16,128]{2,1,0:T(8,128)} %param.17) | copy-start | bytes 1228804
  7.4 8.6 %all-to-all-start = ((f32[4,33,128]{2,1,0:T(8,128)}), f32[4,33,128]{2,1,0:T(8,128)S(1)}, u32[]{:S(2)}, u32[]{:S(2)}) async-start(f32[4,33,128]{2,1,0:T(8,128)} %pad_maximum_fusion.1), calls=%async_computation | async-start | bytes 163840 | tf_op jit(solution)/shard_map/all_to_all | solution.py:146
  16.4 10.2 %collective-permute-start = (f32[600,128]{1,0:T(8,128)S(1)}, f32[600,128]{1,0:T(8,128)S(1)}, u32[]{:S(2)}, u32[]{:S(2)}) collective-permute-start(f32[600,128]{1,0:T(8,128)S(1)} %reshape.212), channel_id=1, source_target_pairs={{0,4},{4,8},{8,12},{12,16},{16,20},{20,24},{24,28},{28,32},{32,36}... | collective-permute-start | bytes 921608 | tf_op jit(solution)/shard_map/ppermute | solution.py:160
  22.8 11.5 %collective-permute-start.1 = (f32[600,128]{1,0:T(8,128)S(1)}, f32[600,128]{1,0:T(8,128)S(1)}, u32[]{:S(2)}, u32[]{:S(2)}) collective-permute-start(f32[600,128]{1,0:T(8,128)S(1)} %reshape.214), channel_id=1, source_target_pairs={{4,0},{8,4},{12,8},{16,12},{20,16},{24,20},{28,24},{32,28},{36,32}... | collective-permute-start | bytes 921608 | tf_op jit(solution)/shard_map/ppermute | solution.py:165
  35.6 4.0 %collective-permute-start.2 = (f32[6,3200]{1,0:T(8,128)S(1)}, f32[6,3200]{1,0:T(8,128)S(1)}, u32[]{:S(2)}, u32[]{:S(2)}) collective-permute-start(f32[6,3200]{1,0:T(8,128)S(1)} %get-tuple-element.36), channel_id=1, source_target_pairs={{0,1},{1,2},{2,3},{4,5},{5,6},{6,7},{8,9},{9,10},{10,11},{12,13},{... | collective-permute-start | bytes 230408 | tf_op jit(solution)/shard_map/ppermute | solution.py:187
  37.8 5.4 %collective-permute-start.3 = (f32[6,3200]{1,0:T(8,128)S(1)}, f32[6,3200]{1,0:T(8,128)S(1)}, u32[]{:S(2)}, u32[]{:S(2)}) collective-permute-start(f32[6,3200]{1,0:T(8,128)S(1)} %get-tuple-element.37), channel_id=1, source_target_pairs={{1,0},{2,1},{3,2},{5,4},{6,5},{7,6},{9,8},{10,9},{11,10},{13,12},{... | collective-permute-start | bytes 230408 | tf_op jit(solution)/shard_map/ppermute | solution.py:188
  66.6 10.6 %copy-start.3 = (s32[64]{0:T(128)S(1)}, s32[64]{0:T(128)}, u32[]{:S(2)}) copy-start(s32[64]{0:T(128)} %param.20) | copy-start | bytes 772
  67.7 10.2 %copy-start.2 = (f32[50,16,128]{2,1,0:T(8,128)}, f32[50,16,128]{2,1,0:T(8,128)S(1)}, u32[]{:S(2)}) copy-start(f32[50,16,128]{2,1,0:T(8,128)S(1)} %fusion.83) | copy-start | bytes 1228804
  68.6 7.7 %all-to-all-start.1 = ((f32[4,32,128]{2,1,0:T(8,128)}), f32[4,32,128]{2,1,0:T(8,128)S(1)}, u32[]{:S(2)}, u32[]{:S(2)}) async-start(f32[4,32,128]{2,1,0:T(8,128)} %fusion.110), calls=%async_computation.1 | async-start | bytes 131072 | tf_op jit(solution)/shard_map/all_to_all | solution.py:229

commit v14 on v13

--- a/solution.py
+++ b/solution.py
@@ -184,8 +184,14 @@
     left_strip = strips[:SWEEPS]
     right_strip = strips[gap : gap + SWEEPS]
     ends = tile_count - 1
-    from_left = lax.ppermute(right_strip, "gy", [(i, i + 1) for i in range(ends)])
-    from_right = lax.ppermute(left_strip, "gy", [(i + 1, i) for i in range(ends)])
+    strip_shape = left_strip.shape
+    packed_strip = (strip_shape[0] * strip_shape[1] // tile_cols, tile_cols)
+    from_left = lax.ppermute(
+        right_strip.reshape(packed_strip), "gy", [(i, i + 1) for i in range(ends)]
+    ).reshape(strip_shape)
+    from_right = lax.ppermute(
+        left_strip.reshape(packed_strip), "gy", [(i + 1, i) for i in range(ends)]
+    ).reshape(strip_shape)
     width = tile_cols + 2 * SWEEPS
     out_lanes = jnp.arange(width, dtype=jnp.int32)[None, :]
     side = jnp.dot(

time: 78.5 us -> 78.3 us (level)
  no operation moved by 1% of the time
where the time goes in v14:
time: 78.3 us; the launch traced here: 77.7 us
  other arithmetic  24.1 us (31%)
  waiting for transfers between devices  20.8 us (27%)
  starting transfers between devices  19.1 us (24%)
  matrix products  8.02 us (10%)
  Pallas kernels  2.48 us (3%)
  between operations  1.62 us (2%)
  local copies, waits for them, and re-layouts  1.57 us (2%)
    select_n x5, other arithmetic, local(): field = jnp.where(inside[None, edge:-edge, edge:-edge], field, 0.0)  14.5 us
    ppermute x1, waiting for transfers between devices, local(): lax.ppermute(stacked[:, :SWEEPS, :].reshape(dense), 'gx', [(i + 1, i) for...  7.72 us
    mul x6, other arithmetic, lateral_core(): vertical = sides[4] * (centre[1:] - centre[:-1])  6.54 us
    ppermute x1, starting transfers between devices, local(): lax.ppermute(stacked[:, tile_rows - SWEEPS:, :].reshape(dense), 'gx', [(i...  6.41 us
    all_to_all x1, waiting for transfers between devices, local(): lax.all_to_all(answered, 'gy', split_axis=0, concat_axis=0, tiled=True)  4.43 us
    all_to_all x1, waiting for transfers between devices, local(): lax.all_to_all(packed, 'gy', split_axis=0, concat_axis=0, tiled=True)  4.31 us
    all_to_all x1, starting transfers between devices, local(): lax.all_to_all(packed, 'gy', split_axis=0, concat_axis=0, tiled=True)  4.01 us
    ppermute x1, waiting for transfers between devices, local(): lax.ppermute(left_strip.reshape(packed_strip), 'gy', [(i + 1, i) for i in...  3.33 us
  transfers between devices with their start and end apart: 6, of which 5 were waited for; matrix products, arithmetic and copies ran while one was open for 2% of the time, Pallas kernels for 0%

profile of v14, /device:TPU:249, one launch (start us, length us, event | category | flops | bytes accessed | tf_op | source)
XLA Modules:
  0.0 77.7 jit_solution(14089299532796004657)
XLA Ops:
  2.9 2.5 %shard_map.112 = f32[20,64,128]{2,1,0:T(8,128)} custom-call(f32[20,64,128]{2,1,0:T(8,128)} %bitcast.56, f32[20,64,128]{2,1,0:T(8,128)} %bitcast.55, f32[64,128]{1,0:T(8,128)} %rain_ref.1), custom_call_target="tpu_custom_call" | custom-call | flops 1966080 | bytes 1966080 | tf_op jit(solution)/shard_map/pallas_call | solution.py:67
  7.4 4.0 %all-to-all-start = ((f32[4,33,128]{2,1,0:T(8,128)}), f32[4,33,128]{2,1,0:T(8,128)S(1)}, u32[]{:S(2)}, u32[]{:S(2)}) async-start(f32[4,33,128]{2,1,0:T(8,128)} %pad_maximum_fusion.1), calls=%async_computation | async-start | bytes 163840 | tf_op jit(solution)/shard_map/all_to_all | solution.py:146
  11.7 4.3 %all-to-all-done = f32[4,33,128]{2,1,0:T(8,128)S(1)} async-done(((f32[4,33,128]{2,1,0:T(8,128)}), f32[4,33,128]{2,1,0:T(8,128)S(1)}, u32[]{:S(2)}, u32[]{:S(2)}) %all-to-all-start) | async-done | bytes 67616 | tf_op jit(solution)/shard_map/all_to_all | solution.py:146
  16.4 6.4 %collective-permute-start = (f32[600,128]{1,0:T(8,128)S(1)}, f32[600,128]{1,0:T(8,128)S(1)}, u32[]{:S(2)}, u32[]{:S(2)}) collective-permute-start(f32[600,128]{1,0:T(8,128)S(1)} %reshape.224), channel_id=1, source_target_pairs={{0,4},{4,8},{8,12},{12,16},{16,20},{20,24},{24,28},{28,32},{32,36}... | collective-permute-start | bytes 921608 | tf_op jit(solution)/shard_map/ppermute | solution.py:160
  22.8 1.9 %collective-permute-start.1 = (f32[600,128]{1,0:T(8,128)S(1)}, f32[600,128]{1,0:T(8,128)S(1)}, u32[]{:S(2)}, u32[]{:S(2)}) collective-permute-start(f32[600,128]{1,0:T(8,128)S(1)} %reshape.226), channel_id=1, source_target_pairs={{4,0},{8,4},{12,8},{16,12},{20,16},{24,20},{28,24},{32,28},{36,32}... | collective-permute-start | bytes 921608 | tf_op jit(solution)/shard_map/ppermute | solution.py:165
  25.6 1.0 %collective-permute-done = f32[600,128]{1,0:T(8,128)S(1)} collective-permute-done((f32[600,128]{1,0:T(8,128)S(1)}, f32[600,128]{1,0:T(8,128)S(1)}, u32[]{:S(2)}, u32[]{:S(2)}) %collective-permute-start) | collective-permute-done | bytes 307232 | tf_op jit(solution)/shard_map/ppermute | solution.py:160
  26.6 7.7 %collective-permute-done.1 = f32[600,128]{1,0:T(8,128)S(1)} collective-permute-done((f32[600,128]{1,0:T(8,128)S(1)}, f32[600,128]{1,0:T(8,128)S(1)}, u32[]{:S(2)}, u32[]{:S(2)}) %collective-permute-start.1) | collective-permute-done | bytes 307232 | tf_op jit(solution)/shard_map/ppermute | solution.py:165
  35.6 2.2 %collective-permute-start.2 = (f32[150,128]{1,0:T(8,128)S(1)}, f32[150,128]{1,0:T(8,128)S(1)}, u32[]{:S(2)}, u32[]{:S(2)}) collective-permute-start(f32[150,128]{1,0:T(8,128)S(1)} %reshape.229), channel_id=1, source_target_pairs={{0,1},{1,2},{2,3},{4,5},{5,6},{6,7},{8,9},{9,10},{10,11},{12,13},{... | collective-permute-start | bytes 230408 | tf_op jit(solution)/shard_map/ppermute | solution.py:189
  37.8 1.3 %collective-permute-start.3 = (f32[150,128]{1,0:T(8,128)S(1)}, f32[150,128]{1,0:T(8,128)S(1)}, u32[]{:S(2)}, u32[]{:S(2)}) collective-permute-start(f32[150,128]{1,0:T(8,128)S(1)} %reshape.231), channel_id=1, source_target_pairs={{1,0},{2,1},{3,2},{5,4},{6,5},{7,6},{9,8},{10,9},{11,10},{13,12},{... | collective-permute-start | bytes 230408 | tf_op jit(solution)/shard_map/ppermute | solution.py:192
  39.6 3.3 %collective-permute-done.3 = f32[150,128]{1,0:T(8,128)S(1)} collective-permute-done((f32[150,128]{1,0:T(8,128)S(1)}, f32[150,128]{1,0:T(8,128)S(1)}, u32[]{:S(2)}, u32[]{:S(2)}) %collective-permute-start.3) | collective-permute-done | bytes 76832 | tf_op jit(solution)/shard_map/ppermute | solution.py:192
  43.0 2.3 %convolution_add_fusion = f32[3200,140]{1,0:T(8,128)S(1)} fusion(f32[3200,128]{1,0:T(8,128)S(1)} %bitcast.53, f32[6,3200]{1,0:T(8,128)S(1)} %reshape.232, f32[6,3200]{1,0:T(8,128)S(1)} %reshape.230, pred[6,140]{1,0:T(8,128)(4,1)S(1)} %get-tuple-element.42, pred[6,140]{1,0:T(8,128)(4,1)S(1)} %get-tuple-element.43), kind=kOutput, calls=%fused_computation | convolution fusion | flops 65000080 | bytes 3585680 | tf_op jit(solution)/shard_map/dot_general | solution.py:197
  45.3 1.7 %fusion.19 = (f32[49,26,138]{2,1,0:T(8,128)S(1)}, f32[49,26,138]{2,1,0:T(8,128)S(1)}) fusion(f32[100,32,140]{2,1,0:T(8,128)S(1)} %bitcast.50), kind=kLoop, calls=%fused_computation.32 | loop fusion | flops 703248 | bytes 4219488 | tf_op jit(solution)/shard_map/mul | solution.py:106
  47.1 3.8 %fusion.6 = (f32[50,26,138]{2,1,0:T(8,128)S(1)}, f32[50,26,138]{2,1,0:T(8,128)S(1)}, f32[50,26,138]{2,1,0:T(8,128)S(1)}, f32[50,26,138]{2,1,0:T(8,128)S(1)}, f32[50,26,138]{2,1,0:T(8,128)S(1)}) fusion(f32[100,32,140]{2,1,0:T(8,128)S(1)} %bitcast.51, f32[49,26,138]{2,1,0:T(8,128)S(1)} %get-tuple-element.32, pred[26,138]{1,0:T(8,128)(4,1)S(1)} %slice.428), kind=kLoop, calls=%fused_computation.8 | loop fusion | flops 4305600 | bytes 11470836 | tf_op jit(solution)/shard_map/jit(_where)/select_n | solution.py:230
  50.9 1.0 %fusion.72 = f32[49,24,136]{2,1,0:T(8,128)S(1)} fusion(f32[50,26,138]{2,1,0:T(8,128)S(1)} %get-tuple-element.27, f32[49,26,138]{2,1,0:T(8,128)S(1)} %get-tuple-element.33), kind=kLoop, calls=%fused_computation.106 | loop fusion | flops 319872 | bytes 2558976 | tf_op jit(solution)/shard_map/mul | solution.py:106
  51.9 2.6 %fusion.63 = f32[50,24,136]{2,1,0:T(8,128)S(1)} fusion(f32[50,26,138]{2,1,0:T(8,128)S(1)} %get-tuple-element.27, f32[50,26,138]{2,1,0:T(8,128)S(1)} %get-tuple-element.31, f32[50,26,138]{2,1,0:T(8,128)S(1)} %get-tuple-element.30, f32[50,26,138]{2,1,0:T(8,128)S(1)} %get-tuple-element.29, f32[50,26,138]{2,1,0:T(8,128)S(1)} %get-tuple-element.28, ...), kind=kLoop, calls=%fused_computation.90 | loop fusion | flops 2611200 | bytes 7171008 | tf_op jit(solution)/shard_map/jit(_where)/select_n | solution.py:230
  54.5 1.0 %fusion.71 = f32[49,22,134]{2,1,0:T(8,128)S(1)} fusion(f32[50,24,136]{2,1,0:T(8,128)S(1)} %fusion.63, f32[49,26,138]{2,1,0:T(8,128)S(1)} %get-tuple-element.33), kind=kLoop, calls=%fused_computation.104 | loop fusion | flops 288904 | bytes 2311232 | tf_op jit(solution)/shard_map/mul | solution.py:106
  55.6 2.6 %fusion.51 = f32[50,22,134]{2,1,0:T(8,128)S(1)} fusion(f32[50,24,136]{2,1,0:T(8,128)S(1)} %fusion.63, f32[50,26,138]{2,1,0:T(8,128)S(1)} %get-tuple-element.31, f32[50,26,138]{2,1,0:T(8,128)S(1)} %get-tuple-element.30, f32[50,26,138]{2,1,0:T(8,128)S(1)} %get-tuple-element.29, f32[50,26,138]{2,1,0:T(8,128)S(1)} %get-tuple-element.28, ...), kind=kLoop, calls=%fused_computation.74 | loop fusion | flops 2358400 | bytes 6476756 | tf_op jit(solution)/shard_map/jit(_where)/select_n | solution.py:230
  58.2 1.1 %fusion.70 = f32[49,20,132]{2,1,0:T(8,128)S(1)} fusion(f32[50,22,134]{2,1,0:T(8,128)S(1)} %fusion.51, f32[49,26,138]{2,1,0:T(8,128)S(1)} %get-tuple-element.33), kind=kLoop, calls=%fused_computation.102 | loop fusion | flops 258720 | bytes 2069760 | tf_op jit(solution)/shard_map/mul | solution.py:106
  59.2 2.7 %fusion.39 = f32[50,20,132]{2,1,0:T(8,128)S(1)} fusion(f32[50,22,134]{2,1,0:T(8,128)S(1)} %fusion.51, f32[50,26,138]{2,1,0:T(8,128)S(1)} %get-tuple-element.31, f32[50,26,138]{2,1,0:T(8,128)S(1)} %get-tuple-element.30, f32[50,26,138]{2,1,0:T(8,128)S(1)} %get-tuple-element.29, f32[50,26,138]{2,1,0:T(8,128)S(1)} %get-tuple-element.28, ...), kind=kLoop, calls=%fused_computation.58 | loop fusion | flops 2112000 | bytes 5800080 | tf_op jit(solution)/shard_map/jit(_where)/select_n | solution.py:230
  62.0 1.3 %fusion.69 = f32[49,18,130]{2,1,0:T(8,128)S(1)} fusion(f32[50,20,132]{2,1,0:T(8,128)S(1)} %fusion.39, f32[49,26,138]{2,1,0:T(8,128)S(1)} %get-tuple-element.33), kind=kLoop, calls=%fused_computation.100 | loop fusion | flops 229320 | bytes 1834560 | tf_op jit(solution)/shard_map/mul | solution.py:106
  63.3 2.7 %fusion.27 = f32[50,18,130]{2,1,0:T(8,128)S(1)} fusion(f32[50,20,132]{2,1,0:T(8,128)S(1)} %fusion.39, f32[50,26,138]{2,1,0:T(8,128)S(1)} %get-tuple-element.31, f32[50,26,138]{2,1,0:T(8,128)S(1)} %get-tuple-element.30, f32[50,26,138]{2,1,0:T(8,128)S(1)} %get-tuple-element.29, f32[50,26,138]{2,1,0:T(8,128)S(1)} %get-tuple-element.28, ...), kind=kLoop, calls=%fused_computation.42 | loop fusion | flops 1872000 | bytes 5140980 | tf_op jit(solution)/shard_map/jit(_where)/select_n | solution.py:230
  66.4 1.0 %fusion.83 = f32[50,16,128]{2,1,0:T(8,128)S(1)} fusion(f32[50,18,130]{2,1,0:T(8,128)S(1)} %fusion.27, f32[50,26,138]{2,1,0:T(8,128)S(1)} %get-tuple-element.31, f32[50,26,138]{2,1,0:T(8,128)S(1)} %get-tuple-element.30, f32[50,26,138]{2,1,0:T(8,128)S(1)} %get-tuple-element.29, f32[50,26,138]{2,1,0:T(8,128)S(1)} %get-tuple-element.28, ...), kind=kLoop, calls=%fused_computation.123 | loop fusion | flops 1536000 | bytes 4497408 | tf_op jit(solution)/shard_map/add | solution.py:112
  68.4 3.3 %all-to-all-start.1 = ((f32[4,32,128]{2,1,0:T(8,128)}), f32[4,32,128]{2,1,0:T(8,128)S(1)}, u32[]{:S(2)}, u32[]{:S(2)}) async-start(f32[4,32,128]{2,1,0:T(8,128)} %fusion.110), calls=%async_computation.1 | async-start | bytes 131072 | tf_op jit(solution)/shard_map/all_to_all | solution.py:235
  71.7 4.4 %all-to-all-done.1 = f32[4,32,128]{2,1,0:T(8,128)S(1)} async-done(((f32[4,32,128]{2,1,0:T(8,128)}), f32[4,32,128]{2,1,0:T(8,128)S(1)}, u32[]{:S(2)}, u32[]{:S(2)}) %all-to-all-start.1) | async-done | bytes 65568 | tf_op jit(solution)/shard_map/all_to_all | solution.py:235
  (57 shorter events, 9.7 us)
Async XLA Ops:
  0.6 5.8 %copy-start.4 = (s32[64]{0:T(128)S(1)}, s32[64]{0:T(128)}, u32[]{:S(2)}) copy-start(s32[64]{0:T(128)} %param.19) | copy-start | bytes 772
  2.9 8.7 %copy-start.5 = (s32[8]{0:T(128)S(1)}, s32[8]{0:T(128)}, u32[]{:S(2)}) copy-start(s32[8]{0:T(128)} %constant.100.clone.1) | copy-start | bytes 100
  2.9 13.2 %copy-start = (f32[50,16,128]{2,1,0:T(8,128)S(1)}, f32[50,16,128]{2,1,0:T(8,128)}, u32[]{:S(2)}) copy-start(f32[50,16,128]{2,1,0:T(8,128)} %param.16) | copy-start | bytes 1228804
  2.9 13.4 %copy-start.1 = (f32[50,16,128]{2,1,0:T(8,128)S(1)}, f32[50,16,128]{2,1,0:T(8,128)}, u32[]{:S(2)}) copy-start(f32[50,16,128]{2,1,0:T(8,128)} %param.17) | copy-start | bytes 1228804
  7.4 8.6 %all-to-all-start = ((f32[4,33,128]{2,1,0:T(8,128)}), f32[4,33,128]{2,1,0:T(8,128)S(1)}, u32[]{:S(2)}, u32[]{:S(2)}) async-start(f32[4,33,128]{2,1,0:T(8,128)} %pad_maximum_fusion.1), calls=%async_computation | async-start | bytes 163840 | tf_op jit(solution)/shard_map/all_to_all | solution.py:146
  16.4 10.2 %collective-permute-start = (f32[600,128]{1,0:T(8,128)S(1)}, f32[600,128]{1,0:T(8,128)S(1)}, u32[]{:S(2)}, u32[]{:S(2)}) collective-permute-start(f32[600,128]{1,0:T(8,128)S(1)} %reshape.224), channel_id=1, source_target_pairs={{0,4},{4,8},{8,12},{12,16},{16,20},{20,24},{24,28},{28,32},{32,36}... | collective-permute-start | bytes 921608 | tf_op jit(solution)/shard_map/ppermute | solution.py:160
  22.8 11.5 %collective-permute-start.1 = (f32[600,128]{1,0:T(8,128)S(1)}, f32[600,128]{1,0:T(8,128)S(1)}, u32[]{:S(2)}, u32[]{:S(2)}) collective-permute-start(f32[600,128]{1,0:T(8,128)S(1)} %reshape.226), channel_id=1, source_target_pairs={{4,0},{8,4},{12,8},{16,12},{20,16},{24,20},{28,24},{32,28},{36,32}... | collective-permute-start | bytes 921608 | tf_op jit(solution)/shard_map/ppermute | solution.py:165
  35.6 4.0 %collective-permute-start.2 = (f32[150,128]{1,0:T(8,128)S(1)}, f32[150,128]{1,0:T(8,128)S(1)}, u32[]{:S(2)}, u32[]{:S(2)}) collective-permute-start(f32[150,128]{1,0:T(8,128)S(1)} %reshape.229), channel_id=1, source_target_pairs={{0,1},{1,2},{2,3},{4,5},{5,6},{6,7},{8,9},{9,10},{10,11},{12,13},{... | collective-permute-start | bytes 230408 | tf_op jit(solution)/shard_map/ppermute | solution.py:189
  37.8 5.1 %collective-permute-start.3 = (f32[150,128]{1,0:T(8,128)S(1)}, f32[150,128]{1,0:T(8,128)S(1)}, u32[]{:S(2)}, u32[]{:S(2)}) collective-permute-start(f32[150,128]{1,0:T(8,128)S(1)} %reshape.231), channel_id=1, source_target_pairs={{1,0},{2,1},{3,2},{5,4},{6,5},{7,6},{9,8},{10,9},{11,10},{13,12},{... | collective-permute-start | bytes 230408 | tf_op jit(solution)/shard_map/ppermute | solution.py:192
  66.4 10.6 %copy-start.3 = (s32[64]{0:T(128)S(1)}, s32[64]{0:T(128)}, u32[]{:S(2)}) copy-start(s32[64]{0:T(128)} %param.20) | copy-start | bytes 772
  67.5 10.2 %copy-start.2 = (f32[50,16,128]{2,1,0:T(8,128)}, f32[50,16,128]{2,1,0:T(8,128)S(1)}, u32[]{:S(2)}) copy-start(f32[50,16,128]{2,1,0:T(8,128)S(1)} %fusion.83) | copy-start | bytes 1228804
  68.4 7.7 %all-to-all-start.1 = ((f32[4,32,128]{2,1,0:T(8,128)}), f32[4,32,128]{2,1,0:T(8,128)S(1)}, u32[]{:S(2)}, u32[]{:S(2)}) async-start(f32[4,32,128]{2,1,0:T(8,128)} %fusion.110), calls=%async_computation.1 | async-start | bytes 131072 | tf_op jit(solution)/shard_map/all_to_all | solution.py:235

commit v15 on v14

--- a/solution.py
+++ b/solution.py
@@ -31,7 +31,7 @@
     return cells
 
 
-def column_kernel(moist_ref, diff_ref, rain_ref, wet_ref, ratio_ref):
+def column_kernel(moist_ref, diff_ref, rain_ref, wet_ref, drain_ref, ratio_ref):
     depth = moist_ref.shape[0]
 
     def body(g, carry):
@@ -53,6 +53,7 @@
             ratio_ref[layer_k, rows, :] = ratio
             wet_ref[layer_k, rows, :] = carried
         solved = carried
+        drain_ref[...] = diff_ref[depth - 1, rows, :] * carried
         for layer_k in range(depth - 2, -1, -1):
             solved = wet_ref[layer_k, rows, :] + ratio_ref[layer_k, rows, :] * solved
             wet_ref[layer_k, rows, :] = solved
@@ -66,9 +67,12 @@
     layered = (depth, blocks, lanes)
     return pl.pallas_call(
         column_kernel,
-        out_shape=jax.ShapeDtypeStruct(layered, jnp.float32),
+        out_shape=(
+            jax.ShapeDtypeStruct(layered, jnp.float32),
+            jax.ShapeDtypeStruct((blocks, lanes), jnp.float32),
+        ),
         in_specs=[pl.BlockSpec(memory_space=pltpu.VMEM)] * 3,
-        out_specs=pl.BlockSpec(memory_space=pltpu.VMEM),
+        out_specs=(pl.BlockSpec(memory_space=pltpu.VMEM), pl.BlockSpec(memory_space=pltpu.VMEM)),
         scratch_shapes=[pltpu.VMEM(layered, jnp.float32)],
         cost_estimate=pl.CostEstimate(
             flops=12 * blocks * depth * lanes, transcendentals=0, bytes_accessed=12 * blocks * depth * lanes
@@ -119,10 +123,9 @@
     capacity = block_count // 2
     tile_rows = head.shape[1]
     tile_cols = head.shape[2]
-    wet = column_solve(moisture, diffusivity, rain)
+    wet, drain = column_solve(moisture, diffusivity, rain)
     depth = moisture.shape[1]
     bottom = wet[depth - 1]
-    drain = diffusivity[:, -1, :] * bottom
     in_use = jnp.arange(block_count, dtype=jnp.int32) < counts[0]
     in_use_f = in_use.astype(jnp.float32)
     to_tile = (

time: 78.3 us -> 78.3 us (level)
  no operation moved by 1% of the time
where the time goes in v15:
time: 78.3 us; the launch traced here: 77.7 us
  other arithmetic  24.1 us (31%)
  waiting for transfers between devices  20.8 us (27%)
  starting transfers between devices  19.1 us (24%)
  matrix products  8.01 us (10%)
  Pallas kernels  2.42 us (3%)
  between operations  1.69 us (2%)
  local copies, waits for them, and re-layouts  1.56 us (2%)
    select_n x5, other arithmetic, local(): field = jnp.where(inside[None, edge:-edge, edge:-edge], field, 0.0)  14.5 us
    ppermute x1, waiting for transfers between devices, local(): lax.ppermute(stacked[:, :SWEEPS, :].reshape(dense), 'gx', [(i + 1, i) for...  7.72 us
    mul x6, other arithmetic, lateral_core(): vertical = sides[4] * (centre[1:] - centre[:-1])  6.54 us
    ppermute x1, starting transfers between devices, local(): lax.ppermute(stacked[:, tile_rows - SWEEPS:, :].reshape(dense), 'gx', [(i...  6.4 us
    all_to_all x1, waiting for transfers between devices, local(): lax.all_to_all(packed, 'gy', split_axis=0, concat_axis=0, tiled=True)  4.39 us
    all_to_all x1, starting transfers between devices, local(): lax.all_to_all(packed, 'gy', split_axis=0, concat_axis=0, tiled=True)  4.01 us
    all_to_all x1, waiting for transfers between devices, local(): lax.all_to_all(answered, 'gy', split_axis=0, concat_axis=0, tiled=True)  3.66 us
    ppermute x1, waiting for transfers between devices, local(): lax.ppermute(left_strip.reshape(packed_strip), 'gy', [(i + 1, i) for i in...  3.33 us
  transfers between devices with their start and end apart: 6, of which 5 were waited for; matrix products, arithmetic and copies ran while one was open for 2% of the time, Pallas kernels for 0%

profile of v15, /device:TPU:249, one launch (start us, length us, event | category | flops | bytes accessed | tf_op | source)
XLA Modules:
  0.0 77.7 jit_solution(10041573944960278433)
XLA Ops:
  3.0 2.4 %shard_map.112 = (f32[20,64,128]{2,1,0:T(8,128)}, f32[64,128]{1,0:T(8,128)}) custom-call(f32[20,64,128]{2,1,0:T(8,128)} %bitcast.55, f32[20,64,128]{2,1,0:T(8,128)} %bitcast.56, f32[64,128]{1,0:T(8,128)} %rain_ref.1), custom_call_target="tpu_custom_call" | custom-call | flops 1966080 | bytes 1966080 | tf_op jit(solution)/shard_map/pallas_call | solution.py:68
  7.4 4.0 %all-to-all-start = ((f32[4,33,128]{2,1,0:T(8,128)}), f32[4,33,128]{2,1,0:T(8,128)S(1)}, u32[]{:S(2)}, u32[]{:S(2)}) async-start(f32[4,33,128]{2,1,0:T(8,128)} %pad_maximum_fusion.1), calls=%async_computation | async-start | bytes 163840 | tf_op jit(solution)/shard_map/all_to_all | solution.py:149
  11.6 4.4 %all-to-all-done = f32[4,33,128]{2,1,0:T(8,128)S(1)} async-done(((f32[4,33,128]{2,1,0:T(8,128)}), f32[4,33,128]{2,1,0:T(8,128)S(1)}, u32[]{:S(2)}, u32[]{:S(2)}) %all-to-all-start) | async-done | bytes 67616 | tf_op jit(solution)/shard_map/all_to_all | solution.py:149
  16.4 6.4 %collective-permute-start = (f32[600,128]{1,0:T(8,128)S(1)}, f32[600,128]{1,0:T(8,128)S(1)}, u32[]{:S(2)}, u32[]{:S(2)}) collective-permute-start(f32[600,128]{1,0:T(8,128)S(1)} %reshape.224), channel_id=1, source_target_pairs={{0,4},{4,8},{8,12},{12,16},{16,20},{20,24},{24,28},{28,32},{32,36}... | collective-permute-start | bytes 921608 | tf_op jit(solution)/shard_map/ppermute | solution.py:163
  22.8 1.9 %collective-permute-start.1 = (f32[600,128]{1,0:T(8,128)S(1)}, f32[600,128]{1,0:T(8,128)S(1)}, u32[]{:S(2)}, u32[]{:S(2)}) collective-permute-start(f32[600,128]{1,0:T(8,128)S(1)} %reshape.226), channel_id=1, source_target_pairs={{4,0},{8,4},{12,8},{16,12},{20,16},{24,20},{28,24},{32,28},{36,32}... | collective-permute-start | bytes 921608 | tf_op jit(solution)/shard_map/ppermute | solution.py:168
  24.8 1.7 %collective-permute-done = f32[600,128]{1,0:T(8,128)S(1)} collective-permute-done((f32[600,128]{1,0:T(8,128)S(1)}, f32[600,128]{1,0:T(8,128)S(1)}, u32[]{:S(2)}, u32[]{:S(2)}) %collective-permute-start) | collective-permute-done | bytes 307232 | tf_op jit(solution)/shard_map/ppermute | solution.py:163
  26.6 7.7 %collective-permute-done.1 = f32[600,128]{1,0:T(8,128)S(1)} collective-permute-done((f32[600,128]{1,0:T(8,128)S(1)}, f32[600,128]{1,0:T(8,128)S(1)}, u32[]{:S(2)}, u32[]{:S(2)}) %collective-permute-start.1) | collective-permute-done | bytes 307232 | tf_op jit(solution)/shard_map/ppermute | solution.py:168
  35.6 2.2 %collective-permute-start.2 = (f32[150,128]{1,0:T(8,128)S(1)}, f32[150,128]{1,0:T(8,128)S(1)}, u32[]{:S(2)}, u32[]{:S(2)}) collective-permute-start(f32[150,128]{1,0:T(8,128)S(1)} %reshape.229), channel_id=1, source_target_pairs={{0,1},{1,2},{2,3},{4,5},{5,6},{6,7},{8,9},{9,10},{10,11},{12,13},{... | collective-permute-start | bytes 230408 | tf_op jit(solution)/shard_map/ppermute | solution.py:192
  37.8 1.3 %collective-permute-start.3 = (f32[150,128]{1,0:T(8,128)S(1)}, f32[150,128]{1,0:T(8,128)S(1)}, u32[]{:S(2)}, u32[]{:S(2)}) collective-permute-start(f32[150,128]{1,0:T(8,128)S(1)} %reshape.231), channel_id=1, source_target_pairs={{1,0},{2,1},{3,2},{5,4},{6,5},{7,6},{9,8},{10,9},{11,10},{13,12},{... | collective-permute-start | bytes 230408 | tf_op jit(solution)/shard_map/ppermute | solution.py:195
  39.6 3.3 %collective-permute-done.3 = f32[150,128]{1,0:T(8,128)S(1)} collective-permute-done((f32[150,128]{1,0:T(8,128)S(1)}, f32[150,128]{1,0:T(8,128)S(1)}, u32[]{:S(2)}, u32[]{:S(2)}) %collective-permute-start.3) | collective-permute-done | bytes 76832 | tf_op jit(solution)/shard_map/ppermute | solution.py:195
  43.0 2.3 %convolution_add_fusion = f32[3200,140]{1,0:T(8,128)S(1)} fusion(f32[3200,128]{1,0:T(8,128)S(1)} %bitcast.54, f32[6,3200]{1,0:T(8,128)S(1)} %reshape.232, f32[6,3200]{1,0:T(8,128)S(1)} %reshape.230, pred[6,140]{1,0:T(8,128)(4,1)S(1)} %get-tuple-element.46, pred[6,140]{1,0:T(8,128)(4,1)S(1)} %get-tuple-element.47), kind=kOutput, calls=%fused_computation | convolution fusion | flops 65000080 | bytes 3585680 | tf_op jit(solution)/shard_map/dot_general | solution.py:200
  45.3 1.7 %fusion.19 = (f32[49,26,138]{2,1,0:T(8,128)S(1)}, f32[49,26,138]{2,1,0:T(8,128)S(1)}) fusion(f32[100,32,140]{2,1,0:T(8,128)S(1)} %bitcast.51), kind=kLoop, calls=%fused_computation.32 | loop fusion | flops 703248 | bytes 4219488 | tf_op jit(solution)/shard_map/mul | solution.py:110
  47.0 3.8 %fusion.6 = (f32[50,26,138]{2,1,0:T(8,128)S(1)}, f32[50,26,138]{2,1,0:T(8,128)S(1)}, f32[50,26,138]{2,1,0:T(8,128)S(1)}, f32[50,26,138]{2,1,0:T(8,128)S(1)}, f32[50,26,138]{2,1,0:T(8,128)S(1)}) fusion(f32[100,32,140]{2,1,0:T(8,128)S(1)} %bitcast.52, f32[49,26,138]{2,1,0:T(8,128)S(1)} %get-tuple-element.36, pred[26,138]{1,0:T(8,128)(4,1)S(1)} %slice.424), kind=kLoop, calls=%fused_computation.8 | loop fusion | flops 4305600 | bytes 11470836 | tf_op jit(solution)/shard_map/jit(_where)/select_n | solution.py:233
  50.8 1.0 %fusion.72 = f32[49,24,136]{2,1,0:T(8,128)S(1)} fusion(f32[50,26,138]{2,1,0:T(8,128)S(1)} %get-tuple-element.31, f32[49,26,138]{2,1,0:T(8,128)S(1)} %get-tuple-element.37), kind=kLoop, calls=%fused_computation.106 | loop fusion | flops 319872 | bytes 2558976 | tf_op jit(solution)/shard_map/mul | solution.py:110
  51.9 2.6 %fusion.63 = f32[50,24,136]{2,1,0:T(8,128)S(1)} fusion(f32[50,26,138]{2,1,0:T(8,128)S(1)} %get-tuple-element.31, f32[50,26,138]{2,1,0:T(8,128)S(1)} %get-tuple-element.35, f32[50,26,138]{2,1,0:T(8,128)S(1)} %get-tuple-element.34, f32[50,26,138]{2,1,0:T(8,128)S(1)} %get-tuple-element.33, f32[50,26,138]{2,1,0:T(8,128)S(1)} %get-tuple-element.32, ...), kind=kLoop, calls=%fused_computation.90 | loop fusion | flops 2611200 | bytes 7171008 | tf_op jit(solution)/shard_map/jit(_where)/select_n | solution.py:233
  54.5 1.0 %fusion.71 = f32[49,22,134]{2,1,0:T(8,128)S(1)} fusion(f32[50,24,136]{2,1,0:T(8,128)S(1)} %fusion.63, f32[49,26,138]{2,1,0:T(8,128)S(1)} %get-tuple-element.37), kind=kLoop, calls=%fused_computation.104 | loop fusion | flops 288904 | bytes 2311232 | tf_op jit(solution)/shard_map/mul | solution.py:110
  55.5 2.6 %fusion.51 = f32[50,22,134]{2,1,0:T(8,128)S(1)} fusion(f32[50,24,136]{2,1,0:T(8,128)S(1)} %fusion.63, f32[50,26,138]{2,1,0:T(8,128)S(1)} %get-tuple-element.35, f32[50,26,138]{2,1,0:T(8,128)S(1)} %get-tuple-element.34, f32[50,26,138]{2,1,0:T(8,128)S(1)} %get-tuple-element.33, f32[50,26,138]{2,1,0:T(8,128)S(1)} %get-tuple-element.32, ...), kind=kLoop, calls=%fused_computation.74 | loop fusion | flops 2358400 | bytes 6476756 | tf_op jit(solution)/shard_map/jit(_where)/select_n | solution.py:233
  58.2 1.1 %fusion.70 = f32[49,20,132]{2,1,0:T(8,128)S(1)} fusion(f32[50,22,134]{2,1,0:T(8,128)S(1)} %fusion.51, f32[49,26,138]{2,1,0:T(8,128)S(1)} %get-tuple-element.37), kind=kLoop, calls=%fused_computation.102 | loop fusion | flops 258720 | bytes 2069760 | tf_op jit(solution)/shard_map/mul | solution.py:110
  59.2 2.7 %fusion.39 = f32[50,20,132]{2,1,0:T(8,128)S(1)} fusion(f32[50,22,134]{2,1,0:T(8,128)S(1)} %fusion.51, f32[50,26,138]{2,1,0:T(8,128)S(1)} %get-tuple-element.35, f32[50,26,138]{2,1,0:T(8,128)S(1)} %get-tuple-element.34, f32[50,26,138]{2,1,0:T(8,128)S(1)} %get-tuple-element.33, f32[50,26,138]{2,1,0:T(8,128)S(1)} %get-tuple-element.32, ...), kind=kLoop, calls=%fused_computation.58 | loop fusion | flops 2112000 | bytes 5800080 | tf_op jit(solution)/shard_map/jit(_where)/select_n | solution.py:233
  62.0 1.3 %fusion.69 = f32[49,18,130]{2,1,0:T(8,128)S(1)} fusion(f32[50,20,132]{2,1,0:T(8,128)S(1)} %fusion.39, f32[49,26,138]{2,1,0:T(8,128)S(1)} %get-tuple-element.37), kind=kLoop, calls=%fused_computation.100 | loop fusion | flops 229320 | bytes 1834560 | tf_op jit(solution)/shard_map/mul | solution.py:110
  63.2 2.7 %fusion.27 = f32[50,18,130]{2,1,0:T(8,128)S(1)} fusion(f32[50,20,132]{2,1,0:T(8,128)S(1)} %fusion.39, f32[50,26,138]{2,1,0:T(8,128)S(1)} %get-tuple-element.35, f32[50,26,138]{2,1,0:T(8,128)S(1)} %get-tuple-element.34, f32[50,26,138]{2,1,0:T(8,128)S(1)} %get-tuple-element.33, f32[50,26,138]{2,1,0:T(8,128)S(1)} %get-tuple-element.32, ...), kind=kLoop, calls=%fused_computation.42 | loop fusion | flops 1872000 | bytes 5140980 | tf_op jit(solution)/shard_map/jit(_where)/select_n | solution.py:233
  66.4 1.0 %fusion.83 = f32[50,16,128]{2,1,0:T(8,128)S(1)} fusion(f32[50,18,130]{2,1,0:T(8,128)S(1)} %fusion.27, f32[50,26,138]{2,1,0:T(8,128)S(1)} %get-tuple-element.35, f32[50,26,138]{2,1,0:T(8,128)S(1)} %get-tuple-element.34, f32[50,26,138]{2,1,0:T(8,128)S(1)} %get-tuple-element.33, f32[50,26,138]{2,1,0:T(8,128)S(1)} %get-tuple-element.32, ...), kind=kLoop, calls=%fused_computation.123 | loop fusion | flops 1536000 | bytes 4497408 | tf_op jit(solution)/shard_map/add | solution.py:116
  68.3 3.3 %all-to-all-start.1 = ((f32[4,32,128]{2,1,0:T(8,128)}), f32[4,32,128]{2,1,0:T(8,128)S(1)}, u32[]{:S(2)}, u32[]{:S(2)}) async-start(f32[4,32,128]{2,1,0:T(8,128)} %fusion.111), calls=%async_computation.1 | async-start | bytes 131072 | tf_op jit(solution)/shard_map/all_to_all | solution.py:238
  72.4 3.7 %all-to-all-done.1 = f32[4,32,128]{2,1,0:T(8,128)S(1)} async-done(((f32[4,32,128]{2,1,0:T(8,128)}), f32[4,32,128]{2,1,0:T(8,128)S(1)}, u32[]{:S(2)}, u32[]{:S(2)}) %all-to-all-start.1) | async-done | bytes 65568 | tf_op jit(solution)/shard_map/all_to_all | solution.py:238
  (57 shorter events, 9.7 us)
Async XLA Ops:
  0.6 10.9 %copy-start.5 = (s32[8]{0:T(128)S(1)}, s32[8]{0:T(128)}, u32[]{:S(2)}) copy-start(s32[8]{0:T(128)} %constant.100.clone.1) | copy-start | bytes 100
  0.6 15.4 %copy-start = (f32[50,16,128]{2,1,0:T(8,128)S(1)}, f32[50,16,128]{2,1,0:T(8,128)}, u32[]{:S(2)}) copy-start(f32[50,16,128]{2,1,0:T(8,128)} %param.16) | copy-start | bytes 1228804
  0.7 5.7 %copy-start.4 = (s32[64]{0:T(128)S(1)}, s32[64]{0:T(128)}, u32[]{:S(2)}) copy-start(s32[64]{0:T(128)} %param.19) | copy-start | bytes 772
  0.7 15.6 %copy-start.1 = (f32[50,16,128]{2,1,0:T(8,128)S(1)}, f32[50,16,128]{2,1,0:T(8,128)}, u32[]{:S(2)}) copy-start(f32[50,16,128]{2,1,0:T(8,128)} %param.17) | copy-start | bytes 1228804
  7.4 8.6 %all-to-all-start = ((f32[4,33,128]{2,1,0:T(8,128)}), f32[4,33,128]{2,1,0:T(8,128)S(1)}, u32[]{:S(2)}, u32[]{:S(2)}) async-start(f32[4,33,128]{2,1,0:T(8,128)} %pad_maximum_fusion.1), calls=%async_computation | async-start | bytes 163840 | tf_op jit(solution)/shard_map/all_to_all | solution.py:149
  16.4 10.2 %collective-permute-start = (f32[600,128]{1,0:T(8,128)S(1)}, f32[600,128]{1,0:T(8,128)S(1)}, u32[]{:S(2)}, u32[]{:S(2)}) collective-permute-start(f32[600,128]{1,0:T(8,128)S(1)} %reshape.224), channel_id=1, source_target_pairs={{0,4},{4,8},{8,12},{12,16},{16,20},{20,24},{24,28},{28,32},{32,36}... | collective-permute-start | bytes 921608 | tf_op jit(solution)/shard_map/ppermute | solution.py:163
  22.8 11.5 %collective-permute-start.1 = (f32[600,128]{1,0:T(8,128)S(1)}, f32[600,128]{1,0:T(8,128)S(1)}, u32[]{:S(2)}, u32[]{:S(2)}) collective-permute-start(f32[600,128]{1,0:T(8,128)S(1)} %reshape.226), channel_id=1, source_target_pairs={{4,0},{8,4},{12,8},{16,12},{20,16},{24,20},{28,24},{32,28},{36,32}... | collective-permute-start | bytes 921608 | tf_op jit(solution)/shard_map/ppermute | solution.py:168
  35.6 4.0 %collective-permute-start.2 = (f32[150,128]{1,0:T(8,128)S(1)}, f32[150,128]{1,0:T(8,128)S(1)}, u32[]{:S(2)}, u32[]{:S(2)}) collective-permute-start(f32[150,128]{1,0:T(8,128)S(1)} %reshape.229), channel_id=1, source_target_pairs={{0,1},{1,2},{2,3},{4,5},{5,6},{6,7},{8,9},{9,10},{10,11},{12,13},{... | collective-permute-start | bytes 230408 | tf_op jit(solution)/shard_map/ppermute | solution.py:192
  37.8 5.1 %collective-permute-start.3 = (f32[150,128]{1,0:T(8,128)S(1)}, f32[150,128]{1,0:T(8,128)S(1)}, u32[]{:S(2)}, u32[]{:S(2)}) collective-permute-start(f32[150,128]{1,0:T(8,128)S(1)} %reshape.231), channel_id=1, source_target_pairs={{1,0},{2,1},{3,2},{5,4},{6,5},{7,6},{9,8},{10,9},{11,10},{13,12},{... | collective-permute-start | bytes 230408 | tf_op jit(solution)/shard_map/ppermute | solution.py:195
  66.4 10.6 %copy-start.3 = (s32[64]{0:T(128)S(1)}, s32[64]{0:T(128)}, u32[]{:S(2)}) copy-start(s32[64]{0:T(128)} %param.20) | copy-start | bytes 772
  67.4 10.2 %copy-start.2 = (f32[50,16,128]{2,1,0:T(8,128)}, f32[50,16,128]{2,1,0:T(8,128)S(1)}, u32[]{:S(2)}) copy-start(f32[50,16,128]{2,1,0:T(8,128)S(1)} %fusion.83) | copy-start | bytes 1228804
  68.3 7.7 %all-to-all-start.1 = ((f32[4,32,128]{2,1,0:T(8,128)}), f32[4,32,128]{2,1,0:T(8,128)S(1)}, u32[]{:S(2)}, u32[]{:S(2)}) async-start(f32[4,32,128]{2,1,0:T(8,128)} %fusion.111), calls=%async_computation.1 | async-start | bytes 131072 | tf_op jit(solution)/shard_map/all_to_all | solution.py:238
